TPU v7x, 512 devices: a whole 4x4x16 slice. The times are simulated.
512 devices in a mesh: tile: 128 (over z, y_hi, x), lev: 4 (over y_lo, core).
Axes of the slice: x: 4, y: 4 (y_hi: 2, y_lo: 2; y = y_hi * 2 + y_lo), z: 16, core: 2. Of those that a mesh axis runs over, the one named last changes fastest.
Arguments:
- forcing: float32 [2, 52, 6144, 128], P(None, 'lev', 'tile'), may hold values from -6 to 6
- lateral_mix: float32 [52], P('lev'), may hold values from 0.05 to 0.15
- sea_mask: int32 [6144, 128], P('tile'), may hold values 0 or 1
- convective: int32 [6144, 128], P('tile'), may hold values 0 or 1
- mixing_inverse: float32 [2, 2, 52, 52], replicated, may hold values from -1.5 to 1.5
- seam_links: int32 [128, 8], P('tile'), may hold values from 0 to 511, as said below
Outputs:
- swept: float32 [2, 52, 6144, 128], P(None, 'lev', 'tile')
Inputs may be any that keep to these rules, and one draw needn't show every extreme that they name: Tile t sits at row t // 16 and column t % (16) of a grid of 8 rows that closes in both directions. seam_links[t, k] = 4 * s + code, where s is the tile beside t in that grid toward the previous row (k = 0), the next row (k = 1), the previous column (k = 2), the next column (k = 3), and diagonally (k = 4: previous row and column, 5: previous row and next column, 6: next row and previous column, 7: next row and next column).
All inputs are finite; a program needn't handle non-finite values. No bound on the sum of `sea_mask` or of `convective` on one device may be relied on, other than what follows from the above.
Results may differ from a plain program's by a relative error of at most 0.0001.
Values sent between devices are 32-bit elements; how exact they have to be, the bound alone decides.
No kernel may reach another device: no remote copies, remote signals or barrier semaphores. Data moves between devices by JAX's collectives and lax.ppermute only.
A program may use at most 64 MiB of HBM per device.

v0:
```python
import jax
import jax.numpy as jnp
from jax import lax
from jax.sharding import PartitionSpec as P

STEPS = 2


SLOT_STEPS = ((-1, 0), (1, 0), (0, -1), (0, 1), (-1, -1), (-1, 1), (1, -1), (1, 1))


def passed_along(value, axis, steps):
    count = lax.axis_size(axis)
    pairs = [(source, (source + steps) % count) for source in range(count)]
    return lax.ppermute(value, axis, pairs)


def strip_set(field):
    return jnp.concatenate(
        [
            field[..., 0, :],
            field[..., -1, :],
            field[..., :, 0],
            field[..., :, -1],
            field[..., 0, 0:1],
            field[..., 0, -1:],
            field[..., -1, 0:1],
            field[..., -1, -1:],
        ],
        axis=-1,
    )


def assemble(field, south, north, west, east, corners):
    middle = jnp.concatenate([west[..., None], field, east[..., None]], axis=-1)
    top_row = jnp.concatenate([corners[0][..., None], south, corners[1][..., None]], axis=-1)
    bottom_row = jnp.concatenate([corners[2][..., None], north, corners[3][..., None]], axis=-1)
    return jnp.concatenate([top_row[..., None, :], middle, bottom_row[..., None, :]], axis=-2)


def stencil(extended, field, rate, wet):
    edge_sum = (
        extended[..., :-2, 1:-1]
        + extended[..., 2:, 1:-1]
        + extended[..., 1:-1, :-2]
        + extended[..., 1:-1, 2:]
    )
    diag_sum = (
        extended[..., :-2, :-2]
        + extended[..., :-2, 2:]
        + extended[..., 2:, :-2]
        + extended[..., 2:, 2:]
    )
    return wet * ((1.0 - 6.0 * rate) * field + rate * edge_sum + 0.5 * rate * diag_sum)


def offset_slots(width, count):
    listing = {}
    for column in range(width):
        for slot in range(8):
            row_move, col_move = SLOT_STEPS[slot]
            moved_by = row_move * width + (column + col_move) % width - column
            distance = -moved_by % count
            if distance not in listing:
                listing[distance] = []
            listing[distance].append(slot)
    return listing


def seam_select(own_strips, seam_links):
    tile_count = lax.axis_size("tile")
    listing = offset_slots(tile_count // 8, tile_count)
    offsets = sorted(listing)
    received = []
    for shift_by in offsets:
        filled = passed_along(own_strips, "tile", shift_by)
        received.append(filled)
    stacked = jnp.stack(received)
    tile_here = lax.axis_index("tile")
    source = seam_links[0] // 4
    codes = seam_links[0] % 4
    distance = (tile_here - source) % tile_count
    offset_table = jnp.array(offsets, jnp.int32)
    selector = (distance[:, None] == offset_table[None, :]).astype(jnp.float32)
    chosen = jnp.einsum("sk,ktlp->stlp", selector, stacked, precision=lax.Precision.HIGHEST)
    return (chosen, codes)


def level_horizontal(adjoint, lateral_mix, wet, seam_links):
    rows = adjoint.shape[2]
    cols = adjoint.shape[3]
    chosen, codes = seam_select(strip_set(adjoint), seam_links)

    def edge(slot, first, last, length):
        part_a = chosen[slot][:, :, first : first + length]
        part_b = chosen[slot][:, :, last : last + length]
        strip = jnp.where(codes[slot] % 2 == 0, part_a, part_b)
        return jnp.where(codes[slot] // 2 == 1, strip[..., ::-1], strip)

    base = 2 * cols + 2 * rows

    def corner(slot):
        return lax.dynamic_index_in_dim(chosen[slot], base + codes[slot], axis=2, keepdims=False)

    south = edge(0, 0, cols, cols)
    north = edge(1, 0, cols, cols)
    west = edge(2, 2 * cols, 2 * cols + rows, rows)
    east = edge(3, 2 * cols, 2 * cols + rows, rows)
    corners = [corner(4), corner(5), corner(6), corner(7)]
    extended = assemble(adjoint, south, north, west, east, corners)
    rate = lateral_mix[None, :, None, None]
    return stencil(extended, adjoint, rate, wet[None, None])


def local(forcing, lateral_mix, sea_mask, convective, mixing_inverse, seam_links):
    wet = sea_mask.astype(jnp.float32)
    depth = forcing.shape[1]
    lev_here = lax.axis_index("lev")
    adjoint = forcing
    for step in range(STEPS):
        lateral = level_horizontal(adjoint, lateral_mix, wet, seam_links)
        own_levels = lax.dynamic_slice_in_dim(mixing_inverse, lev_here * depth, depth, axis=3)
        both_states = jnp.einsum(
            "tsml,tmxy->tslxy",
            own_levels,
            lax.all_gather(lateral, "lev", axis=1, tiled=True),
            precision=lax.Precision.HIGHEST,
        )
        adjoint = jnp.where(convective[None, None] == 1, both_states[:, 1], both_states[:, 0])
    return adjoint


def solution(mesh):
    return jax.shard_map(
        local,
        mesh=mesh,
        in_specs=(
            P(None, "lev", "tile", None),
            P("lev"),
            P("tile", None),
            P("tile", None),
            P(),
            P("tile", None),
        ),
        out_specs=P(None, "lev", "tile", None),
        check_vma=False,
    )
```

profile of v0, /device:TPU:1, one launch (start us, length us, event | category | flops | bytes accessed | tf_op | source)
XLA Modules:
  0.0 261.6 jit_solution(10945361443010133119)
XLA Ops:
  11.8 3.9 %collective-permute-start = (f32[2,13,356]{2,0,1:T(2,128)S(1)}, f32[2,13,356]{2,0,1:T(2,128)S(1)}, u32[]{:S(2)}, u32[]{:S(2)}) collective-permute-start(f32[2,13,356]{2,0,1:T(2,128)S(1)} %concatenate.58), channel_id=1, source_target_pairs={{0,4},{4,8},{8,12},{12,16},{16,20},{20,24},{24,28},{28,32},{32,36}... | collective-permute-start | bytes 111080 | tf_op jit(solution)/shard_map/ppermute | solution.py:15
  15.7 8.5 %collective-permute-start.1 = (f32[2,13,356]{2,0,1:T(2,128)S(1)}, f32[2,13,356]{2,0,1:T(2,128)S(1)}, u32[]{:S(2)}, u32[]{:S(2)}) collective-permute-start(f32[2,13,356]{2,0,1:T(2,128)S(1)} %concatenate.58), channel_id=1, source_target_pairs={{0,60},{4,64},{8,68},{12,72},{16,76},{20,80},{24,84},{28,88},{32,9... | collective-permute-start | bytes 111080 | tf_op jit(solution)/shard_map/ppermute | solution.py:15
  24.2 6.1 %collective-permute-start.2 = (f32[2,13,356]{2,0,1:T(2,128)S(1)}, f32[2,13,356]{2,0,1:T(2,128)S(1)}, u32[]{:S(2)}, u32[]{:S(2)}) collective-permute-start(f32[2,13,356]{2,0,1:T(2,128)S(1)} %concatenate.58), channel_id=1, source_target_pairs={{0,64},{4,68},{8,72},{12,76},{16,80},{20,84},{24,88},{28,92},{32,9... | collective-permute-start | bytes 111080 | tf_op jit(solution)/shard_map/ppermute | solution.py:15
  30.4 2.2 collective-permute-start.3
  32.6 14.2 %collective-permute-start.4 = (f32[2,13,356]{2,0,1:T(2,128)S(1)}, f32[2,13,356]{2,0,1:T(2,128)S(1)}, u32[]{:S(2)}, u32[]{:S(2)}) collective-permute-start(f32[2,13,356]{2,0,1:T(2,128)S(1)} %concatenate.58), channel_id=1, source_target_pairs={{0,124},{4,128},{8,132},{12,136},{16,140},{20,144},{24,148},{28,15... | collective-permute-start | bytes 111080 | tf_op jit(solution)/shard_map/ppermute | solution.py:15
  46.9 1.9 collective-permute-start.5
  48.8 7.3 %collective-permute-start.6 = (f32[2,13,356]{2,0,1:T(2,128)S(1)}, f32[2,13,356]{2,0,1:T(2,128)S(1)}, u32[]{:S(2)}, u32[]{:S(2)}) collective-permute-start(f32[2,13,356]{2,0,1:T(2,128)S(1)} %concatenate.58), channel_id=1, source_target_pairs={{0,444},{4,448},{8,452},{12,456},{16,460},{20,464},{24,468},{28,47... | collective-permute-start | bytes 111080 | tf_op jit(solution)/shard_map/ppermute | solution.py:15
  56.1 4.0 %collective-permute-start.7 = (f32[2,13,356]{2,0,1:T(2,128)S(1)}, f32[2,13,356]{2,0,1:T(2,128)S(1)}, u32[]{:S(2)}, u32[]{:S(2)}) collective-permute-start(f32[2,13,356]{2,0,1:T(2,128)S(1)} %concatenate.58), channel_id=1, source_target_pairs={{0,448},{4,452},{8,456},{12,460},{16,464},{20,468},{24,472},{28,47... | collective-permute-start | bytes 111080 | tf_op jit(solution)/shard_map/ppermute | solution.py:15
  60.1 1.9 collective-permute-start.8
  62.0 10.3 %collective-permute-start.9 = (f32[2,13,356]{2,0,1:T(2,128)S(1)}, f32[2,13,356]{2,0,1:T(2,128)S(1)}, u32[]{:S(2)}, u32[]{:S(2)}) collective-permute-start(f32[2,13,356]{2,0,1:T(2,128)S(1)} %concatenate.58), channel_id=1, source_target_pairs={{0,508},{4,0},{8,4},{12,8},{16,12},{20,16},{24,20},{28,24},{32,28}... | collective-permute-start | bytes 111080 | tf_op jit(solution)/shard_map/ppermute | solution.py:15
  97.4 38.6 %all-gather.3.cloned.1.call-done = f32[2,52,48,128]{3,2,0,1:T(8,128)} async-done(((f32[2,13,48,128]{3,2,0,1:T(8,128)}), f32[2,52,48,128]{3,2,0,1:T(8,128)}) %all-gather.3.cloned.1.call-update) | async-done | bytes 2555920 | tf_op jit(solution)/shard_map/all_gather | solution.py:126
  135.9 4.8 %fusion.2 = f32[2,2,13,48,128]{4,2,3,1,0:T(8,128)S(1)} fusion(f32[2,52,48,128,1]{3,2,0,1,4:T(8,128)} %bitcast.191, f32[2,2,52,13]{2,3,1,0:T(8,128)S(1)} %copy.953), kind=kOutput, calls=%fused_computation.2 | convolution fusion | flops 199360512 | bytes 3844672 | tf_op jit(solution)/shard_map/tsml,tmxy->tslxy/dot_general | solution.py:123
  142.0 3.1 %collective-permute-start.10 = (f32[2,13,356]{2,1,0:T(8,128)S(1)}, f32[2,13,356]{2,1,0:T(8,128)S(1)}, u32[]{:S(2)}, u32[]{:S(2)}) collective-permute-start(f32[2,13,356]{2,1,0:T(8,128)S(1)} %concatenate.66), channel_id=1, source_target_pairs={{0,4},{4,8},{8,12},{12,16},{16,20},{20,24},{24,28},{28,32},{32,36}... | collective-permute-start | bytes 111080 | tf_op jit(solution)/shard_map/ppermute | solution.py:15
  145.1 7.8 %collective-permute-start.11 = (f32[2,13,356]{2,1,0:T(8,128)S(1)}, f32[2,13,356]{2,1,0:T(8,128)S(1)}, u32[]{:S(2)}, u32[]{:S(2)}) collective-permute-start(f32[2,13,356]{2,1,0:T(8,128)S(1)} %concatenate.66), channel_id=1, source_target_pairs={{0,60},{4,64},{8,68},{12,72},{16,76},{20,80},{24,84},{28,88},{32,9... | collective-permute-start | bytes 111080 | tf_op jit(solution)/shard_map/ppermute | solution.py:15
  152.9 5.4 %collective-permute-start.12 = (f32[2,13,356]{2,1,0:T(8,128)S(1)}, f32[2,13,356]{2,1,0:T(8,128)S(1)}, u32[]{:S(2)}, u32[]{:S(2)}) collective-permute-start(f32[2,13,356]{2,1,0:T(8,128)S(1)} %concatenate.66), channel_id=1, source_target_pairs={{0,64},{4,68},{8,72},{12,76},{16,80},{20,84},{24,88},{28,92},{32,9... | collective-permute-start | bytes 111080 | tf_op jit(solution)/shard_map/ppermute | solution.py:15
  158.3 1.9 collective-permute-start.13
  160.2 12.3 %collective-permute-start.14 = (f32[2,13,356]{2,1,0:T(8,128)S(1)}, f32[2,13,356]{2,1,0:T(8,128)S(1)}, u32[]{:S(2)}, u32[]{:S(2)}) collective-permute-start(f32[2,13,356]{2,1,0:T(8,128)S(1)} %concatenate.66), channel_id=1, source_target_pairs={{0,124},{4,128},{8,132},{12,136},{16,140},{20,144},{24,148},{28,15... | collective-permute-start | bytes 111080 | tf_op jit(solution)/shard_map/ppermute | solution.py:15
  172.6 1.9 collective-permute-start.15
  174.5 9.4 %collective-permute-start.16 = (f32[2,13,356]{2,1,0:T(8,128)S(1)}, f32[2,13,356]{2,1,0:T(8,128)S(1)}, u32[]{:S(2)}, u32[]{:S(2)}) collective-permute-start(f32[2,13,356]{2,1,0:T(8,128)S(1)} %concatenate.66), channel_id=1, source_target_pairs={{0,444},{4,448},{8,452},{12,456},{16,460},{20,464},{24,468},{28,47... | collective-permute-start | bytes 111080 | tf_op jit(solution)/shard_map/ppermute | solution.py:15
  184.0 1.9 collective-permute-start.17
  186.0 1.9 collective-permute-start.18
  187.9 8.1 %collective-permute-start.19 = (f32[2,13,356]{2,1,0:T(8,128)S(1)}, f32[2,13,356]{2,1,0:T(8,128)S(1)}, u32[]{:S(2)}, u32[]{:S(2)}) collective-permute-start(f32[2,13,356]{2,1,0:T(8,128)S(1)} %concatenate.66), channel_id=1, source_target_pairs={{0,508},{4,0},{8,4},{12,8},{16,12},{20,16},{24,20},{28,24},{32,28}... | collective-permute-start | bytes 111080 | tf_op jit(solution)/shard_map/ppermute | solution.py:15
  204.0 44.8 %all-gather.5.cloned.1.call-done = f32[2,52,48,128]{3,2,0,1:T(8,128)} async-done(((f32[2,13,48,128]{3,2,0,1:T(8,128)}), f32[2,52,48,128]{3,2,0,1:T(8,128)}) %all-gather.5.cloned.1.call-update) | async-done | bytes 2555920 | tf_op jit(solution)/shard_map/all_gather | solution.py:126
  248.8 4.8 %fusion = f32[2,2,13,48,128]{4,2,3,0,1:T(8,128)S(1)} fusion(f32[2,52,48,128]{3,2,0,1:T(8,128)} %all-gather.5.cloned.1.call-done, f32[2,2,52,13]{2,3,1,0:T(8,128)S(1)} %copy.953), kind=kOutput, calls=%fused_computation | convolution fusion | flops 199360512 | bytes 3844672 | tf_op jit(solution)/shard_map/tsml,tmxy->tslxy/dot_general | solution.py:123
  (157 shorter events, 24.7 us)
Async XLA Ops:
  6.5 90.5 %copy-start = (f32[2,2,52,52]{3,1,2,0:T(2,128)S(1)}, f32[2,2,52,52]{3,1,2,0:T(2,128)}, u32[]{:S(2)}) copy-start(f32[2,2,52,52]{3,1,2,0:T(2,128)} %param.12) | copy-start | bytes 129796
  6.5 129.4 %all-gather.3.cloned.1.call-start = ((), (), s32[]{:S(2)}) async-start(), calls=%async_computation | async-start | bytes 3194880 | tf_op jit(solution)/shard_map/all_gather | solution.py:126
  8.9 79.2 %copy-start.1 = (f32[2,13,48,128]{3,2,1,0:T(8,128)S(1)}, f32[2,13,48,128]{3,2,1,0:T(8,128)}, u32[]{:S(2)}) copy-start(f32[2,13,48,128]{3,2,1,0:T(8,128)} %param.8) | copy-start | bytes 1916932
  11.8 35.1 %collective-permute-start = (f32[2,13,356]{2,0,1:T(2,128)S(1)}, f32[2,13,356]{2,0,1:T(2,128)S(1)}, u32[]{:S(2)}, u32[]{:S(2)}) collective-permute-start(f32[2,13,356]{2,0,1:T(2,128)S(1)} %concatenate.58), channel_id=1, source_target_pairs={{0,4},{4,8},{8,12},{12,16},{16,20},{20,24},{24,28},{28,32},{32,36}... | collective-permute-start | bytes 111080 | tf_op jit(solution)/shard_map/ppermute | solution.py:15
  15.7 33.1 %collective-permute-start.1 = (f32[2,13,356]{2,0,1:T(2,128)S(1)}, f32[2,13,356]{2,0,1:T(2,128)S(1)}, u32[]{:S(2)}, u32[]{:S(2)}) collective-permute-start(f32[2,13,356]{2,0,1:T(2,128)S(1)} %concatenate.58), channel_id=1, source_target_pairs={{0,60},{4,64},{8,68},{12,72},{16,76},{20,80},{24,84},{28,88},{32,9... | collective-permute-start | bytes 111080 | tf_op jit(solution)/shard_map/ppermute | solution.py:15
  24.2 31.8 %collective-permute-start.2 = (f32[2,13,356]{2,0,1:T(2,128)S(1)}, f32[2,13,356]{2,0,1:T(2,128)S(1)}, u32[]{:S(2)}, u32[]{:S(2)}) collective-permute-start(f32[2,13,356]{2,0,1:T(2,128)S(1)} %concatenate.58), channel_id=1, source_target_pairs={{0,64},{4,68},{8,72},{12,76},{16,80},{20,84},{24,88},{28,92},{32,9... | collective-permute-start | bytes 111080 | tf_op jit(solution)/shard_map/ppermute | solution.py:15
  30.4 29.7 %collective-permute-start.3 = (f32[2,13,356]{2,0,1:T(2,128)S(1)}, f32[2,13,356]{2,0,1:T(2,128)S(1)}, u32[]{:S(2)}, u32[]{:S(2)}) collective-permute-start(f32[2,13,356]{2,0,1:T(2,128)S(1)} %concatenate.58), channel_id=1, source_target_pairs={{0,68},{4,72},{8,76},{12,80},{16,84},{20,88},{24,92},{28,96},{32,1... | collective-permute-start | bytes 111080 | tf_op jit(solution)/shard_map/ppermute | solution.py:15
  32.6 29.4 %collective-permute-start.4 = (f32[2,13,356]{2,0,1:T(2,128)S(1)}, f32[2,13,356]{2,0,1:T(2,128)S(1)}, u32[]{:S(2)}, u32[]{:S(2)}) collective-permute-start(f32[2,13,356]{2,0,1:T(2,128)S(1)} %concatenate.58), channel_id=1, source_target_pairs={{0,124},{4,128},{8,132},{12,136},{16,140},{20,144},{24,148},{28,15... | collective-permute-start | bytes 111080 | tf_op jit(solution)/shard_map/ppermute | solution.py:15
  46.9 41.9 %collective-permute-start.5 = (f32[2,13,356]{2,0,1:T(2,128)S(1)}, f32[2,13,356]{2,0,1:T(2,128)S(1)}, u32[]{:S(2)}, u32[]{:S(2)}) collective-permute-start(f32[2,13,356]{2,0,1:T(2,128)S(1)} %concatenate.58), channel_id=1, source_target_pairs={{0,388},{4,392},{8,396},{12,400},{16,404},{20,408},{24,412},{28,41... | collective-permute-start | bytes 111080 | tf_op jit(solution)/shard_map/ppermute | solution.py:15
  48.8 40.0 %collective-permute-start.6 = (f32[2,13,356]{2,0,1:T(2,128)S(1)}, f32[2,13,356]{2,0,1:T(2,128)S(1)}, u32[]{:S(2)}, u32[]{:S(2)}) collective-permute-start(f32[2,13,356]{2,0,1:T(2,128)S(1)} %concatenate.58), channel_id=1, source_target_pairs={{0,444},{4,448},{8,452},{12,456},{16,460},{20,464},{24,468},{28,47... | collective-permute-start | bytes 111080 | tf_op jit(solution)/shard_map/ppermute | solution.py:15
  56.1 32.8 %collective-permute-start.7 = (f32[2,13,356]{2,0,1:T(2,128)S(1)}, f32[2,13,356]{2,0,1:T(2,128)S(1)}, u32[]{:S(2)}, u32[]{:S(2)}) collective-permute-start(f32[2,13,356]{2,0,1:T(2,128)S(1)} %concatenate.58), channel_id=1, source_target_pairs={{0,448},{4,452},{8,456},{12,460},{16,464},{20,468},{24,472},{28,47... | collective-permute-start | bytes 111080 | tf_op jit(solution)/shard_map/ppermute | solution.py:15
  60.1 28.9 %collective-permute-start.8 = (f32[2,13,356]{2,0,1:T(2,128)S(1)}, f32[2,13,356]{2,0,1:T(2,128)S(1)}, u32[]{:S(2)}, u32[]{:S(2)}) collective-permute-start(f32[2,13,356]{2,0,1:T(2,128)S(1)} %concatenate.58), channel_id=1, source_target_pairs={{0,452},{4,456},{8,460},{12,464},{16,468},{20,472},{24,476},{28,48... | collective-permute-start | bytes 111080 | tf_op jit(solution)/shard_map/ppermute | solution.py:15
  62.0 27.0 %collective-permute-start.9 = (f32[2,13,356]{2,0,1:T(2,128)S(1)}, f32[2,13,356]{2,0,1:T(2,128)S(1)}, u32[]{:S(2)}, u32[]{:S(2)}) collective-permute-start(f32[2,13,356]{2,0,1:T(2,128)S(1)} %concatenate.58), channel_id=1, source_target_pairs={{0,508},{4,0},{8,4},{12,8},{16,12},{20,16},{24,20},{28,24},{32,28}... | collective-permute-start | bytes 111080 | tf_op jit(solution)/shard_map/ppermute | solution.py:15
  96.8 152.0 %all-gather.5.cloned.1.call-start = ((), (), s32[]{:S(2)}) async-start(), calls=%async_computation.1 | async-start | bytes 3194880 | tf_op jit(solution)/shard_map/all_gather | solution.py:126
  142.0 30.6 %collective-permute-start.10 = (f32[2,13,356]{2,1,0:T(8,128)S(1)}, f32[2,13,356]{2,1,0:T(8,128)S(1)}, u32[]{:S(2)}, u32[]{:S(2)}) collective-permute-start(f32[2,13,356]{2,1,0:T(8,128)S(1)} %concatenate.66), channel_id=1, source_target_pairs={{0,4},{4,8},{8,12},{12,16},{16,20},{20,24},{24,28},{28,32},{32,36}... | collective-permute-start | bytes 111080 | tf_op jit(solution)/shard_map/ppermute | solution.py:15
  145.1 29.4 %collective-permute-start.11 = (f32[2,13,356]{2,1,0:T(8,128)S(1)}, f32[2,13,356]{2,1,0:T(8,128)S(1)}, u32[]{:S(2)}, u32[]{:S(2)}) collective-permute-start(f32[2,13,356]{2,1,0:T(8,128)S(1)} %concatenate.66), channel_id=1, source_target_pairs={{0,60},{4,64},{8,68},{12,72},{16,76},{20,80},{24,84},{28,88},{32,9... | collective-permute-start | bytes 111080 | tf_op jit(solution)/shard_map/ppermute | solution.py:15
  152.9 31.1 %collective-permute-start.12 = (f32[2,13,356]{2,1,0:T(8,128)S(1)}, f32[2,13,356]{2,1,0:T(8,128)S(1)}, u32[]{:S(2)}, u32[]{:S(2)}) collective-permute-start(f32[2,13,356]{2,1,0:T(8,128)S(1)} %concatenate.66), channel_id=1, source_target_pairs={{0,64},{4,68},{8,72},{12,76},{16,80},{20,84},{24,88},{28,92},{32,9... | collective-permute-start | bytes 111080 | tf_op jit(solution)/shard_map/ppermute | solution.py:15
  158.3 27.6 %collective-permute-start.13 = (f32[2,13,356]{2,1,0:T(8,128)S(1)}, f32[2,13,356]{2,1,0:T(8,128)S(1)}, u32[]{:S(2)}, u32[]{:S(2)}) collective-permute-start(f32[2,13,356]{2,1,0:T(8,128)S(1)} %concatenate.66), channel_id=1, source_target_pairs={{0,68},{4,72},{8,76},{12,80},{16,84},{20,88},{24,92},{28,96},{32,1... | collective-permute-start | bytes 111080 | tf_op jit(solution)/shard_map/ppermute | solution.py:15
  160.2 27.7 %collective-permute-start.14 = (f32[2,13,356]{2,1,0:T(8,128)S(1)}, f32[2,13,356]{2,1,0:T(8,128)S(1)}, u32[]{:S(2)}, u32[]{:S(2)}) collective-permute-start(f32[2,13,356]{2,1,0:T(8,128)S(1)} %concatenate.66), channel_id=1, source_target_pairs={{0,124},{4,128},{8,132},{12,136},{16,140},{20,144},{24,148},{28,15... | collective-permute-start | bytes 111080 | tf_op jit(solution)/shard_map/ppermute | solution.py:15
  172.6 23.5 %collective-permute-start.15 = (f32[2,13,356]{2,1,0:T(8,128)S(1)}, f32[2,13,356]{2,1,0:T(8,128)S(1)}, u32[]{:S(2)}, u32[]{:S(2)}) collective-permute-start(f32[2,13,356]{2,1,0:T(8,128)S(1)} %concatenate.66), channel_id=1, source_target_pairs={{0,388},{4,392},{8,396},{12,400},{16,404},{20,408},{24,412},{28,41... | collective-permute-start | bytes 111080 | tf_op jit(solution)/shard_map/ppermute | solution.py:15
  174.5 21.5 %collective-permute-start.16 = (f32[2,13,356]{2,1,0:T(8,128)S(1)}, f32[2,13,356]{2,1,0:T(8,128)S(1)}, u32[]{:S(2)}, u32[]{:S(2)}) collective-permute-start(f32[2,13,356]{2,1,0:T(8,128)S(1)} %concatenate.66), channel_id=1, source_target_pairs={{0,444},{4,448},{8,452},{12,456},{16,460},{20,464},{24,468},{28,47... | collective-permute-start | bytes 111080 | tf_op jit(solution)/shard_map/ppermute | solution.py:15
  184.0 12.1 %collective-permute-start.17 = (f32[2,13,356]{2,1,0:T(8,128)S(1)}, f32[2,13,356]{2,1,0:T(8,128)S(1)}, u32[]{:S(2)}, u32[]{:S(2)}) collective-permute-start(f32[2,13,356]{2,1,0:T(8,128)S(1)} %concatenate.66), channel_id=1, source_target_pairs={{0,448},{4,452},{8,456},{12,460},{16,464},{20,468},{24,472},{28,47... | collective-permute-start | bytes 111080 | tf_op jit(solution)/shard_map/ppermute | solution.py:15
  186.0 10.2 %collective-permute-start.18 = (f32[2,13,356]{2,1,0:T(8,128)S(1)}, f32[2,13,356]{2,1,0:T(8,128)S(1)}, u32[]{:S(2)}, u32[]{:S(2)}) collective-permute-start(f32[2,13,356]{2,1,0:T(8,128)S(1)} %concatenate.66), channel_id=1, source_target_pairs={{0,452},{4,456},{8,460},{12,464},{16,468},{20,472},{24,476},{28,48... | collective-permute-start | bytes 111080 | tf_op jit(solution)/shard_map/ppermute | solution.py:15
  187.9 9.1 %collective-permute-start.19 = (f32[2,13,356]{2,1,0:T(8,128)S(1)}, f32[2,13,356]{2,1,0:T(8,128)S(1)}, u32[]{:S(2)}, u32[]{:S(2)}) collective-permute-start(f32[2,13,356]{2,1,0:T(8,128)S(1)} %concatenate.66), channel_id=1, source_target_pairs={{0,508},{4,0},{8,4},{12,8},{16,12},{20,16},{24,20},{28,24},{32,28}... | collective-permute-start | bytes 111080 | tf_op jit(solution)/shard_map/ppermute | solution.py:15
  (5 other events, 156.8 us)
Sparse Core Ops, SparseCore 0:
  96.9 38.9 all-gather.2
  204.1 44.6 all-gather.4
where the time goes:
time: 263 us; the launch traced here: 262 us
  starting transfers between devices  114 us (43%)
  waiting for transfers between devices  84.3 us (32%)
  between operations  29.8 us (11%)
  local copies, waits for them, and re-layouts  15.7 us (6%)
  matrix products  10.5 us (4%)
  other arithmetic  6.93 us (3%)
    ppermute x20, starting transfers between devices, passed_along(): return lax.ppermute(value, axis, pairs)  114 us
    all_gather x2, waiting for transfers between devices, local(): lax.all_gather(lateral, 'lev', axis=1, tiled=True)  83.4 us
    dot_general x2, matrix products, local(): jnp.einsum('tsml,tmxy->tslxy', own_levels, lax.all_gather(lateral, 'lev',...  9.63 us
  transfers between devices with their start and end apart: 22, of which 3 were waited for; matrix products, arithmetic and copies ran while one was open for 1% of the time, Pallas kernels for 0%

commit v1 on v0

v1 whole, which is shorter than its diff:
```python
import jax
import jax.numpy as jnp
from jax import lax
from jax.sharding import PartitionSpec as P

STEPS = 2
GRID_ROWS = 8

SLOT_STEPS = ((-1, 0), (1, 0), (0, -1), (0, 1), (-1, -1), (-1, 1), (1, -1), (1, 1))


def slot_pairs(count, slot):
    width = count // GRID_ROWS
    row_move, col_move = SLOT_STEPS[slot]
    pairs = []
    for target in range(count):
        row, col = divmod(target, width)
        source = ((row + row_move) % GRID_ROWS) * width + (col + col_move) % width
        pairs.append((source, target))
    return pairs


def pick(pair, code):
    strip = jnp.where(code % 2 == 0, pair[..., 0, :], pair[..., 1, :])
    return jnp.where(code // 2 == 1, strip[..., ::-1], strip)


def stencil(extended, field, rate, wet):
    edge_sum = (
        extended[..., :-2, 1:-1]
        + extended[..., 2:, 1:-1]
        + extended[..., 1:-1, :-2]
        + extended[..., 1:-1, 2:]
    )
    diag_sum = (
        extended[..., :-2, :-2]
        + extended[..., :-2, 2:]
        + extended[..., 2:, :-2]
        + extended[..., 2:, 2:]
    )
    return wet * ((1.0 - 6.0 * rate) * field + rate * edge_sum + 0.5 * rate * diag_sum)


def horizontal(field, rate, wet, codes):
    count = lax.axis_size("tile")
    row_pair = jnp.stack([field[..., 0, :], field[..., -1, :]], axis=-2)
    col_pair = jnp.stack([field[..., :, 0], field[..., :, -1]], axis=-2)
    corner_set = jnp.stack(
        [field[..., 0, 0], field[..., 0, -1], field[..., -1, 0], field[..., -1, -1]], axis=-1
    )
    payloads = [row_pair, row_pair, col_pair, col_pair] + [corner_set] * 4
    got = [lax.ppermute(payloads[slot], "tile", slot_pairs(count, slot)) for slot in range(8)]
    south = pick(got[0], codes[0])
    north = pick(got[1], codes[1])
    west = pick(got[2], codes[2])
    east = pick(got[3], codes[3])
    corners = []
    for slot in range(4, 8):
        cell = got[slot]
        code = codes[slot]
        value = jnp.where(
            code == 0,
            cell[..., 0],
            jnp.where(code == 1, cell[..., 1], jnp.where(code == 2, cell[..., 2], cell[..., 3])),
        )
        corners.append(value)
    middle = jnp.concatenate([west[..., None], field, east[..., None]], axis=-1)
    top_row = jnp.concatenate([corners[0][..., None], south, corners[1][..., None]], axis=-1)
    bottom_row = jnp.concatenate([corners[2][..., None], north, corners[3][..., None]], axis=-1)
    extended = jnp.concatenate([top_row[..., None, :], middle, bottom_row[..., None, :]], axis=-2)
    return stencil(extended, field, rate, wet)


def column_mix(lateral, mixing_inverse, convective_rows):
    columns = lax.all_to_all(lateral, "lev", 2, 1, tiled=True)
    both_states = jnp.einsum(
        "tsml,tmxy->tslxy", mixing_inverse, columns, precision=lax.Precision.HIGHEST
    )
    mixed = jnp.where(convective_rows[None, None], both_states[:, 1], both_states[:, 0])
    return lax.all_to_all(mixed, "lev", 1, 2, tiled=True)


def local(forcing, lateral_mix, sea_mask, convective, mixing_inverse, seam_links):
    wet = sea_mask.astype(jnp.float32)[None, None]
    rate = lateral_mix[None, :, None, None]
    codes = seam_links[0] % 4
    parts = lax.axis_size("lev")
    rows = forcing.shape[2] // parts
    lev_here = lax.axis_index("lev")
    convective_rows = lax.dynamic_slice_in_dim(convective, lev_here * rows, rows, axis=0) == 1
    adjoint = forcing
    for step in range(STEPS):
        lateral = horizontal(adjoint, rate, wet, codes)
        adjoint = column_mix(lateral, mixing_inverse, convective_rows)
    return adjoint


def solution(mesh):
    return jax.shard_map(
        local,
        mesh=mesh,
        in_specs=(
            P(None, "lev", "tile", None),
            P("lev"),
            P("tile", None),
            P("tile", None),
            P(),
            P("tile", None),
        ),
        out_specs=P(None, "lev", "tile", None),
        check_vma=False,
    )
```

time: 263 us -> 208 us (0.79)
  waiting for transfers between devices: 84.3 us -> 19.3 us
  blocking collectives: 0 us -> 39.8 us
  starting transfers between devices: 114 us -> 91.7 us
  other arithmetic: 6.93 us -> 21.5 us
  between operations: 29.8 us -> 18.8 us
  matrix products: 10.5 us -> 2.55 us
  local copies, waits for them, and re-layouts: 15.7 us -> 12.1 us
    all_gather x2 -> x0, waiting for transfers between devices: 83.4 us -> none  [local(): lax.all_gather(lateral, 'lev', axis=1, tiled=True)]
    all_to_all x0 -> x3, blocking collectives: none -> 39.8 us  [the longest x2 24.8 us: column_mix(): return lax.all_to_all(mixed, 'lev', 1, 2, tiled=True)]
    ppermute x20 -> x16, starting transfers between devices: 114 us -> 83.3 us  [horizontal(): lax.ppermute(payloads[slot], 'tile', slot_pairs(count, slot))]
    ppermute x20 -> x16, waiting for transfers between devices: 0.87 us -> 10.8 us  [horizontal(): lax.ppermute(payloads[slot], 'tile', slot_pairs(count, slot))]
    all_to_all x0 -> x1, waiting for transfers between devices: none -> 8.49 us  [column_mix(): columns = lax.all_to_all(lateral, 'lev', 2, 1, tiled=True)]
    all_to_all x0 -> x1, starting transfers between devices: none -> 8.4 us  [column_mix(): columns = lax.all_to_all(lateral, 'lev', 2, 1, tiled=True)]
    dot_general x4 -> x2, matrix products: 10.5 us -> 2.55 us  [column_mix(): jnp.einsum('tsml,tmxy->tslxy', mixing_inverse, columns, precision=lax.Pre...]
    concatenate x2, other arithmetic: 2.56 us -> 10.1 us  [horizontal(): jnp.concatenate([top_row[..., None, :], middle, bottom_row[..., None, :]]...]
  transfers between devices with their start and end apart: 22 -> 17, of which waited for: 3 -> 5; matrix products, arithmetic and copies ran while one was open for 1% -> 3% of each run, Pallas kernels for 0% -> 0%
where the time goes in v1:
time: 208 us; the launch traced here: 206 us
  starting transfers between devices  91.7 us (44%)
  blocking collectives  39.8 us (19%)
  other arithmetic  21.5 us (10%)
  waiting for transfers between devices  19.3 us (9%)
  between operations  18.8 us (9%)
  local copies, waits for them, and re-layouts  12.1 us (6%)
  matrix products  2.55 us (1%)
    ppermute x16, starting transfers between devices, horizontal(): lax.ppermute(payloads[slot], 'tile', slot_pairs(count, slot))  83.3 us
    all_to_all x2, blocking collectives, column_mix(): return lax.all_to_all(mixed, 'lev', 1, 2, tiled=True)  24.8 us
    all_to_all x1, blocking collectives, column_mix(): columns = lax.all_to_all(lateral, 'lev', 2, 1, tiled=True)  15 us
    ppermute x16, waiting for transfers between devices, horizontal(): lax.ppermute(payloads[slot], 'tile', slot_pairs(count, slot))  10.8 us
    concatenate x2, other arithmetic, horizontal(): jnp.concatenate([top_row[..., None, :], middle, bottom_row[..., None, :]]...  10.1 us
    mul x2, other arithmetic, stencil(): wet * ((1.0 - 6.0 * rate) * field + rate * edge_sum + 0.5 * rate * diag_sum)  9.79 us
    all_to_all x1, waiting for transfers between devices, column_mix(): columns = lax.all_to_all(lateral, 'lev', 2, 1, tiled=True)  8.49 us
    all_to_all x1, starting transfers between devices, column_mix(): columns = lax.all_to_all(lateral, 'lev', 2, 1, tiled=True)  8.4 us
  transfers between devices with their start and end apart: 17, of which 5 were waited for; matrix products, arithmetic and copies ran while one was open for 3% of the time, Pallas kernels for 0%

profile of v1, /device:TPU:1, one launch (start us, length us, event | category | flops | bytes accessed | tf_op | source)
XLA Modules:
  0.0 205.8 jit_solution(1402742683233269442)
XLA Ops:
  2.2 3.9 %collective-permute-start.3 = (f32[2,13,2,48]{3,0,1,2:T(2,128)S(1)}, f32[2,13,2,48]{3,0,1,2:T(2,128)S(1)}, u32[]{:S(2)}, u32[]{:S(2)}) collective-permute-start(f32[2,13,2,48]{3,0,1,2:T(2,128)S(1)} %pad_maximum_fusion.6), channel_id=1, source_target_pairs={{60,0},{0,4},{4,8},{8,12},{12,16},{16,20},{20,24},{24,28},{28,32},... | collective-permute-start | bytes 29960 | tf_op jit(solution)/shard_map/ppermute | solution.py:52
  6.1 7.2 %collective-permute-start.4 = (f32[2,13,2,48]{3,0,1,2:T(2,128)S(1)}, f32[2,13,2,48]{3,0,1,2:T(2,128)S(1)}, u32[]{:S(2)}, u32[]{:S(2)}) collective-permute-start(f32[2,13,2,48]{3,0,1,2:T(2,128)S(1)} %pad_maximum_fusion.6), channel_id=1, source_target_pairs={{4,0},{8,4},{12,8},{16,12},{20,16},{24,20},{28,24},{32,28},{36,32}... | collective-permute-start | bytes 29960 | tf_op jit(solution)/shard_map/ppermute | solution.py:52
  13.4 11.1 %collective-permute-start.6 = (f32[2,13,2,128]{3,0,1,2:T(2,128)S(1)}, f32[2,13,2,128]{3,0,1,2:T(2,128)S(1)}, u32[]{:S(2)}, u32[]{:S(2)}) collective-permute-start(f32[2,13,2,128]{3,0,1,2:T(2,128)S(1)} %copy_dynamic-update-slice_fusion), channel_id=1, source_target_pairs={{64,0},{68,4},{72,8},{76,12},{80,16},{84,20},{88,24},{92,28},{96,3... | collective-permute-start | bytes 79880 | tf_op jit(solution)/shard_map/ppermute | solution.py:52
  24.5 1.9 collective-permute-start.1
  26.7 1.9 collective-permute-start
  47.9 7.4 %collective-permute-start.2 = (f32[2,13,4]{1,0,2:T(2,128)S(1)}, f32[2,13,4]{1,0,2:T(2,128)S(1)}, u32[]{:S(2)}, u32[]{:S(2)}) collective-permute-start(f32[2,13,4]{1,0,2:T(2,128)S(1)} %pad_maximum_fusion.9), channel_id=1, source_target_pairs={{452,0},{456,4},{460,8},{464,12},{468,16},{472,20},{476,24},{480,2... | collective-permute-start | bytes 1256 | tf_op jit(solution)/shard_map/ppermute | solution.py:52
  58.0 9.0 %collective-permute-done.5 = f32[2,13,4]{1,0,2:T(2,128)S(1)} collective-permute-done((f32[2,13,4]{1,0,2:T(2,128)S(1)}, f32[2,13,4]{1,0,2:T(2,128)S(1)}, u32[]{:S(2)}, u32[]{:S(2)}) %collective-permute-start.5) | collective-permute-done | bytes 448 | tf_op jit(solution)/shard_map/ppermute | solution.py:52
  67.0 8.0 %collective-permute-start.7 = (f32[2,13,4]{1,0,2:T(2,128)S(1)}, f32[2,13,4]{1,0,2:T(2,128)S(1)}, u32[]{:S(2)}, u32[]{:S(2)}) collective-permute-start(f32[2,13,4]{1,0,2:T(2,128)S(1)} %pad_maximum_fusion.9), channel_id=1, source_target_pairs={{68,0},{72,4},{76,8},{80,12},{84,16},{88,20},{92,24},{96,28},{100,... | collective-permute-start | bytes 1256 | tf_op jit(solution)/shard_map/ppermute | solution.py:52
  77.6 5.1 %maximum_maximum_fusion = (f32[2,13,49,130]{3,0,2,1:T(2,128)S(1)}, f32[2,13,49,130]{3,0,2,1:T(2,128)S(1)}) fusion(f32[2,13,48,1]{3,0,2,1:T(2,128)S(1)} %copy.345, f32[2,13,48,128]{3,0,2,1:T(2,128)S(1)} %copy.336, f32[2,13,48,1]{3,0,2,1:T(2,128)S(1)} %copy.343, f32[2,13,1,130]{3,0,2,1:T(2,128)S(1)} %get-tuple-element.35, ...), kind=kLoop, calls=%fused_computation.2 | loop fusion | flops 993720 | bytes 2000960 | tf_op jit(solution)/shard_map/concatenate | solution.py:70
  82.7 4.9 %fusion.14 = f32[2,13,48,128]{3,0,2,1:T(2,128)S(1)} fusion(f32[2,13,49,130]{3,0,2,1:T(2,128)S(1)} %get-tuple-element.12, f32[2,13,49,130]{3,0,2,1:T(2,128)S(1)} %get-tuple-element.11, f32[2,13,48,1]{3,0,2,1:T(2,128)S(1)} %copy.345, f32[2,13,48,128]{3,0,2,1:T(2,128)S(1)} %copy.336, f32[2,13,48,1]{3,0,2,1:T(2,128)S(1)} %copy.343, f32[13]{0:T(128)S(1)} %get-tuple-element.26, ...), kind=kLoop, calls=%fused_computation.31 | loop fusion | flops 2236416 | bytes 5146524 | tf_op jit(solution)/shard_map/mul | solution.py:41
  88.6 8.4 %all-to-all-start = ((f32[2,13,48,128]{3,0,1,2:T(2,128)}), f32[2,13,48,128]{3,0,1,2:T(2,128)S(1)}, u32[]{:S(2)}, u32[]{:S(2)}) async-start(f32[2,13,48,128]{3,0,1,2:T(2,128)} %copy.353), calls=%async_computation | async-start | bytes 1277952 | tf_op jit(solution)/shard_map/all_to_all | solution.py:75
  97.7 8.5 %all-to-all-done = f32[2,13,48,128]{3,0,1,2:T(2,128)S(1)} async-done(((f32[2,13,48,128]{3,0,1,2:T(2,128)}), f32[2,13,48,128]{3,0,1,2:T(2,128)S(1)}, u32[]{:S(2)}, u32[]{:S(2)}) %all-to-all-start) | async-done | bytes 639008 | tf_op jit(solution)/shard_map/all_to_all | solution.py:75
  108.3 12.4 %all_to_all.72 = f32[2,52,12,128]{3,0,2,1:T(2,128)S(1)} all-to-all(f32[2,52,12,128]{3,0,2,1:T(2,128)S(1)} %copy.359), channel_id=1, replica_groups=mesh['tile'=128,'lev'=4] {'lev'}, dimensions={1} | all-to-all | bytes 1277952 | tf_op jit(solution)/shard_map/all_to_all | solution.py:80
  123.2 10.2 %collective-permute-start.15 = (f32[2,13,4]{1,0,2:T(2,128)S(1)}, f32[2,13,4]{1,0,2:T(2,128)S(1)}, u32[]{:S(2)}, u32[]{:S(2)}) collective-permute-start(f32[2,13,4]{1,0,2:T(2,128)S(1)} %pad_maximum_fusion.10), channel_id=1, source_target_pairs={{68,0},{72,4},{76,8},{80,12},{84,16},{88,20},{92,24},{96,28},{100,... | collective-permute-start | bytes 1256 | tf_op jit(solution)/shard_map/ppermute | solution.py:52
  133.4 6.7 %collective-permute-start.14 = (f32[2,13,2,128]{3,0,1,2:T(2,128)S(1)}, f32[2,13,2,128]{3,0,1,2:T(2,128)S(1)}, u32[]{:S(2)}, u32[]{:S(2)}) collective-permute-start(f32[2,13,2,128]{3,0,1,2:T(2,128)S(1)} %pad_maximum_fusion.7), channel_id=1, source_target_pairs={{64,0},{68,4},{72,8},{76,12},{80,16},{84,20},{88,24},{92,28},{96,3... | collective-permute-start | bytes 79880 | tf_op jit(solution)/shard_map/ppermute | solution.py:52
  140.1 1.9 collective-permute-start.9
  142.0 2.1 %collective-permute-start.8 = (f32[2,13,4]{1,0,2:T(2,128)S(1)}, f32[2,13,4]{1,0,2:T(2,128)S(1)}, u32[]{:S(2)}, u32[]{:S(2)}) collective-permute-start(f32[2,13,4]{1,0,2:T(2,128)S(1)} %pad_maximum_fusion.10), channel_id=1, source_target_pairs={{508,0},{448,4},{452,8},{456,12},{460,16},{464,20},{468,24},{472,2... | collective-permute-start | bytes 1256 | tf_op jit(solution)/shard_map/ppermute | solution.py:52
  145.5 7.3 %collective-permute-start.10 = (f32[2,13,4]{1,0,2:T(2,128)S(1)}, f32[2,13,4]{1,0,2:T(2,128)S(1)}, u32[]{:S(2)}, u32[]{:S(2)}) collective-permute-start(f32[2,13,4]{1,0,2:T(2,128)S(1)} %pad_maximum_fusion.10), channel_id=1, source_target_pairs={{452,0},{456,4},{460,8},{464,12},{468,16},{472,20},{476,24},{480,2... | collective-permute-start | bytes 1256 | tf_op jit(solution)/shard_map/ppermute | solution.py:52
  152.9 1.9 collective-permute-start.11
  154.8 7.9 %collective-permute-start.12 = (f32[2,13,2,48]{3,0,1,2:T(2,128)S(1)}, f32[2,13,2,48]{3,0,1,2:T(2,128)S(1)}, u32[]{:S(2)}, u32[]{:S(2)}) collective-permute-start(f32[2,13,2,48]{3,0,1,2:T(2,128)S(1)} %pad_maximum_fusion.8), channel_id=1, source_target_pairs={{4,0},{8,4},{12,8},{16,12},{20,16},{24,20},{28,24},{32,28},{36,32}... | collective-permute-start | bytes 29960 | tf_op jit(solution)/shard_map/ppermute | solution.py:52
  165.1 5.1 %maximum_maximum_fusion.1 = (f32[2,13,49,130]{3,0,2,1:T(2,128)S(1)}, f32[2,13,49,130]{3,0,2,1:T(2,128)S(1)}) fusion(f32[2,13,48,1]{3,0,2,1:T(2,128)S(1)} %copy.372, f32[2,13,48,128]{3,0,2,1:T(2,128)S(1)} %bitcast.138, f32[2,13,48,1]{3,0,2,1:T(2,128)S(1)} %copy.371, f32[2,13,1,130]{3,0,2,1:T(2,128)S(1)} %maximum_bitcast_fusion.2, ...), kind=kLoop, calls=%fused_computation.4 | loop fusion | flops 993720 | bytes 2000960 | tf_op jit(solution)/shard_map/concatenate | solution.py:70
  170.1 4.9 %fusion.7 = f32[2,13,48,128]{3,0,2,1:T(2,128)S(1)} fusion(f32[2,13,49,130]{3,0,2,1:T(2,128)S(1)} %get-tuple-element.10, f32[2,13,49,130]{3,0,2,1:T(2,128)S(1)} %get-tuple-element.9, f32[2,13,48,1]{3,0,2,1:T(2,128)S(1)} %copy.372, f32[2,13,48,128]{3,0,2,1:T(2,128)S(1)} %bitcast.139, f32[2,13,48,1]{3,0,2,1:T(2,128)S(1)} %copy.371, ...), kind=kLoop, calls=%fused_computation.18 | loop fusion | flops 2236416 | bytes 5146524 | tf_op jit(solution)/shard_map/mul | solution.py:41
  175.3 15.0 %all_to_all.73 = f32[2,13,48,128]{3,0,1,2:T(2,128)S(1)} all-to-all(f32[2,13,48,128]{3,0,1,2:T(2,128)S(1)} %copy.379), channel_id=1, replica_groups=mesh['tile'=128,'lev'=4] {'lev'}, dimensions={2} | all-to-all | bytes 1277952 | tf_op jit(solution)/shard_map/all_to_all | solution.py:75
  192.4 12.5 %all_to_all.74 = f32[2,52,12,128]{3,0,2,1:T(2,128)S(1)} all-to-all(f32[2,52,12,128]{3,0,2,1:T(2,128)S(1)} %copy.385), channel_id=1, replica_groups=mesh['tile'=128,'lev'=4] {'lev'}, dimensions={1} | all-to-all | bytes 1277952 | tf_op jit(solution)/shard_map/all_to_all | solution.py:80
  (114 shorter events, 21.8 us)
Async XLA Ops:
  0.0 106.5 %copy-start = (f32[2,2,52,52]{3,1,2,0:T(2,128)S(1)}, f32[2,2,52,52]{3,1,2,0:T(2,128)}, u32[]{:S(2)}) copy-start(f32[2,2,52,52]{3,1,2,0:T(2,128)} %param.10) | copy-start | bytes 129796
  1.5 11.8 %copy-start.1 = (f32[2,13,48,128]{3,2,1,0:T(8,128)S(1)}, f32[2,13,48,128]{3,2,1,0:T(8,128)}, u32[]{:S(2)}) copy-start(f32[2,13,48,128]{3,2,1,0:T(8,128)} %param.6) | copy-start | bytes 1916932
  1.6 27.1 %copy-start.4 = (s32[1,8]{1,0:T(1,128)S(1)}, s32[1,8]{1,0:T(1,128)}, u32[]{:S(2)}) copy-start(s32[1,8]{1,0:T(1,128)} %param.11) | copy-start | bytes 100
  1.8 46.0 %copy-start.3 = (f32[13]{0:T(128)S(1)}, f32[13]{0:T(128)}, u32[]{:S(2)}) copy-start(f32[13]{0:T(128)} %param.7) | copy-start | bytes 160
  1.8 46.0 %copy-start.2 = (s32[48,128]{1,0:T(8,128)S(1)}, s32[48,128]{1,0:T(8,128)}, u32[]{:S(2)}) copy-start(s32[48,128]{1,0:T(8,128)} %param.8) | copy-start | bytes 73732
  2.2 73.9 %collective-permute-start.3 = (f32[2,13,2,48]{3,0,1,2:T(2,128)S(1)}, f32[2,13,2,48]{3,0,1,2:T(2,128)S(1)}, u32[]{:S(2)}, u32[]{:S(2)}) collective-permute-start(f32[2,13,2,48]{3,0,1,2:T(2,128)S(1)} %pad_maximum_fusion.6), channel_id=1, source_target_pairs={{60,0},{0,4},{4,8},{8,12},{12,16},{16,20},{20,24},{24,28},{28,32},... | collective-permute-start | bytes 29960 | tf_op jit(solution)/shard_map/ppermute | solution.py:52
  6.1 70.1 %collective-permute-start.4 = (f32[2,13,2,48]{3,0,1,2:T(2,128)S(1)}, f32[2,13,2,48]{3,0,1,2:T(2,128)S(1)}, u32[]{:S(2)}, u32[]{:S(2)}) collective-permute-start(f32[2,13,2,48]{3,0,1,2:T(2,128)S(1)} %pad_maximum_fusion.6), channel_id=1, source_target_pairs={{4,0},{8,4},{12,8},{16,12},{20,16},{24,20},{28,24},{32,28},{36,32}... | collective-permute-start | bytes 29960 | tf_op jit(solution)/shard_map/ppermute | solution.py:52
  13.4 63.7 %collective-permute-start.6 = (f32[2,13,2,128]{3,0,1,2:T(2,128)S(1)}, f32[2,13,2,128]{3,0,1,2:T(2,128)S(1)}, u32[]{:S(2)}, u32[]{:S(2)}) collective-permute-start(f32[2,13,2,128]{3,0,1,2:T(2,128)S(1)} %copy_dynamic-update-slice_fusion), channel_id=1, source_target_pairs={{64,0},{68,4},{72,8},{76,12},{80,16},{84,20},{88,24},{92,28},{96,3... | collective-permute-start | bytes 79880 | tf_op jit(solution)/shard_map/ppermute | solution.py:52
  24.5 52.8 %collective-permute-start.1 = (f32[2,13,2,128]{3,0,1,2:T(2,128)S(1)}, f32[2,13,2,128]{3,0,1,2:T(2,128)S(1)}, u32[]{:S(2)}, u32[]{:S(2)}) collective-permute-start(f32[2,13,2,128]{3,0,1,2:T(2,128)S(1)} %copy_dynamic-update-slice_fusion), channel_id=1, source_target_pairs={{448,0},{452,4},{456,8},{460,12},{464,16},{468,20},{472,24},{476,2... | collective-permute-start | bytes 79880 | tf_op jit(solution)/shard_map/ppermute | solution.py:52
  26.7 21.2 %collective-permute-start = (f32[2,13,4]{1,0,2:T(2,128)S(1)}, f32[2,13,4]{1,0,2:T(2,128)S(1)}, u32[]{:S(2)}, u32[]{:S(2)}) collective-permute-start(f32[2,13,4]{1,0,2:T(2,128)S(1)} %pad_maximum_fusion.9), channel_id=1, source_target_pairs={{508,0},{448,4},{452,8},{456,12},{460,16},{464,20},{468,24},{472,2... | collective-permute-start | bytes 1256 | tf_op jit(solution)/shard_map/ppermute | solution.py:52
  47.9 8.2 %collective-permute-start.2 = (f32[2,13,4]{1,0,2:T(2,128)S(1)}, f32[2,13,4]{1,0,2:T(2,128)S(1)}, u32[]{:S(2)}, u32[]{:S(2)}) collective-permute-start(f32[2,13,4]{1,0,2:T(2,128)S(1)} %pad_maximum_fusion.9), channel_id=1, source_target_pairs={{452,0},{456,4},{460,8},{464,12},{468,16},{472,20},{476,24},{480,2... | collective-permute-start | bytes 1256 | tf_op jit(solution)/shard_map/ppermute | solution.py:52
  56.1 10.9 %collective-permute-start.5 = (f32[2,13,4]{1,0,2:T(2,128)S(1)}, f32[2,13,4]{1,0,2:T(2,128)S(1)}, u32[]{:S(2)}, u32[]{:S(2)}) collective-permute-start(f32[2,13,4]{1,0,2:T(2,128)S(1)} %pad_maximum_fusion.9), channel_id=1, source_target_pairs={{124,0},{64,4},{68,8},{72,12},{76,16},{80,20},{84,24},{88,28},{92,... | collective-permute-start | bytes 1256 | tf_op jit(solution)/shard_map/ppermute | solution.py:52
  67.0 8.8 %collective-permute-start.7 = (f32[2,13,4]{1,0,2:T(2,128)S(1)}, f32[2,13,4]{1,0,2:T(2,128)S(1)}, u32[]{:S(2)}, u32[]{:S(2)}) collective-permute-start(f32[2,13,4]{1,0,2:T(2,128)S(1)} %pad_maximum_fusion.9), channel_id=1, source_target_pairs={{68,0},{72,4},{76,8},{80,12},{84,16},{88,20},{92,24},{96,28},{100,... | collective-permute-start | bytes 1256 | tf_op jit(solution)/shard_map/ppermute | solution.py:52
  88.6 17.6 %all-to-all-start = ((f32[2,13,48,128]{3,0,1,2:T(2,128)}), f32[2,13,48,128]{3,0,1,2:T(2,128)S(1)}, u32[]{:S(2)}, u32[]{:S(2)}) async-start(f32[2,13,48,128]{3,0,1,2:T(2,128)} %copy.353), calls=%async_computation | async-start | bytes 1277952 | tf_op jit(solution)/shard_map/all_to_all | solution.py:75
  121.2 24.3 %collective-permute-start.13 = (f32[2,13,4]{1,0,2:T(2,128)S(1)}, f32[2,13,4]{1,0,2:T(2,128)S(1)}, u32[]{:S(2)}, u32[]{:S(2)}) collective-permute-start(f32[2,13,4]{1,0,2:T(2,128)S(1)} %pad_maximum_fusion.10), channel_id=1, source_target_pairs={{124,0},{64,4},{68,8},{72,12},{76,16},{80,20},{84,24},{88,28},{92,... | collective-permute-start | bytes 1256 | tf_op jit(solution)/shard_map/ppermute | solution.py:52
  123.2 29.7 %collective-permute-start.15 = (f32[2,13,4]{1,0,2:T(2,128)S(1)}, f32[2,13,4]{1,0,2:T(2,128)S(1)}, u32[]{:S(2)}, u32[]{:S(2)}) collective-permute-start(f32[2,13,4]{1,0,2:T(2,128)S(1)} %pad_maximum_fusion.10), channel_id=1, source_target_pairs={{68,0},{72,4},{76,8},{80,12},{84,16},{88,20},{92,24},{96,28},{100,... | collective-permute-start | bytes 1256 | tf_op jit(solution)/shard_map/ppermute | solution.py:52
  133.4 31.1 %collective-permute-start.14 = (f32[2,13,2,128]{3,0,1,2:T(2,128)S(1)}, f32[2,13,2,128]{3,0,1,2:T(2,128)S(1)}, u32[]{:S(2)}, u32[]{:S(2)}) collective-permute-start(f32[2,13,2,128]{3,0,1,2:T(2,128)S(1)} %pad_maximum_fusion.7), channel_id=1, source_target_pairs={{64,0},{68,4},{72,8},{76,12},{80,16},{84,20},{88,24},{92,28},{96,3... | collective-permute-start | bytes 79880 | tf_op jit(solution)/shard_map/ppermute | solution.py:52
  140.1 24.5 %collective-permute-start.9 = (f32[2,13,2,128]{3,0,1,2:T(2,128)S(1)}, f32[2,13,2,128]{3,0,1,2:T(2,128)S(1)}, u32[]{:S(2)}, u32[]{:S(2)}) collective-permute-start(f32[2,13,2,128]{3,0,1,2:T(2,128)S(1)} %pad_maximum_fusion.7), channel_id=1, source_target_pairs={{448,0},{452,4},{456,8},{460,12},{464,16},{468,20},{472,24},{476,2... | collective-permute-start | bytes 79880 | tf_op jit(solution)/shard_map/ppermute | solution.py:52
  142.0 12.8 %collective-permute-start.8 = (f32[2,13,4]{1,0,2:T(2,128)S(1)}, f32[2,13,4]{1,0,2:T(2,128)S(1)}, u32[]{:S(2)}, u32[]{:S(2)}) collective-permute-start(f32[2,13,4]{1,0,2:T(2,128)S(1)} %pad_maximum_fusion.10), channel_id=1, source_target_pairs={{508,0},{448,4},{452,8},{456,12},{460,16},{464,20},{468,24},{472,2... | collective-permute-start | bytes 1256 | tf_op jit(solution)/shard_map/ppermute | solution.py:52
  145.5 17.2 %collective-permute-start.10 = (f32[2,13,4]{1,0,2:T(2,128)S(1)}, f32[2,13,4]{1,0,2:T(2,128)S(1)}, u32[]{:S(2)}, u32[]{:S(2)}) collective-permute-start(f32[2,13,4]{1,0,2:T(2,128)S(1)} %pad_maximum_fusion.10), channel_id=1, source_target_pairs={{452,0},{456,4},{460,8},{464,12},{468,16},{472,20},{476,24},{480,2... | collective-permute-start | bytes 1256 | tf_op jit(solution)/shard_map/ppermute | solution.py:52
  152.9 10.3 %collective-permute-start.11 = (f32[2,13,2,48]{3,0,1,2:T(2,128)S(1)}, f32[2,13,2,48]{3,0,1,2:T(2,128)S(1)}, u32[]{:S(2)}, u32[]{:S(2)}) collective-permute-start(f32[2,13,2,48]{3,0,1,2:T(2,128)S(1)} %pad_maximum_fusion.8), channel_id=1, source_target_pairs={{60,0},{0,4},{4,8},{8,12},{12,16},{16,20},{20,24},{24,28},{28,32},... | collective-permute-start | bytes 29960 | tf_op jit(solution)/shard_map/ppermute | solution.py:52
  154.8 8.8 %collective-permute-start.12 = (f32[2,13,2,48]{3,0,1,2:T(2,128)S(1)}, f32[2,13,2,48]{3,0,1,2:T(2,128)S(1)}, u32[]{:S(2)}, u32[]{:S(2)}) collective-permute-start(f32[2,13,2,48]{3,0,1,2:T(2,128)S(1)} %pad_maximum_fusion.8), channel_id=1, source_target_pairs={{4,0},{8,4},{12,8},{16,12},{20,16},{24,20},{28,24},{32,28},{36,32}... | collective-permute-start | bytes 29960 | tf_op jit(solution)/shard_map/ppermute | solution.py:52

commit v2 on v1

--- a/solution.py
+++ b/solution.py
@@ -43,21 +43,39 @@
 
 def horizontal(field, rate, wet, codes):
     count = lax.axis_size("tile")
-    row_pair = jnp.stack([field[..., 0, :], field[..., -1, :]], axis=-2)
-    col_pair = jnp.stack([field[..., :, 0], field[..., :, -1]], axis=-2)
     corner_set = jnp.stack(
         [field[..., 0, 0], field[..., 0, -1], field[..., -1, 0], field[..., -1, -1]], axis=-1
     )
-    payloads = [row_pair, row_pair, col_pair, col_pair] + [corner_set] * 4
-    got = [lax.ppermute(payloads[slot], "tile", slot_pairs(count, slot)) for slot in range(8)]
-    south = pick(got[0], codes[0])
-    north = pick(got[1], codes[1])
-    west = pick(got[2], codes[2])
-    east = pick(got[3], codes[3])
+    side = jnp.concatenate([field[..., :, 0], field[..., :, -1], corner_set], axis=-1)
+    from_west = lax.ppermute(side, "tile", slot_pairs(count, 2))
+    from_east = lax.ppermute(side, "tile", slot_pairs(count, 3))
+    cols = field.shape[-1]
+    rows = field.shape[-2]
+    span = 2 * rows
+    upright = jnp.concatenate(
+        [field[..., 0, :], field[..., -1, :], from_west[..., span:], from_east[..., span:]], axis=-1
+    )
+    from_south = lax.ppermute(upright, "tile", slot_pairs(count, 0))
+    from_north = lax.ppermute(upright, "tile", slot_pairs(count, 1))
+
+    def strips(got, length):
+        return jnp.stack([got[..., :length], got[..., length : 2 * length]], axis=-2)
+
+    south = pick(strips(from_south, cols), codes[0])
+    north = pick(strips(from_north, cols), codes[1])
+    west = pick(strips(from_west, rows), codes[2])
+    east = pick(strips(from_east, rows), codes[3])
+    base = 2 * cols
+    sources = [
+        (from_south, base),
+        (from_south, base + 4),
+        (from_north, base),
+        (from_north, base + 4),
+    ]
     corners = []
-    for slot in range(4, 8):
-        cell = got[slot]
+    for slot, (got, first) in zip(range(4, 8), sources):
         code = codes[slot]
+        cell = got[..., first : first + 4]
         value = jnp.where(
             code == 0,
             cell[..., 0],

time: 208 us -> 160 us (0.77)
  starting transfers between devices: 91.7 us -> 46.2 us
  waiting for transfers between devices: 19.3 us -> 13.9 us
    ppermute x16 -> x8, starting transfers between devices: 83.3 us -> 40.1 us  [the longest x2 15 us: horizontal(): from_east = lax.ppermute(side, 'tile', slot_pairs(count, 3))]
    ppermute x16 -> x8, waiting for transfers between devices: 10.8 us -> 5.41 us  [the longest x2 4.68 us: horizontal(): from_south = lax.ppermute(upright, 'tile', slot_pairs(count, 0))]
    all_to_all x1, starting transfers between devices: 8.4 us -> 6.11 us  [column_mix(): columns = lax.all_to_all(lateral, 'lev', 2, 1, tiled=True)]
  transfers between devices with their start and end apart: 17 -> 9, of which waited for: 5 -> 4; matrix products, arithmetic and copies ran while one was open for 3% -> 3% of each run, Pallas kernels for 0% -> 0%
where the time goes in v2:
time: 160 us; the launch traced here: 158 us
  starting transfers between devices  46.2 us (29%)
  blocking collectives  39.8 us (25%)
  other arithmetic  22.8 us (14%)
  between operations  18.9 us (12%)
  waiting for transfers between devices  13.9 us (9%)
  local copies, waits for them, and re-layouts  13.8 us (9%)
  matrix products  2.55 us (2%)
    all_to_all x2, blocking collectives, column_mix(): return lax.all_to_all(mixed, 'lev', 1, 2, tiled=True)  24.8 us
    ppermute x2, starting transfers between devices, horizontal(): from_east = lax.ppermute(side, 'tile', slot_pairs(count, 3))  15 us
    all_to_all x1, blocking collectives, column_mix(): columns = lax.all_to_all(lateral, 'lev', 2, 1, tiled=True)  15 us
    ppermute x2, starting transfers between devices, horizontal(): from_north = lax.ppermute(upright, 'tile', slot_pairs(count, 1))  13 us
    concatenate x2, other arithmetic, horizontal(): jnp.concatenate([top_row[..., None, :], middle, bottom_row[..., None, :]]...  10.1 us
    mul x2, other arithmetic, stencil(): wet * ((1.0 - 6.0 * rate) * field + rate * edge_sum + 0.5 * rate * diag_sum)  9.79 us
    all_to_all x1, waiting for transfers between devices, column_mix(): columns = lax.all_to_all(lateral, 'lev', 2, 1, tiled=True)  8.49 us
    ppermute x2, starting transfers between devices, horizontal(): from_south = lax.ppermute(upright, 'tile', slot_pairs(count, 0))  6.18 us
  transfers between devices with their start and end apart: 9, of which 4 were waited for; matrix products, arithmetic and copies ran while one was open for 3% of the time, Pallas kernels for 0%

profile of v2, /device:TPU:1, one launch (start us, length us, event | category | flops | bytes accessed | tf_op | source)
XLA Modules:
  0.0 157.9 jit_solution(4196648744160838649)
XLA Ops:
  0.0 1.4 slice_reduce_fusion
  1.4 1.5 fusion.41
  4.1 3.9 %collective-permute-start = (f32[2,13,100]{2,0,1:T(2,128)S(1)}, f32[2,13,100]{2,0,1:T(2,128)S(1)}, u32[]{:S(2)}, u32[]{:S(2)}) collective-permute-start(f32[2,13,100]{2,0,1:T(2,128)S(1)} %concatenate.64), channel_id=1, source_target_pairs={{60,0},{0,4},{4,8},{8,12},{12,16},{16,20},{20,24},{24,28},{28,32},... | collective-permute-start | bytes 31208 | tf_op jit(solution)/shard_map/ppermute | solution.py:50
  8.1 7.2 %collective-permute-start.1 = (f32[2,13,100]{2,0,1:T(2,128)S(1)}, f32[2,13,100]{2,0,1:T(2,128)S(1)}, u32[]{:S(2)}, u32[]{:S(2)}) collective-permute-start(f32[2,13,100]{2,0,1:T(2,128)S(1)} %concatenate.64), channel_id=1, source_target_pairs={{4,0},{8,4},{12,8},{16,12},{20,16},{24,20},{28,24},{32,28},{36,32}... | collective-permute-start | bytes 31208 | tf_op jit(solution)/shard_map/ppermute | solution.py:51
  35.0 11.1 %collective-permute-start.3 = (f32[2,13,264]{2,0,1:T(2,128)S(1)}, f32[2,13,264]{2,0,1:T(2,128)S(1)}, u32[]{:S(2)}, u32[]{:S(2)}) collective-permute-start(f32[2,13,264]{2,0,1:T(2,128)S(1)} %pad_maximum_fusion.6), channel_id=1, source_target_pairs={{64,0},{68,4},{72,8},{76,12},{80,16},{84,20},{88,24},{92,28},{96,3... | collective-permute-start | bytes 82376 | tf_op jit(solution)/shard_map/ppermute | solution.py:59
  46.1 1.9 %collective-permute-start.2 = (f32[2,13,264]{2,0,1:T(2,128)S(1)}, f32[2,13,264]{2,0,1:T(2,128)S(1)}, u32[]{:S(2)}, u32[]{:S(2)}) collective-permute-start(f32[2,13,264]{2,0,1:T(2,128)S(1)} %pad_maximum_fusion.6), channel_id=1, source_target_pairs={{448,0},{452,4},{456,8},{460,12},{464,16},{468,20},{472,24},{476,2... | collective-permute-start | bytes 82376 | tf_op jit(solution)/shard_map/ppermute | solution.py:58
  49.4 3.5 %collective-permute-done.2 = f32[2,13,264]{2,0,1:T(2,128)S(1)} collective-permute-done((f32[2,13,264]{2,0,1:T(2,128)S(1)}, f32[2,13,264]{2,0,1:T(2,128)S(1)}, u32[]{:S(2)}, u32[]{:S(2)}) %collective-permute-start.2) | collective-permute-done | bytes 27488 | tf_op jit(solution)/shard_map/ppermute | solution.py:58
  53.6 5.0 %maximum_maximum_fusion = (f32[2,13,49,130]{3,0,2,1:T(2,128)S(1)}, f32[2,13,49,130]{3,0,2,1:T(2,128)S(1)}) fusion(f32[2,13,48,1]{3,0,2,1:T(2,128)S(1)} %copy.199, f32[2,13,48,128]{3,0,2,1:T(2,128)S(1)} %copy.188, f32[2,13,48,1]{3,0,2,1:T(2,128)S(1)} %copy.197, f32[2,13,1,130]{3,0,2,1:T(2,128)S(1)} %maximum_bitcast_fusion, ...), kind=kLoop, calls=%fused_computation.2 | loop fusion | flops 993720 | bytes 2000960 | tf_op jit(solution)/shard_map/concatenate | solution.py:88
  58.7 4.9 %fusion.14 = f32[2,13,48,128]{3,0,2,1:T(2,128)S(1)} fusion(f32[2,13,49,130]{3,0,2,1:T(2,128)S(1)} %get-tuple-element.12, f32[2,13,49,130]{3,0,2,1:T(2,128)S(1)} %get-tuple-element.11, f32[2,13,48,1]{3,0,2,1:T(2,128)S(1)} %copy.199, f32[2,13,48,128]{3,0,2,1:T(2,128)S(1)} %copy.188, f32[2,13,48,1]{3,0,2,1:T(2,128)S(1)} %copy.197, f32[13]{0:T(128)S(1)} %get-tuple-element.34, ...), kind=kLoop, calls=%fused_computation.31 | loop fusion | flops 2236416 | bytes 5146524 | tf_op jit(solution)/shard_map/mul | solution.py:41
  63.6 1.1 copy.205
  64.6 6.1 %all-to-all-start = ((f32[2,13,48,128]{3,0,1,2:T(2,128)}), f32[2,13,48,128]{3,0,1,2:T(2,128)S(1)}, u32[]{:S(2)}, u32[]{:S(2)}) async-start(f32[2,13,48,128]{3,0,1,2:T(2,128)} %copy.205), calls=%async_computation | async-start | bytes 1277952 | tf_op jit(solution)/shard_map/all_to_all | solution.py:93
  71.5 8.5 %all-to-all-done = f32[2,13,48,128]{3,0,1,2:T(2,128)S(1)} async-done(((f32[2,13,48,128]{3,0,1,2:T(2,128)}), f32[2,13,48,128]{3,0,1,2:T(2,128)S(1)}, u32[]{:S(2)}, u32[]{:S(2)}) %all-to-all-start) | async-done | bytes 639008 | tf_op jit(solution)/shard_map/all_to_all | solution.py:93
  80.2 1.3 convolution_bitcast_fusion.1
  82.1 12.4 %all_to_all.72 = f32[2,52,12,128]{3,0,2,1:T(2,128)S(1)} all-to-all(f32[2,52,12,128]{3,0,2,1:T(2,128)S(1)} %copy.211), channel_id=1, replica_groups=mesh['tile'=128,'lev'=4] {'lev'}, dimensions={1} | all-to-all | bytes 1277952 | tf_op jit(solution)/shard_map/all_to_all | solution.py:98
  96.9 1.9 %collective-permute-start.4 = (f32[2,13,100]{2,0,1:T(2,128)S(1)}, f32[2,13,100]{2,0,1:T(2,128)S(1)}, u32[]{:S(2)}, u32[]{:S(2)}) collective-permute-start(f32[2,13,100]{2,0,1:T(2,128)S(1)} %concatenate.73), channel_id=1, source_target_pairs={{60,0},{0,4},{4,8},{8,12},{12,16},{16,20},{20,24},{24,28},{28,32},... | collective-permute-start | bytes 31208 | tf_op jit(solution)/shard_map/ppermute | solution.py:50
  98.9 7.9 %collective-permute-start.5 = (f32[2,13,100]{2,0,1:T(2,128)S(1)}, f32[2,13,100]{2,0,1:T(2,128)S(1)}, u32[]{:S(2)}, u32[]{:S(2)}) collective-permute-start(f32[2,13,100]{2,0,1:T(2,128)S(1)} %concatenate.73), channel_id=1, source_target_pairs={{4,0},{8,4},{12,8},{16,12},{20,16},{24,20},{28,24},{32,28},{36,32}... | collective-permute-start | bytes 31208 | tf_op jit(solution)/shard_map/ppermute | solution.py:51
  107.7 1.9 %collective-permute-start.7 = (f32[2,13,264]{2,0,1:T(2,128)S(1)}, f32[2,13,264]{2,0,1:T(2,128)S(1)}, u32[]{:S(2)}, u32[]{:S(2)}) collective-permute-start(f32[2,13,264]{2,0,1:T(2,128)S(1)} %pad_maximum_fusion.7), channel_id=1, source_target_pairs={{64,0},{68,4},{72,8},{76,12},{80,16},{84,20},{88,24},{92,28},{96,3... | collective-permute-start | bytes 82376 | tf_op jit(solution)/shard_map/ppermute | solution.py:59
  109.7 4.3 %collective-permute-start.6 = (f32[2,13,264]{2,0,1:T(2,128)S(1)}, f32[2,13,264]{2,0,1:T(2,128)S(1)}, u32[]{:S(2)}, u32[]{:S(2)}) collective-permute-start(f32[2,13,264]{2,0,1:T(2,128)S(1)} %pad_maximum_fusion.7), channel_id=1, source_target_pairs={{448,0},{452,4},{456,8},{460,12},{464,16},{468,20},{472,24},{476,2... | collective-permute-start | bytes 82376 | tf_op jit(solution)/shard_map/ppermute | solution.py:58
  115.3 1.2 collective-permute-done.6
  117.2 5.0 %maximum_maximum_fusion.1 = (f32[2,13,49,130]{3,0,2,1:T(2,128)S(1)}, f32[2,13,49,130]{3,0,2,1:T(2,128)S(1)}) fusion(f32[2,13,48,1]{3,0,2,1:T(2,128)S(1)} %copy.225, f32[2,13,48,128]{3,0,2,1:T(2,128)S(1)} %bitcast.112, f32[2,13,48,1]{3,0,2,1:T(2,128)S(1)} %copy.224, f32[2,13,1,130]{3,0,2,1:T(2,128)S(1)} %maximum_bitcast_fusion.2, ...), kind=kLoop, calls=%fused_computation.4 | loop fusion | flops 993720 | bytes 2000960 | tf_op jit(solution)/shard_map/concatenate | solution.py:88
  122.3 4.9 %fusion.7 = f32[2,13,48,128]{3,0,2,1:T(2,128)S(1)} fusion(f32[2,13,49,130]{3,0,2,1:T(2,128)S(1)} %get-tuple-element.10, f32[2,13,49,130]{3,0,2,1:T(2,128)S(1)} %get-tuple-element.9, f32[2,13,48,1]{3,0,2,1:T(2,128)S(1)} %copy.225, f32[2,13,48,128]{3,0,2,1:T(2,128)S(1)} %bitcast.113, f32[2,13,48,1]{3,0,2,1:T(2,128)S(1)} %copy.224, ...), kind=kLoop, calls=%fused_computation.18 | loop fusion | flops 2236416 | bytes 5146524 | tf_op jit(solution)/shard_map/mul | solution.py:41
  127.4 15.0 %all_to_all.73 = f32[2,13,48,128]{3,0,1,2:T(2,128)S(1)} all-to-all(f32[2,13,48,128]{3,0,1,2:T(2,128)S(1)} %copy.230), channel_id=1, replica_groups=mesh['tile'=128,'lev'=4] {'lev'}, dimensions={2} | all-to-all | bytes 1277952 | tf_op jit(solution)/shard_map/all_to_all | solution.py:93
  142.6 1.3 convolution_bitcast_fusion
  144.5 12.5 %all_to_all.74 = f32[2,52,12,128]{3,0,2,1:T(2,128)S(1)} all-to-all(f32[2,52,12,128]{3,0,2,1:T(2,128)S(1)} %copy.236), channel_id=1, replica_groups=mesh['tile'=128,'lev'=4] {'lev'}, dimensions={1} | all-to-all | bytes 1277952 | tf_op jit(solution)/shard_map/all_to_all | solution.py:98
  (97 shorter events, 13.5 us)
Async XLA Ops:
  0.0 80.2 %copy-start = (f32[2,2,52,52]{3,1,2,0:T(2,128)S(1)}, f32[2,2,52,52]{3,1,2,0:T(2,128)}, u32[]{:S(2)}) copy-start(f32[2,2,52,52]{3,1,2,0:T(2,128)} %param.10) | copy-start | bytes 129796
  2.9 12.3 %copy-start.1 = (f32[2,13,48,128]{3,2,1,0:T(8,128)S(1)}, f32[2,13,48,128]{3,2,1,0:T(8,128)}, u32[]{:S(2)}) copy-start(f32[2,13,48,128]{3,2,1,0:T(8,128)} %param.6) | copy-start | bytes 1916932
  2.9 12.4 %copy-start.4 = (s32[1,8]{1,0:T(1,128)S(1)}, s32[1,8]{1,0:T(1,128)}, u32[]{:S(2)}) copy-start(s32[1,8]{1,0:T(1,128)} %param.11) | copy-start | bytes 100
  2.9 12.4 %copy-start.3 = (f32[13]{0:T(128)S(1)}, f32[13]{0:T(128)}, u32[]{:S(2)}) copy-start(f32[13]{0:T(128)} %param.7) | copy-start | bytes 160
  3.6 31.1 %copy-start.2 = (s32[48,128]{1,0:T(8,128)S(1)}, s32[48,128]{1,0:T(8,128)}, u32[]{:S(2)}) copy-start(s32[48,128]{1,0:T(8,128)} %param.8) | copy-start | bytes 73732
  4.1 30.6 %collective-permute-start = (f32[2,13,100]{2,0,1:T(2,128)S(1)}, f32[2,13,100]{2,0,1:T(2,128)S(1)}, u32[]{:S(2)}, u32[]{:S(2)}) collective-permute-start(f32[2,13,100]{2,0,1:T(2,128)S(1)} %concatenate.64), channel_id=1, source_target_pairs={{60,0},{0,4},{4,8},{8,12},{12,16},{16,20},{20,24},{24,28},{28,32},... | collective-permute-start | bytes 31208 | tf_op jit(solution)/shard_map/ppermute | solution.py:50
  8.1 26.7 %collective-permute-start.1 = (f32[2,13,100]{2,0,1:T(2,128)S(1)}, f32[2,13,100]{2,0,1:T(2,128)S(1)}, u32[]{:S(2)}, u32[]{:S(2)}) collective-permute-start(f32[2,13,100]{2,0,1:T(2,128)S(1)} %concatenate.64), channel_id=1, source_target_pairs={{4,0},{8,4},{12,8},{16,12},{20,16},{24,20},{28,24},{32,28},{36,32}... | collective-permute-start | bytes 31208 | tf_op jit(solution)/shard_map/ppermute | solution.py:51
  35.0 14.3 %collective-permute-start.3 = (f32[2,13,264]{2,0,1:T(2,128)S(1)}, f32[2,13,264]{2,0,1:T(2,128)S(1)}, u32[]{:S(2)}, u32[]{:S(2)}) collective-permute-start(f32[2,13,264]{2,0,1:T(2,128)S(1)} %pad_maximum_fusion.6), channel_id=1, source_target_pairs={{64,0},{68,4},{72,8},{76,12},{80,16},{84,20},{88,24},{92,28},{96,3... | collective-permute-start | bytes 82376 | tf_op jit(solution)/shard_map/ppermute | solution.py:59
  46.1 6.8 %collective-permute-start.2 = (f32[2,13,264]{2,0,1:T(2,128)S(1)}, f32[2,13,264]{2,0,1:T(2,128)S(1)}, u32[]{:S(2)}, u32[]{:S(2)}) collective-permute-start(f32[2,13,264]{2,0,1:T(2,128)S(1)} %pad_maximum_fusion.6), channel_id=1, source_target_pairs={{448,0},{452,4},{456,8},{460,12},{464,16},{468,20},{472,24},{476,2... | collective-permute-start | bytes 82376 | tf_op jit(solution)/shard_map/ppermute | solution.py:58
  64.6 15.3 %all-to-all-start = ((f32[2,13,48,128]{3,0,1,2:T(2,128)}), f32[2,13,48,128]{3,0,1,2:T(2,128)S(1)}, u32[]{:S(2)}, u32[]{:S(2)}) async-start(f32[2,13,48,128]{3,0,1,2:T(2,128)} %copy.205), calls=%async_computation | async-start | bytes 1277952 | tf_op jit(solution)/shard_map/all_to_all | solution.py:93
  96.9 9.8 %collective-permute-start.4 = (f32[2,13,100]{2,0,1:T(2,128)S(1)}, f32[2,13,100]{2,0,1:T(2,128)S(1)}, u32[]{:S(2)}, u32[]{:S(2)}) collective-permute-start(f32[2,13,100]{2,0,1:T(2,128)S(1)} %concatenate.73), channel_id=1, source_target_pairs={{60,0},{0,4},{4,8},{8,12},{12,16},{16,20},{20,24},{24,28},{28,32},... | collective-permute-start | bytes 31208 | tf_op jit(solution)/shard_map/ppermute | solution.py:50
  98.9 8.7 %collective-permute-start.5 = (f32[2,13,100]{2,0,1:T(2,128)S(1)}, f32[2,13,100]{2,0,1:T(2,128)S(1)}, u32[]{:S(2)}, u32[]{:S(2)}) collective-permute-start(f32[2,13,100]{2,0,1:T(2,128)S(1)} %concatenate.73), channel_id=1, source_target_pairs={{4,0},{8,4},{12,8},{16,12},{20,16},{24,20},{28,24},{32,28},{36,32}... | collective-permute-start | bytes 31208 | tf_op jit(solution)/shard_map/ppermute | solution.py:51
  107.7 7.5 %collective-permute-start.7 = (f32[2,13,264]{2,0,1:T(2,128)S(1)}, f32[2,13,264]{2,0,1:T(2,128)S(1)}, u32[]{:S(2)}, u32[]{:S(2)}) collective-permute-start(f32[2,13,264]{2,0,1:T(2,128)S(1)} %pad_maximum_fusion.7), channel_id=1, source_target_pairs={{64,0},{68,4},{72,8},{76,12},{80,16},{84,20},{88,24},{92,28},{96,3... | collective-permute-start | bytes 82376 | tf_op jit(solution)/shard_map/ppermute | solution.py:59
  109.7 6.8 %collective-permute-start.6 = (f32[2,13,264]{2,0,1:T(2,128)S(1)}, f32[2,13,264]{2,0,1:T(2,128)S(1)}, u32[]{:S(2)}, u32[]{:S(2)}) collective-permute-start(f32[2,13,264]{2,0,1:T(2,128)S(1)} %pad_maximum_fusion.7), channel_id=1, source_target_pairs={{448,0},{452,4},{456,8},{460,12},{464,16},{468,20},{472,24},{476,2... | collective-permute-start | bytes 82376 | tf_op jit(solution)/shard_map/ppermute | solution.py:58

commit v3 on v2

--- a/solution.py
+++ b/solution.py
@@ -89,27 +89,42 @@
     return stencil(extended, field, rate, wet)
 
 
-def column_mix(lateral, mixing_inverse, convective_rows):
-    columns = lax.all_to_all(lateral, "lev", 2, 1, tiled=True)
-    both_states = jnp.einsum(
-        "tsml,tmxy->tslxy", mixing_inverse, columns, precision=lax.Precision.HIGHEST
+def column_mix(lateral, stacked_inverse, convective_rows):
+    parts = lax.axis_size("lev")
+    tracers, depth, rows, cols = lateral.shape
+    part_rows = rows // parts
+    outgoing = jnp.transpose(
+        lateral.reshape(tracers, depth, parts, part_rows, cols), (2, 0, 1, 3, 4)
     )
-    mixed = jnp.where(convective_rows[None, None], both_states[:, 1], both_states[:, 0])
-    return lax.all_to_all(mixed, "lev", 1, 2, tiled=True)
+    columns = lax.all_to_all(outgoing, "lev", 0, 0, tiled=True)
+    mixed = []
+    for tracer in range(tracers):
+        flat = columns[:, tracer].reshape(parts * depth, part_rows * cols)
+        both_states = jnp.dot(
+            stacked_inverse[tracer], flat, precision=lax.Precision.HIGHEST
+        ).reshape(2, parts, depth, part_rows, cols)
+        mixed.append(jnp.where(convective_rows[None, None], both_states[1], both_states[0]))
+    returning = lax.all_to_all(jnp.stack(mixed, axis=1), "lev", 0, 0, tiled=True)
+    return jnp.transpose(returning, (1, 2, 0, 3, 4)).reshape(tracers, depth, rows, cols)
 
 
 def local(forcing, lateral_mix, sea_mask, convective, mixing_inverse, seam_links):
-    wet = sea_mask.astype(jnp.float32)[None, None]
-    rate = lateral_mix[None, :, None, None]
+    wet = sea_mask.astype(jnp.float32)[None]
+    plane_rate = jnp.tile(lateral_mix, forcing.shape[0])[:, None, None]
     codes = seam_links[0] % 4
     parts = lax.axis_size("lev")
     rows = forcing.shape[2] // parts
     lev_here = lax.axis_index("lev")
     convective_rows = lax.dynamic_slice_in_dim(convective, lev_here * rows, rows, axis=0) == 1
+    stacked_inverse = jnp.swapaxes(mixing_inverse, 2, 3).reshape(
+        mixing_inverse.shape[0], -1, mixing_inverse.shape[2]
+    )
+    tracers, depth, rows, cols = forcing.shape
     adjoint = forcing
     for step in range(STEPS):
-        lateral = horizontal(adjoint, rate, wet, codes)
-        adjoint = column_mix(lateral, mixing_inverse, convective_rows)
+        planes = adjoint.reshape(tracers * depth, rows, cols)
+        lateral = horizontal(planes, plane_rate, wet, codes)
+        adjoint = column_mix(lateral.reshape(tracers, depth, rows, cols), stacked_inverse, convective_rows)
     return adjoint
 
 

time: 160 us -> 152 us (0.950)
  other arithmetic: 22.8 us -> 7.51 us
  waiting for transfers between devices: 13.9 us -> 20.2 us
  local copies, waits for them, and re-layouts: 13.8 us -> 16.3 us
    concatenate x2, other arithmetic: 10.1 us -> 2.27 us  [horizontal(): jnp.concatenate([top_row[..., None, :], middle, bottom_row[..., None, :]]...]
    mul x2, other arithmetic: 9.79 us -> 2.67 us  [stencil(): wet * ((1.0 - 6.0 * rate) * field + rate * edge_sum + 0.5 * rate * diag_sum)]
    ppermute x2, waiting for transfers between devices: 0.01 us -> 6.94 us  [horizontal(): from_west = lax.ppermute(side, 'tile', slot_pairs(count, 2))]
    slice x3 -> x7, local copies, waits for them, and re-layouts: 0.29 us -> 3.52 us  [the longest x2 3.33 us: column_mix(): flat = columns[:, tracer].reshape(parts * depth, part_rows * cols)]
    ppermute x2, starting transfers between devices: 15 us -> 17.3 us  [horizontal(): from_east = lax.ppermute(side, 'tile', slot_pairs(count, 3))]
    ppermute x2, starting transfers between devices: 5.87 us -> 3.84 us  [horizontal(): from_west = lax.ppermute(side, 'tile', slot_pairs(count, 2))]
    transpose x0 -> x4, local copies, waits for them, and re-layouts: none -> 1.98 us  [the longest x2 1.82 us: column_mix(): jnp.transpose(lateral.reshape(tracers, depth, parts, part_rows, cols), (2...]
where the time goes in v3:
time: 152 us; the launch traced here: 151 us
  starting transfers between devices  45.9 us (30%)
  blocking collectives  40.1 us (26%)
  waiting for transfers between devices  20.2 us (13%)
  between operations  18.3 us (12%)
  local copies, waits for them, and re-layouts  16.3 us (11%)
  other arithmetic  7.51 us (5%)
  matrix products  2.85 us (2%)
    all_to_all x2, blocking collectives, column_mix(): lax.all_to_all(jnp.stack(mixed, axis=1), 'lev', 0, 0, tiled=True)  24.8 us
    ppermute x2, starting transfers between devices, horizontal(): from_east = lax.ppermute(side, 'tile', slot_pairs(count, 3))  17.3 us
    all_to_all x1, blocking collectives, column_mix(): columns = lax.all_to_all(outgoing, 'lev', 0, 0, tiled=True)  15.3 us
    ppermute x2, starting transfers between devices, horizontal(): from_north = lax.ppermute(upright, 'tile', slot_pairs(count, 1))  12.6 us
    all_to_all x1, waiting for transfers between devices, column_mix(): columns = lax.all_to_all(outgoing, 'lev', 0, 0, tiled=True)  8.28 us
    ppermute x2, waiting for transfers between devices, horizontal(): from_west = lax.ppermute(side, 'tile', slot_pairs(count, 2))  6.94 us
    ppermute x2, starting transfers between devices, horizontal(): from_south = lax.ppermute(upright, 'tile', slot_pairs(count, 0))  6.36 us
    all_to_all x1, starting transfers between devices, column_mix(): columns = lax.all_to_all(outgoing, 'lev', 0, 0, tiled=True)  5.83 us
  transfers between devices with their start and end apart: 9, of which 4 were waited for; matrix products, arithmetic and copies ran while one was open for 3% of the time, Pallas kernels for 0%

profile of v3, /device:TPU:1, one launch (start us, length us, event | category | flops | bytes accessed | tf_op | source)
XLA Modules:
  0.0 151.2 jit_solution(16533297568491687511)
XLA Ops:
  0.0 1.2 fusion.39
  1.2 1.6 %fusion.40 = (f32[26,48,1]{2,1,0:T(8,128)S(1)}, f32[26,48,1]{2,1,0:T(8,128)S(1)}) fusion(f32[26,48,128]{2,1,0:T(8,128)} %bitcast.110), kind=kLoop, calls=%fused_computation.118 | loop fusion | bytes 19968 | tf_op jit(solution)/shard_map/slice | solution.py:49
  3.5 9.2 %collective-permute-start.1 = (f32[26,100]{1,0:T(8,128)S(1)}, f32[26,100]{1,0:T(8,128)S(1)}, u32[]{:S(2)}, u32[]{:S(2)}) collective-permute-start(f32[26,100]{1,0:T(8,128)S(1)} %concatenate.64), channel_id=1, source_target_pairs={{4,0},{8,4},{12,8},{16,12},{20,16},{24,20},{28,24},{32,28},{36,32}... | collective-permute-start | bytes 31208 | tf_op jit(solution)/shard_map/ppermute | solution.py:51
  12.7 1.9 %collective-permute-start = (f32[26,100]{1,0:T(8,128)S(1)}, f32[26,100]{1,0:T(8,128)S(1)}, u32[]{:S(2)}, u32[]{:S(2)}) collective-permute-start(f32[26,100]{1,0:T(8,128)S(1)} %concatenate.64), channel_id=1, source_target_pairs={{60,0},{0,4},{4,8},{8,12},{12,16},{16,20},{20,24},{24,28},{28,32},... | collective-permute-start | bytes 31208 | tf_op jit(solution)/shard_map/ppermute | solution.py:50
  33.3 10.7 %collective-permute-start.3 = (f32[26,264]{1,0:T(8,128)S(1)}, f32[26,264]{1,0:T(8,128)S(1)}, u32[]{:S(2)}, u32[]{:S(2)}) collective-permute-start(f32[26,264]{1,0:T(8,128)S(1)} %pad_maximum_fusion.8), channel_id=1, source_target_pairs={{64,0},{68,4},{72,8},{76,12},{80,16},{84,20},{88,24},{92,28},{96,3... | collective-permute-start | bytes 82376 | tf_op jit(solution)/shard_map/ppermute | solution.py:59
  44.0 1.9 %collective-permute-start.2 = (f32[26,264]{1,0:T(8,128)S(1)}, f32[26,264]{1,0:T(8,128)S(1)}, u32[]{:S(2)}, u32[]{:S(2)}) collective-permute-start(f32[26,264]{1,0:T(8,128)S(1)} %pad_maximum_fusion.8), channel_id=1, source_target_pairs={{448,0},{452,4},{456,8},{460,12},{464,16},{468,20},{472,24},{476,2... | collective-permute-start | bytes 82376 | tf_op jit(solution)/shard_map/ppermute | solution.py:58
  47.3 3.7 %collective-permute-done.2 = f32[26,264]{1,0:T(8,128)S(1)} collective-permute-done((f32[26,264]{1,0:T(8,128)S(1)}, f32[26,264]{1,0:T(8,128)S(1)}, u32[]{:S(2)}, u32[]{:S(2)}) %collective-permute-start.2) | collective-permute-done | bytes 27488 | tf_op jit(solution)/shard_map/ppermute | solution.py:58
  51.3 1.1 maximum_maximum_fusion
  52.4 1.3 fusion.9
  53.9 1.3 copy.209
  55.2 5.8 %all-to-all-start = ((f32[4,2,13,12,128]{4,1,3,2,0:T(2,128)}), f32[4,2,13,12,128]{4,1,3,2,0:T(2,128)S(1)}, u32[]{:S(2)}, u32[]{:S(2)}) async-start(f32[4,2,13,12,128]{4,1,3,2,0:T(2,128)} %copy.209), calls=%async_computation | async-start | bytes 1277952 | tf_op jit(solution)/shard_map/all_to_all | solution.py:99
  61.9 8.3 %all-to-all-done = f32[4,2,13,12,128]{4,1,3,2,0:T(2,128)S(1)} async-done(((f32[4,2,13,12,128]{4,1,3,2,0:T(2,128)}), f32[4,2,13,12,128]{4,1,3,2,0:T(2,128)S(1)}, u32[]{:S(2)}, u32[]{:S(2)}) %all-to-all-start) | async-done | bytes 639008 | tf_op jit(solution)/shard_map/all_to_all | solution.py:99
  70.2 1.7 %slice_reduce_fusion.3 = (f32[4,13,12,128]{3,2,1,0:T(8,128)S(1)}, f32[4,13,12,128]{3,2,1,0:T(8,128)S(1)}) fusion(f32[4,2,13,12,128]{4,1,3,2,0:T(2,128)S(1)} %all-to-all-done), kind=kLoop, calls=%fused_computation.39 | loop fusion | bytes 1277952 | tf_op jit(solution)/shard_map/slice | solution.py:102
  74.7 12.3 %all_to_all.20 = f32[4,2,13,12,128]{4,1,3,2,0:T(2,128)S(1)} all-to-all(f32[4,2,13,12,128]{4,1,3,2,0:T(2,128)S(1)} %copy.210), channel_id=1, replica_groups=mesh['tile'=128,'lev'=4] {'lev'}, dimensions={0} | all-to-all | bytes 1277952 | tf_op jit(solution)/shard_map/all_to_all | solution.py:107
  88.4 8.1 %collective-permute-start.5 = (f32[26,100]{1,0:T(8,128)S(1)}, f32[26,100]{1,0:T(8,128)S(1)}, u32[]{:S(2)}, u32[]{:S(2)}) collective-permute-start(f32[26,100]{1,0:T(8,128)S(1)} %concatenate.73), channel_id=1, source_target_pairs={{4,0},{8,4},{12,8},{16,12},{20,16},{24,20},{28,24},{32,28},{36,32}... | collective-permute-start | bytes 31208 | tf_op jit(solution)/shard_map/ppermute | solution.py:51
  96.5 1.9 %collective-permute-start.4 = (f32[26,100]{1,0:T(8,128)S(1)}, f32[26,100]{1,0:T(8,128)S(1)}, u32[]{:S(2)}, u32[]{:S(2)}) collective-permute-start(f32[26,100]{1,0:T(8,128)S(1)} %concatenate.73), channel_id=1, source_target_pairs={{60,0},{0,4},{4,8},{8,12},{12,16},{16,20},{20,24},{24,28},{28,32},... | collective-permute-start | bytes 31208 | tf_op jit(solution)/shard_map/ppermute | solution.py:50
  98.5 6.9 %collective-permute-done.4 = f32[26,100]{1,0:T(8,128)S(1)} collective-permute-done((f32[26,100]{1,0:T(8,128)S(1)}, f32[26,100]{1,0:T(8,128)S(1)}, u32[]{:S(2)}, u32[]{:S(2)}) %collective-permute-start.4) | collective-permute-done | bytes 10432 | tf_op jit(solution)/shard_map/ppermute | solution.py:50
  105.6 1.9 %collective-permute-start.7 = (f32[26,264]{1,0:T(8,128)S(1)}, f32[26,264]{1,0:T(8,128)S(1)}, u32[]{:S(2)}, u32[]{:S(2)}) collective-permute-start(f32[26,264]{1,0:T(8,128)S(1)} %pad_maximum_fusion.9), channel_id=1, source_target_pairs={{64,0},{68,4},{72,8},{76,12},{80,16},{84,20},{88,24},{92,28},{96,3... | collective-permute-start | bytes 82376 | tf_op jit(solution)/shard_map/ppermute | solution.py:59
  107.5 4.4 %collective-permute-start.6 = (f32[26,264]{1,0:T(8,128)S(1)}, f32[26,264]{1,0:T(8,128)S(1)}, u32[]{:S(2)}, u32[]{:S(2)}) collective-permute-start(f32[26,264]{1,0:T(8,128)S(1)} %pad_maximum_fusion.9), channel_id=1, source_target_pairs={{448,0},{452,4},{456,8},{460,12},{464,16},{468,20},{472,24},{476,2... | collective-permute-start | bytes 82376 | tf_op jit(solution)/shard_map/ppermute | solution.py:58
  113.4 1.2 collective-permute-done.6
  116.0 1.3 fusion.2
  118.0 15.3 %all_to_all.21 = f32[4,2,13,12,128]{4,1,3,2,0:T(2,128)S(1)} all-to-all(f32[4,2,13,12,128]{4,1,3,2,0:T(2,128)S(1)} %copy.225), channel_id=1, replica_groups=mesh['tile'=128,'lev'=4] {'lev'}, dimensions={0} | all-to-all | bytes 1277952 | tf_op jit(solution)/shard_map/all_to_all | solution.py:99
  133.2 1.7 %slice_reduce_fusion.1 = (f32[4,13,12,128]{3,2,1,0:T(8,128)S(1)}, f32[4,13,12,128]{3,2,1,0:T(8,128)S(1)}) fusion(f32[4,2,13,12,128]{4,1,3,2,0:T(2,128)S(1)} %all_to_all.21), kind=kLoop, calls=%fused_computation.37 | loop fusion | bytes 1277952 | tf_op jit(solution)/shard_map/slice | solution.py:102
  137.7 12.5 %all_to_all.22 = f32[4,2,13,12,128]{4,1,3,2,0:T(2,128)S(1)} all-to-all(f32[4,2,13,12,128]{4,1,3,2,0:T(2,128)S(1)} %copy.226), channel_id=1, replica_groups=mesh['tile'=128,'lev'=4] {'lev'}, dimensions={0} | all-to-all | bytes 1277952 | tf_op jit(solution)/shard_map/all_to_all | solution.py:107
  (128 shorter events, 15.5 us)
Async XLA Ops:
  1.2 13.5 %copy-start = (f32[2,13,48,128]{3,2,1,0:T(8,128)S(1)}, f32[2,13,48,128]{3,2,1,0:T(8,128)}, u32[]{:S(2)}) copy-start(f32[2,13,48,128]{3,2,1,0:T(8,128)} %param.6) | copy-start | bytes 1916932
  1.2 13.5 %copy-start.3 = (s32[1,8]{1,0:T(1,128)S(1)}, s32[1,8]{1,0:T(1,128)}, u32[]{:S(2)}) copy-start(s32[1,8]{1,0:T(1,128)} %param.11) | copy-start | bytes 100
  1.2 13.5 %copy-start.4 = (f32[13]{0:T(128)S(1)}, f32[13]{0:T(128)}, u32[]{:S(2)}) copy-start(f32[13]{0:T(128)} %param.7) | copy-start | bytes 160
  2.8 30.3 %copy-start.2 = (s32[48,128]{1,0:T(8,128)S(1)}, s32[48,128]{1,0:T(8,128)}, u32[]{:S(2)}) copy-start(s32[48,128]{1,0:T(8,128)} %param.8) | copy-start | bytes 73732
  3.5 29.6 %collective-permute-start.1 = (f32[26,100]{1,0:T(8,128)S(1)}, f32[26,100]{1,0:T(8,128)S(1)}, u32[]{:S(2)}, u32[]{:S(2)}) collective-permute-start(f32[26,100]{1,0:T(8,128)S(1)} %concatenate.64), channel_id=1, source_target_pairs={{4,0},{8,4},{12,8},{16,12},{20,16},{24,20},{28,24},{32,28},{36,32}... | collective-permute-start | bytes 31208 | tf_op jit(solution)/shard_map/ppermute | solution.py:51
  12.7 20.4 %collective-permute-start = (f32[26,100]{1,0:T(8,128)S(1)}, f32[26,100]{1,0:T(8,128)S(1)}, u32[]{:S(2)}, u32[]{:S(2)}) collective-permute-start(f32[26,100]{1,0:T(8,128)S(1)} %concatenate.64), channel_id=1, source_target_pairs={{60,0},{0,4},{4,8},{8,12},{12,16},{16,20},{20,24},{24,28},{28,32},... | collective-permute-start | bytes 31208 | tf_op jit(solution)/shard_map/ppermute | solution.py:50
  33.3 13.6 %collective-permute-start.3 = (f32[26,264]{1,0:T(8,128)S(1)}, f32[26,264]{1,0:T(8,128)S(1)}, u32[]{:S(2)}, u32[]{:S(2)}) collective-permute-start(f32[26,264]{1,0:T(8,128)S(1)} %pad_maximum_fusion.8), channel_id=1, source_target_pairs={{64,0},{68,4},{72,8},{76,12},{80,16},{84,20},{88,24},{92,28},{96,3... | collective-permute-start | bytes 82376 | tf_op jit(solution)/shard_map/ppermute | solution.py:59
  44.0 7.0 %collective-permute-start.2 = (f32[26,264]{1,0:T(8,128)S(1)}, f32[26,264]{1,0:T(8,128)S(1)}, u32[]{:S(2)}, u32[]{:S(2)}) collective-permute-start(f32[26,264]{1,0:T(8,128)S(1)} %pad_maximum_fusion.8), channel_id=1, source_target_pairs={{448,0},{452,4},{456,8},{460,12},{464,16},{468,20},{472,24},{476,2... | collective-permute-start | bytes 82376 | tf_op jit(solution)/shard_map/ppermute | solution.py:58
  53.9 7.2 %copy-start.1 = (f32[2,2,52,52]{3,1,2,0:T(2,128)S(1)}, f32[2,2,52,52]{3,1,2,0:T(2,128)}, u32[]{:S(2)}) copy-start(f32[2,2,52,52]{3,1,2,0:T(2,128)} %param.10) | copy-start | bytes 129796
  55.2 15.0 %all-to-all-start = ((f32[4,2,13,12,128]{4,1,3,2,0:T(2,128)}), f32[4,2,13,12,128]{4,1,3,2,0:T(2,128)S(1)}, u32[]{:S(2)}, u32[]{:S(2)}) async-start(f32[4,2,13,12,128]{4,1,3,2,0:T(2,128)} %copy.209), calls=%async_computation | async-start | bytes 1277952 | tf_op jit(solution)/shard_map/all_to_all | solution.py:99
  88.4 10.1 %collective-permute-start.5 = (f32[26,100]{1,0:T(8,128)S(1)}, f32[26,100]{1,0:T(8,128)S(1)}, u32[]{:S(2)}, u32[]{:S(2)}) collective-permute-start(f32[26,100]{1,0:T(8,128)S(1)} %concatenate.73), channel_id=1, source_target_pairs={{4,0},{8,4},{12,8},{16,12},{20,16},{24,20},{28,24},{32,28},{36,32}... | collective-permute-start | bytes 31208 | tf_op jit(solution)/shard_map/ppermute | solution.py:51
  96.5 9.0 %collective-permute-start.4 = (f32[26,100]{1,0:T(8,128)S(1)}, f32[26,100]{1,0:T(8,128)S(1)}, u32[]{:S(2)}, u32[]{:S(2)}) collective-permute-start(f32[26,100]{1,0:T(8,128)S(1)} %concatenate.73), channel_id=1, source_target_pairs={{60,0},{0,4},{4,8},{8,12},{12,16},{16,20},{20,24},{24,28},{28,32},... | collective-permute-start | bytes 31208 | tf_op jit(solution)/shard_map/ppermute | solution.py:50
  105.6 7.4 %collective-permute-start.7 = (f32[26,264]{1,0:T(8,128)S(1)}, f32[26,264]{1,0:T(8,128)S(1)}, u32[]{:S(2)}, u32[]{:S(2)}) collective-permute-start(f32[26,264]{1,0:T(8,128)S(1)} %pad_maximum_fusion.9), channel_id=1, source_target_pairs={{64,0},{68,4},{72,8},{76,12},{80,16},{84,20},{88,24},{92,28},{96,3... | collective-permute-start | bytes 82376 | tf_op jit(solution)/shard_map/ppermute | solution.py:59
  107.5 7.0 %collective-permute-start.6 = (f32[26,264]{1,0:T(8,128)S(1)}, f32[26,264]{1,0:T(8,128)S(1)}, u32[]{:S(2)}, u32[]{:S(2)}) collective-permute-start(f32[26,264]{1,0:T(8,128)S(1)} %pad_maximum_fusion.9), channel_id=1, source_target_pairs={{448,0},{452,4},{456,8},{460,12},{464,16},{468,20},{472,24},{476,2... | collective-permute-start | bytes 82376 | tf_op jit(solution)/shard_map/ppermute | solution.py:58

commit v4 on v3

--- a/solution.py
+++ b/solution.py
@@ -89,6 +89,18 @@
     return stencil(extended, field, rate, wet)
 
 
+def lev_exchange(outgoing):
+    parts = outgoing.shape[0]
+    here = lax.axis_index("lev")
+    by_shift = [lax.dynamic_index_in_dim(outgoing, here, axis=0, keepdims=False)]
+    for shift in range(1, parts):
+        sent = lax.dynamic_index_in_dim(outgoing, (here + shift) % parts, axis=0, keepdims=False)
+        pairs = [(source, (source + shift) % parts) for source in range(parts)]
+        by_shift.append(lax.ppermute(sent, "lev", pairs))
+    order = (here - jnp.arange(parts)) % parts
+    return jnp.take(jnp.stack(by_shift), order, axis=0)
+
+
 def column_mix(lateral, stacked_inverse, convective_rows):
     parts = lax.axis_size("lev")
     tracers, depth, rows, cols = lateral.shape
@@ -96,7 +108,7 @@
     outgoing = jnp.transpose(
         lateral.reshape(tracers, depth, parts, part_rows, cols), (2, 0, 1, 3, 4)
     )
-    columns = lax.all_to_all(outgoing, "lev", 0, 0, tiled=True)
+    columns = lev_exchange(outgoing)
     mixed = []
     for tracer in range(tracers):
         flat = columns[:, tracer].reshape(parts * depth, part_rows * cols)
@@ -104,7 +116,7 @@
             stacked_inverse[tracer], flat, precision=lax.Precision.HIGHEST
         ).reshape(2, parts, depth, part_rows, cols)
         mixed.append(jnp.where(convective_rows[None, None], both_states[1], both_states[0]))
-    returning = lax.all_to_all(jnp.stack(mixed, axis=1), "lev", 0, 0, tiled=True)
+    returning = lev_exchange(jnp.stack(mixed, axis=1))
     return jnp.transpose(returning, (1, 2, 0, 3, 4)).reshape(tracers, depth, rows, cols)
 
 

time: 152 us -> 156 us (1.026)
  blocking collectives: 40.1 us -> 0 us
  starting transfers between devices: 45.9 us -> 72.8 us
  waiting for transfers between devices: 20.2 us -> 33.4 us
  local copies, waits for them, and re-layouts: 16.3 us -> 18.4 us
  other arithmetic: 7.51 us -> 9.39 us
    all_to_all x3 -> x0, blocking collectives: 40.1 us -> none  [the longest x2 24.8 us: column_mix(): lax.all_to_all(jnp.stack(mixed, axis=1), 'lev', 0, 0, tiled=True)]
    ppermute x0 -> x12, starting transfers between devices: none -> 32.7 us  [lev_exchange(): by_shift.append(lax.ppermute(sent, 'lev', pairs))]
    ppermute x0 -> x12, waiting for transfers between devices: none -> 21.5 us  [lev_exchange(): by_shift.append(lax.ppermute(sent, 'lev', pairs))]
    all_to_all x1 -> x0, waiting for transfers between devices: 8.28 us -> none  [column_mix(): columns = lax.all_to_all(outgoing, 'lev', 0, 0, tiled=True)]
    all_to_all x1 -> x0, starting transfers between devices: 5.83 us -> none  [column_mix(): columns = lax.all_to_all(outgoing, 'lev', 0, 0, tiled=True)]
    gather x0 -> x4, local copies, waits for them, and re-layouts: none -> 3.67 us  [lev_exchange(): return jnp.take(jnp.stack(by_shift), order, axis=0)]
    transpose x2 -> x0, local copies, waits for them, and re-layouts: 1.82 us -> none  [column_mix(): jnp.transpose(lateral.reshape(tracers, depth, parts, part_rows, cols), (2...]
  transfers between devices with their start and end apart: 9 -> 20, of which waited for: 4 -> 11; matrix products, arithmetic and copies ran while one was open for 3% -> 3% of each run, Pallas kernels for 0% -> 0%
where the time goes in v4:
time: 156 us; the launch traced here: 155 us
  starting transfers between devices  72.8 us (47%)
  waiting for transfers between devices  33.4 us (21%)
  local copies, waits for them, and re-layouts  18.4 us (12%)
  between operations  18.3 us (12%)
  other arithmetic  9.39 us (6%)
  matrix products  2.85 us (2%)
    ppermute x12, starting transfers between devices, lev_exchange(): by_shift.append(lax.ppermute(sent, 'lev', pairs))  32.7 us
    ppermute x12, waiting for transfers between devices, lev_exchange(): by_shift.append(lax.ppermute(sent, 'lev', pairs))  21.5 us
    ppermute x2, starting transfers between devices, horizontal(): from_east = lax.ppermute(side, 'tile', slot_pairs(count, 3))  17.4 us
    ppermute x2, starting transfers between devices, horizontal(): from_north = lax.ppermute(upright, 'tile', slot_pairs(count, 1))  12.6 us
    ppermute x2, waiting for transfers between devices, horizontal(): from_west = lax.ppermute(side, 'tile', slot_pairs(count, 2))  6.94 us
    ppermute x2, starting transfers between devices, horizontal(): from_south = lax.ppermute(upright, 'tile', slot_pairs(count, 0))  6.36 us
    ppermute x2, waiting for transfers between devices, horizontal(): from_south = lax.ppermute(upright, 'tile', slot_pairs(count, 0))  4.94 us
    ppermute x2, starting transfers between devices, horizontal(): from_west = lax.ppermute(side, 'tile', slot_pairs(count, 2))  3.84 us
  transfers between devices with their start and end apart: 20, of which 11 were waited for; matrix products, arithmetic and copies ran while one was open for 3% of the time, Pallas kernels for 0%

profile of v4, /device:TPU:1, one launch (start us, length us, event | category | flops | bytes accessed | tf_op | source)
XLA Modules:
  0.0 155.2 jit_solution(6475641694231691060)
XLA Ops:
  3.5 9.2 %collective-permute-start.1 = (f32[26,100]{1,0:T(8,128)S(1)}, f32[26,100]{1,0:T(8,128)S(1)}, u32[]{:S(2)}, u32[]{:S(2)}) collective-permute-start(f32[26,100]{1,0:T(8,128)S(1)} %concatenate.64), channel_id=1, source_target_pairs={{4,0},{8,4},{12,8},{16,12},{20,16},{24,20},{28,24},{32,28},{36,32}... | collective-permute-start | bytes 31208 | tf_op jit(solution)/shard_map/ppermute | solution.py:51
  12.7 1.9 %collective-permute-start = (f32[26,100]{1,0:T(8,128)S(1)}, f32[26,100]{1,0:T(8,128)S(1)}, u32[]{:S(2)}, u32[]{:S(2)}) collective-permute-start(f32[26,100]{1,0:T(8,128)S(1)} %concatenate.64), channel_id=1, source_target_pairs={{60,0},{0,4},{4,8},{8,12},{12,16},{16,20},{20,24},{24,28},{28,32},... | collective-permute-start | bytes 31208 | tf_op jit(solution)/shard_map/ppermute | solution.py:50
  33.9 10.7 %collective-permute-start.3 = (f32[26,264]{1,0:T(8,128)S(1)}, f32[26,264]{1,0:T(8,128)S(1)}, u32[]{:S(2)}, u32[]{:S(2)}) collective-permute-start(f32[26,264]{1,0:T(8,128)S(1)} %pad_maximum_fusion.10), channel_id=1, source_target_pairs={{64,0},{68,4},{72,8},{76,12},{80,16},{84,20},{88,24},{92,28},{96,3... | collective-permute-start | bytes 82376 | tf_op jit(solution)/shard_map/ppermute | solution.py:59
  47.8 3.7 %collective-permute-done.2 = f32[26,264]{1,0:T(8,128)S(1)} collective-permute-done((f32[26,264]{1,0:T(8,128)S(1)}, f32[26,264]{1,0:T(8,128)S(1)}, u32[]{:S(2)}, u32[]{:S(2)}) %collective-permute-start.2) | collective-permute-done | bytes 27488 | tf_op jit(solution)/shard_map/ppermute | solution.py:58
  54.8 4.6 %collective-permute-start.4 = (f32[2,13,12,128]{3,0,2,1:T(2,128)S(1)}, f32[2,13,12,128]{3,0,2,1:T(2,128)S(1)}, u32[]{:S(2)}, u32[]{:S(2)}) collective-permute-start(f32[2,13,12,128]{3,0,2,1:T(2,128)S(1)} %bitcast.189), channel_id=1, source_target_pairs={{0,1},{1,2},{2,3},{3,0},{4,5},{5,6},{6,7},{7,4},{8,9},{9,10},{10,1... | collective-permute-start | bytes 479240 | tf_op jit(solution)/shard_map/ppermute | solution.py:99
  59.3 3.0 %collective-permute-start.5 = (f32[2,13,12,128]{3,0,2,1:T(2,128)S(1)}, f32[2,13,12,128]{3,0,2,1:T(2,128)S(1)}, u32[]{:S(2)}, u32[]{:S(2)}) collective-permute-start(f32[2,13,12,128]{3,0,2,1:T(2,128)S(1)} %bitcast.185), channel_id=1, source_target_pairs={{0,2},{1,3},{2,0},{3,1},{4,6},{5,7},{6,4},{7,5},{8,10},{9,11},{10,... | collective-permute-start | bytes 479240 | tf_op jit(solution)/shard_map/ppermute | solution.py:99
  62.3 1.9 %collective-permute-start.6 = (f32[2,13,12,128]{3,0,2,1:T(2,128)S(1)}, f32[2,13,12,128]{3,0,2,1:T(2,128)S(1)}, u32[]{:S(2)}, u32[]{:S(2)}) collective-permute-start(f32[2,13,12,128]{3,0,2,1:T(2,128)S(1)} %bitcast.183), channel_id=1, source_target_pairs={{0,3},{1,0},{2,1},{3,2},{4,7},{5,4},{6,5},{7,6},{8,11},{9,8},{10,9... | collective-permute-start | bytes 479240 | tf_op jit(solution)/shard_map/ppermute | solution.py:99
  64.6 2.6 %collective-permute-done.5 = f32[2,13,12,128]{3,0,2,1:T(2,128)S(1)} collective-permute-done((f32[2,13,12,128]{3,0,2,1:T(2,128)S(1)}, f32[2,13,12,128]{3,0,2,1:T(2,128)S(1)}, u32[]{:S(2)}, u32[]{:S(2)}) %collective-permute-start.5) | collective-permute-done | bytes 159776 | tf_op jit(solution)/shard_map/ppermute | solution.py:99
  76.8 2.4 %collective-permute-start.8 = (f32[2,13,12,128]{3,2,1,0:T(8,128)S(1)}, f32[2,13,12,128]{3,2,1,0:T(8,128)S(1)}, u32[]{:S(2)}, u32[]{:S(2)}) collective-permute-start(f32[2,13,12,128]{3,2,1,0:T(8,128)S(1)} %get-tuple-element.24), channel_id=1, source_target_pairs={{0,2},{1,3},{2,0},{3,1},{4,6},{5,7},{6,4},{7,5},{8,10},{9,11},{10,... | collective-permute-start | bytes 479240 | tf_op jit(solution)/shard_map/ppermute | solution.py:99
  79.2 2.7 %collective-permute-start.9 = (f32[2,13,12,128]{3,2,1,0:T(8,128)S(1)}, f32[2,13,12,128]{3,2,1,0:T(8,128)S(1)}, u32[]{:S(2)}, u32[]{:S(2)}) collective-permute-start(f32[2,13,12,128]{3,2,1,0:T(8,128)S(1)} %get-tuple-element.25), channel_id=1, source_target_pairs={{0,3},{1,0},{2,1},{3,2},{4,7},{5,4},{6,5},{7,6},{8,11},{9,8},{10,9... | collective-permute-start | bytes 479240 | tf_op jit(solution)/shard_map/ppermute | solution.py:99
  81.9 3.1 %collective-permute-done.8 = f32[2,13,12,128]{3,2,1,0:T(8,128)S(1)} collective-permute-done((f32[2,13,12,128]{3,2,1,0:T(8,128)S(1)}, f32[2,13,12,128]{3,2,1,0:T(8,128)S(1)}, u32[]{:S(2)}, u32[]{:S(2)}) %collective-permute-start.8) | collective-permute-done | bytes 159776 | tf_op jit(solution)/shard_map/ppermute | solution.py:99
  85.0 2.9 %collective-permute-done.9 = f32[2,13,12,128]{3,2,1,0:T(8,128)S(1)} collective-permute-done((f32[2,13,12,128]{3,2,1,0:T(8,128)S(1)}, f32[2,13,12,128]{3,2,1,0:T(8,128)S(1)}, u32[]{:S(2)}, u32[]{:S(2)}) %collective-permute-start.9) | collective-permute-done | bytes 159776 | tf_op jit(solution)/shard_map/ppermute | solution.py:99
  90.1 8.2 %collective-permute-start.11 = (f32[26,100]{1,0:T(8,128)S(1)}, f32[26,100]{1,0:T(8,128)S(1)}, u32[]{:S(2)}, u32[]{:S(2)}) collective-permute-start(f32[26,100]{1,0:T(8,128)S(1)} %concatenate.73), channel_id=1, source_target_pairs={{4,0},{8,4},{12,8},{16,12},{20,16},{24,20},{28,24},{32,28},{36,32}... | collective-permute-start | bytes 31208 | tf_op jit(solution)/shard_map/ppermute | solution.py:51
  98.3 1.9 %collective-permute-start.10 = (f32[26,100]{1,0:T(8,128)S(1)}, f32[26,100]{1,0:T(8,128)S(1)}, u32[]{:S(2)}, u32[]{:S(2)}) collective-permute-start(f32[26,100]{1,0:T(8,128)S(1)} %concatenate.73), channel_id=1, source_target_pairs={{60,0},{0,4},{4,8},{8,12},{12,16},{16,20},{20,24},{24,28},{28,32},... | collective-permute-start | bytes 31208 | tf_op jit(solution)/shard_map/ppermute | solution.py:50
  100.3 6.9 %collective-permute-done.10 = f32[26,100]{1,0:T(8,128)S(1)} collective-permute-done((f32[26,100]{1,0:T(8,128)S(1)}, f32[26,100]{1,0:T(8,128)S(1)}, u32[]{:S(2)}, u32[]{:S(2)}) %collective-permute-start.10) | collective-permute-done | bytes 10432 | tf_op jit(solution)/shard_map/ppermute | solution.py:50
  109.3 4.4 %collective-permute-start.12 = (f32[26,264]{1,0:T(8,128)S(1)}, f32[26,264]{1,0:T(8,128)S(1)}, u32[]{:S(2)}, u32[]{:S(2)}) collective-permute-start(f32[26,264]{1,0:T(8,128)S(1)} %pad_maximum_fusion.11), channel_id=1, source_target_pairs={{448,0},{452,4},{456,8},{460,12},{464,16},{468,20},{472,24},{476,2... | collective-permute-start | bytes 82376 | tf_op jit(solution)/shard_map/ppermute | solution.py:58
  119.6 3.9 %collective-permute-start.14 = (f32[2,13,12,128]{3,0,2,1:T(2,128)S(1)}, f32[2,13,12,128]{3,0,2,1:T(2,128)S(1)}, u32[]{:S(2)}, u32[]{:S(2)}) collective-permute-start(f32[2,13,12,128]{3,0,2,1:T(2,128)S(1)} %bitcast.194), channel_id=1, source_target_pairs={{0,1},{1,2},{2,3},{3,0},{4,5},{5,6},{6,7},{7,4},{8,9},{9,10},{10,1... | collective-permute-start | bytes 479240 | tf_op jit(solution)/shard_map/ppermute | solution.py:99
  123.5 3.9 %collective-permute-start.15 = (f32[2,13,12,128]{3,0,2,1:T(2,128)S(1)}, f32[2,13,12,128]{3,0,2,1:T(2,128)S(1)}, u32[]{:S(2)}, u32[]{:S(2)}) collective-permute-start(f32[2,13,12,128]{3,0,2,1:T(2,128)S(1)} %bitcast.191), channel_id=1, source_target_pairs={{0,2},{1,3},{2,0},{3,1},{4,6},{5,7},{6,4},{7,5},{8,10},{9,11},{10,... | collective-permute-start | bytes 479240 | tf_op jit(solution)/shard_map/ppermute | solution.py:99
  129.5 2.1 %collective-permute-done.15 = f32[2,13,12,128]{3,0,2,1:T(2,128)S(1)} collective-permute-done((f32[2,13,12,128]{3,0,2,1:T(2,128)S(1)}, f32[2,13,12,128]{3,0,2,1:T(2,128)S(1)}, u32[]{:S(2)}, u32[]{:S(2)}) %collective-permute-start.15) | collective-permute-done | bytes 159776 | tf_op jit(solution)/shard_map/ppermute | solution.py:99
  131.6 2.5 %collective-permute-done.16 = f32[2,13,12,128]{3,0,2,1:T(2,128)S(1)} collective-permute-done((f32[2,13,12,128]{3,0,2,1:T(2,128)S(1)}, f32[2,13,12,128]{3,0,2,1:T(2,128)S(1)}, u32[]{:S(2)}, u32[]{:S(2)}) %collective-permute-start.16) | collective-permute-done | bytes 159776 | tf_op jit(solution)/shard_map/ppermute | solution.py:99
  142.0 1.9 %collective-permute-start.18 = (f32[2,13,12,128]{3,2,1,0:T(8,128)S(1)}, f32[2,13,12,128]{3,2,1,0:T(8,128)S(1)}, u32[]{:S(2)}, u32[]{:S(2)}) collective-permute-start(f32[2,13,12,128]{3,2,1,0:T(8,128)S(1)} %get-tuple-element.16), channel_id=1, source_target_pairs={{0,2},{1,3},{2,0},{3,1},{4,6},{5,7},{6,4},{7,5},{8,10},{9,11},{10,... | collective-permute-start | bytes 479240 | tf_op jit(solution)/shard_map/ppermute | solution.py:99
  143.9 2.7 %collective-permute-start.19 = (f32[2,13,12,128]{3,2,1,0:T(8,128)S(1)}, f32[2,13,12,128]{3,2,1,0:T(8,128)S(1)}, u32[]{:S(2)}, u32[]{:S(2)}) collective-permute-start(f32[2,13,12,128]{3,2,1,0:T(8,128)S(1)} %get-tuple-element.17), channel_id=1, source_target_pairs={{0,3},{1,0},{2,1},{3,2},{4,7},{5,4},{6,5},{7,6},{8,11},{9,8},{10,9... | collective-permute-start | bytes 479240 | tf_op jit(solution)/shard_map/ppermute | solution.py:99
  146.6 3.6 %collective-permute-done.18 = f32[2,13,12,128]{3,2,1,0:T(8,128)S(1)} collective-permute-done((f32[2,13,12,128]{3,2,1,0:T(8,128)S(1)}, f32[2,13,12,128]{3,2,1,0:T(8,128)S(1)}, u32[]{:S(2)}, u32[]{:S(2)}) %collective-permute-start.18) | collective-permute-done | bytes 159776 | tf_op jit(solution)/shard_map/ppermute | solution.py:99
  150.2 2.9 %collective-permute-done.19 = f32[2,13,12,128]{3,2,1,0:T(8,128)S(1)} collective-permute-done((f32[2,13,12,128]{3,2,1,0:T(8,128)S(1)}, f32[2,13,12,128]{3,2,1,0:T(8,128)S(1)}, u32[]{:S(2)}, u32[]{:S(2)}) %collective-permute-start.19) | collective-permute-done | bytes 159776 | tf_op jit(solution)/shard_map/ppermute | solution.py:99
  (168 shorter events, 43.2 us)
Async XLA Ops:
  1.2 13.5 %copy-start.3 = (s32[1,8]{1,0:T(1,128)S(1)}, s32[1,8]{1,0:T(1,128)}, u32[]{:S(2)}) copy-start(s32[1,8]{1,0:T(1,128)} %param.13) | copy-start | bytes 100
  1.2 13.5 %copy-start.4 = (f32[13]{0:T(128)S(1)}, f32[13]{0:T(128)}, u32[]{:S(2)}) copy-start(f32[13]{0:T(128)} %param.9) | copy-start | bytes 160
  1.2 14.3 %copy-start.1 = (f32[2,2,52,52]{3,1,2,0:T(2,128)S(1)}, f32[2,2,52,52]{3,1,2,0:T(2,128)}, u32[]{:S(2)}) copy-start(f32[2,2,52,52]{3,1,2,0:T(2,128)} %param.12) | copy-start | bytes 129796
  2.8 30.8 %copy-start.2 = (s32[48,128]{1,0:T(8,128)S(1)}, s32[48,128]{1,0:T(8,128)}, u32[]{:S(2)}) copy-start(s32[48,128]{1,0:T(8,128)} %param.10) | copy-start | bytes 73732
  3.5 30.1 %collective-permute-start.1 = (f32[26,100]{1,0:T(8,128)S(1)}, f32[26,100]{1,0:T(8,128)S(1)}, u32[]{:S(2)}, u32[]{:S(2)}) collective-permute-start(f32[26,100]{1,0:T(8,128)S(1)} %concatenate.64), channel_id=1, source_target_pairs={{4,0},{8,4},{12,8},{16,12},{20,16},{24,20},{28,24},{32,28},{36,32}... | collective-permute-start | bytes 31208 | tf_op jit(solution)/shard_map/ppermute | solution.py:51
  12.7 21.0 %collective-permute-start = (f32[26,100]{1,0:T(8,128)S(1)}, f32[26,100]{1,0:T(8,128)S(1)}, u32[]{:S(2)}, u32[]{:S(2)}) collective-permute-start(f32[26,100]{1,0:T(8,128)S(1)} %concatenate.64), channel_id=1, source_target_pairs={{60,0},{0,4},{4,8},{8,12},{12,16},{16,20},{20,24},{24,28},{28,32},... | collective-permute-start | bytes 31208 | tf_op jit(solution)/shard_map/ppermute | solution.py:50
  33.9 13.6 %collective-permute-start.3 = (f32[26,264]{1,0:T(8,128)S(1)}, f32[26,264]{1,0:T(8,128)S(1)}, u32[]{:S(2)}, u32[]{:S(2)}) collective-permute-start(f32[26,264]{1,0:T(8,128)S(1)} %pad_maximum_fusion.10), channel_id=1, source_target_pairs={{64,0},{68,4},{72,8},{76,12},{80,16},{84,20},{88,24},{92,28},{96,3... | collective-permute-start | bytes 82376 | tf_op jit(solution)/shard_map/ppermute | solution.py:59
  44.5 7.0 %collective-permute-start.2 = (f32[26,264]{1,0:T(8,128)S(1)}, f32[26,264]{1,0:T(8,128)S(1)}, u32[]{:S(2)}, u32[]{:S(2)}) collective-permute-start(f32[26,264]{1,0:T(8,128)S(1)} %pad_maximum_fusion.10), channel_id=1, source_target_pairs={{448,0},{452,4},{456,8},{460,12},{464,16},{468,20},{472,24},{476,2... | collective-permute-start | bytes 82376 | tf_op jit(solution)/shard_map/ppermute | solution.py:58
  54.8 9.8 %collective-permute-start.4 = (f32[2,13,12,128]{3,0,2,1:T(2,128)S(1)}, f32[2,13,12,128]{3,0,2,1:T(2,128)S(1)}, u32[]{:S(2)}, u32[]{:S(2)}) collective-permute-start(f32[2,13,12,128]{3,0,2,1:T(2,128)S(1)} %bitcast.189), channel_id=1, source_target_pairs={{0,1},{1,2},{2,3},{3,0},{4,5},{5,6},{6,7},{7,4},{8,9},{9,10},{10,1... | collective-permute-start | bytes 479240 | tf_op jit(solution)/shard_map/ppermute | solution.py:99
  59.3 7.8 %collective-permute-start.5 = (f32[2,13,12,128]{3,0,2,1:T(2,128)S(1)}, f32[2,13,12,128]{3,0,2,1:T(2,128)S(1)}, u32[]{:S(2)}, u32[]{:S(2)}) collective-permute-start(f32[2,13,12,128]{3,0,2,1:T(2,128)S(1)} %bitcast.185), channel_id=1, source_target_pairs={{0,2},{1,3},{2,0},{3,1},{4,6},{5,7},{6,4},{7,5},{8,10},{9,11},{10,... | collective-permute-start | bytes 479240 | tf_op jit(solution)/shard_map/ppermute | solution.py:99
  62.3 6.6 %collective-permute-start.6 = (f32[2,13,12,128]{3,0,2,1:T(2,128)S(1)}, f32[2,13,12,128]{3,0,2,1:T(2,128)S(1)}, u32[]{:S(2)}, u32[]{:S(2)}) collective-permute-start(f32[2,13,12,128]{3,0,2,1:T(2,128)S(1)} %bitcast.183), channel_id=1, source_target_pairs={{0,3},{1,0},{2,1},{3,2},{4,7},{5,4},{6,5},{7,6},{8,11},{9,8},{10,9... | collective-permute-start | bytes 479240 | tf_op jit(solution)/shard_map/ppermute | solution.py:99
  74.9 7.0 %collective-permute-start.7 = (f32[2,13,12,128]{3,2,1,0:T(8,128)S(1)}, f32[2,13,12,128]{3,2,1,0:T(8,128)S(1)}, u32[]{:S(2)}, u32[]{:S(2)}) collective-permute-start(f32[2,13,12,128]{3,2,1,0:T(8,128)S(1)} %get-tuple-element.23), channel_id=1, source_target_pairs={{0,1},{1,2},{2,3},{3,0},{4,5},{5,6},{6,7},{7,4},{8,9},{9,10},{10,1... | collective-permute-start | bytes 479240 | tf_op jit(solution)/shard_map/ppermute | solution.py:99
  76.8 8.2 %collective-permute-start.8 = (f32[2,13,12,128]{3,2,1,0:T(8,128)S(1)}, f32[2,13,12,128]{3,2,1,0:T(8,128)S(1)}, u32[]{:S(2)}, u32[]{:S(2)}) collective-permute-start(f32[2,13,12,128]{3,2,1,0:T(8,128)S(1)} %get-tuple-element.24), channel_id=1, source_target_pairs={{0,2},{1,3},{2,0},{3,1},{4,6},{5,7},{6,4},{7,5},{8,10},{9,11},{10,... | collective-permute-start | bytes 479240 | tf_op jit(solution)/shard_map/ppermute | solution.py:99
  79.2 8.8 %collective-permute-start.9 = (f32[2,13,12,128]{3,2,1,0:T(8,128)S(1)}, f32[2,13,12,128]{3,2,1,0:T(8,128)S(1)}, u32[]{:S(2)}, u32[]{:S(2)}) collective-permute-start(f32[2,13,12,128]{3,2,1,0:T(8,128)S(1)} %get-tuple-element.25), channel_id=1, source_target_pairs={{0,3},{1,0},{2,1},{3,2},{4,7},{5,4},{6,5},{7,6},{8,11},{9,8},{10,9... | collective-permute-start | bytes 479240 | tf_op jit(solution)/shard_map/ppermute | solution.py:99
  90.1 10.1 %collective-permute-start.11 = (f32[26,100]{1,0:T(8,128)S(1)}, f32[26,100]{1,0:T(8,128)S(1)}, u32[]{:S(2)}, u32[]{:S(2)}) collective-permute-start(f32[26,100]{1,0:T(8,128)S(1)} %concatenate.73), channel_id=1, source_target_pairs={{4,0},{8,4},{12,8},{16,12},{20,16},{24,20},{28,24},{32,28},{36,32}... | collective-permute-start | bytes 31208 | tf_op jit(solution)/shard_map/ppermute | solution.py:51
  98.3 9.0 %collective-permute-start.10 = (f32[26,100]{1,0:T(8,128)S(1)}, f32[26,100]{1,0:T(8,128)S(1)}, u32[]{:S(2)}, u32[]{:S(2)}) collective-permute-start(f32[26,100]{1,0:T(8,128)S(1)} %concatenate.73), channel_id=1, source_target_pairs={{60,0},{0,4},{4,8},{8,12},{12,16},{16,20},{20,24},{24,28},{28,32},... | collective-permute-start | bytes 31208 | tf_op jit(solution)/shard_map/ppermute | solution.py:50
  107.4 7.4 %collective-permute-start.13 = (f32[26,264]{1,0:T(8,128)S(1)}, f32[26,264]{1,0:T(8,128)S(1)}, u32[]{:S(2)}, u32[]{:S(2)}) collective-permute-start(f32[26,264]{1,0:T(8,128)S(1)} %pad_maximum_fusion.11), channel_id=1, source_target_pairs={{64,0},{68,4},{72,8},{76,12},{80,16},{84,20},{88,24},{92,28},{96,3... | collective-permute-start | bytes 82376 | tf_op jit(solution)/shard_map/ppermute | solution.py:59
  109.3 7.0 %collective-permute-start.12 = (f32[26,264]{1,0:T(8,128)S(1)}, f32[26,264]{1,0:T(8,128)S(1)}, u32[]{:S(2)}, u32[]{:S(2)}) collective-permute-start(f32[26,264]{1,0:T(8,128)S(1)} %pad_maximum_fusion.11), channel_id=1, source_target_pairs={{448,0},{452,4},{456,8},{460,12},{464,16},{468,20},{472,24},{476,2... | collective-permute-start | bytes 82376 | tf_op jit(solution)/shard_map/ppermute | solution.py:58
  119.6 9.8 %collective-permute-start.14 = (f32[2,13,12,128]{3,0,2,1:T(2,128)S(1)}, f32[2,13,12,128]{3,0,2,1:T(2,128)S(1)}, u32[]{:S(2)}, u32[]{:S(2)}) collective-permute-start(f32[2,13,12,128]{3,0,2,1:T(2,128)S(1)} %bitcast.194), channel_id=1, source_target_pairs={{0,1},{1,2},{2,3},{3,0},{4,5},{5,6},{6,7},{7,4},{8,9},{9,10},{10,1... | collective-permute-start | bytes 479240 | tf_op jit(solution)/shard_map/ppermute | solution.py:99
  123.5 8.1 %collective-permute-start.15 = (f32[2,13,12,128]{3,0,2,1:T(2,128)S(1)}, f32[2,13,12,128]{3,0,2,1:T(2,128)S(1)}, u32[]{:S(2)}, u32[]{:S(2)}) collective-permute-start(f32[2,13,12,128]{3,0,2,1:T(2,128)S(1)} %bitcast.191), channel_id=1, source_target_pairs={{0,2},{1,3},{2,0},{3,1},{4,6},{5,7},{6,4},{7,5},{8,10},{9,11},{10,... | collective-permute-start | bytes 479240 | tf_op jit(solution)/shard_map/ppermute | solution.py:99
  127.4 6.6 %collective-permute-start.16 = (f32[2,13,12,128]{3,0,2,1:T(2,128)S(1)}, f32[2,13,12,128]{3,0,2,1:T(2,128)S(1)}, u32[]{:S(2)}, u32[]{:S(2)}) collective-permute-start(f32[2,13,12,128]{3,0,2,1:T(2,128)S(1)} %bitcast.187), channel_id=1, source_target_pairs={{0,3},{1,0},{2,1},{3,2},{4,7},{5,4},{6,5},{7,6},{8,11},{9,8},{10,9... | collective-permute-start | bytes 479240 | tf_op jit(solution)/shard_map/ppermute | solution.py:99
  140.0 6.6 %collective-permute-start.17 = (f32[2,13,12,128]{3,2,1,0:T(8,128)S(1)}, f32[2,13,12,128]{3,2,1,0:T(8,128)S(1)}, u32[]{:S(2)}, u32[]{:S(2)}) collective-permute-start(f32[2,13,12,128]{3,2,1,0:T(8,128)S(1)} %get-tuple-element.15), channel_id=1, source_target_pairs={{0,1},{1,2},{2,3},{3,0},{4,5},{5,6},{6,7},{7,4},{8,9},{9,10},{10,1... | collective-permute-start | bytes 479240 | tf_op jit(solution)/shard_map/ppermute | solution.py:99
  142.0 8.2 %collective-permute-start.18 = (f32[2,13,12,128]{3,2,1,0:T(8,128)S(1)}, f32[2,13,12,128]{3,2,1,0:T(8,128)S(1)}, u32[]{:S(2)}, u32[]{:S(2)}) collective-permute-start(f32[2,13,12,128]{3,2,1,0:T(8,128)S(1)} %get-tuple-element.16), channel_id=1, source_target_pairs={{0,2},{1,3},{2,0},{3,1},{4,6},{5,7},{6,4},{7,5},{8,10},{9,11},{10,... | collective-permute-start | bytes 479240 | tf_op jit(solution)/shard_map/ppermute | solution.py:99
  143.9 9.2 %collective-permute-start.19 = (f32[2,13,12,128]{3,2,1,0:T(8,128)S(1)}, f32[2,13,12,128]{3,2,1,0:T(8,128)S(1)}, u32[]{:S(2)}, u32[]{:S(2)}) collective-permute-start(f32[2,13,12,128]{3,2,1,0:T(8,128)S(1)} %get-tuple-element.17), channel_id=1, source_target_pairs={{0,3},{1,0},{2,1},{3,2},{4,7},{5,4},{6,5},{7,6},{8,11},{9,8},{10,9... | collective-permute-start | bytes 479240 | tf_op jit(solution)/shard_map/ppermute | solution.py:99
  (1 other events, 13.5 us)

commit v5 on v3

--- a/solution.py
+++ b/solution.py
@@ -89,7 +89,7 @@
     return stencil(extended, field, rate, wet)
 
 
-def column_mix(lateral, stacked_inverse, convective_rows):
+def to_rows(lateral):
     parts = lax.axis_size("lev")
     tracers, depth, rows, cols = lateral.shape
     part_rows = rows // parts
@@ -97,35 +97,119 @@
         lateral.reshape(tracers, depth, parts, part_rows, cols), (2, 0, 1, 3, 4)
     )
     columns = lax.all_to_all(outgoing, "lev", 0, 0, tiled=True)
+    return jnp.transpose(columns, (1, 0, 2, 3, 4)).reshape(tracers, parts * depth, part_rows, cols)
+
+
+def to_levels(block):
+    parts = lax.axis_size("lev")
+    tracers, levels, part_rows, cols = block.shape
+    depth = levels // parts
+    outgoing = jnp.transpose(block.reshape(tracers, parts, depth, part_rows, cols), (1, 0, 2, 3, 4))
+    returning = lax.all_to_all(outgoing, "lev", 0, 0, tiled=True)
+    return jnp.transpose(returning, (1, 2, 0, 3, 4)).reshape(tracers, depth, parts * part_rows, cols)
+
+
+def column_mix(block, stacked_inverse, convective_rows):
+    tracers, levels, part_rows, cols = block.shape
     mixed = []
     for tracer in range(tracers):
-        flat = columns[:, tracer].reshape(parts * depth, part_rows * cols)
+        flat = block[tracer].reshape(levels, part_rows * cols)
         both_states = jnp.dot(
             stacked_inverse[tracer], flat, precision=lax.Precision.HIGHEST
-        ).reshape(2, parts, depth, part_rows, cols)
-        mixed.append(jnp.where(convective_rows[None, None], both_states[1], both_states[0]))
-    returning = lax.all_to_all(jnp.stack(mixed, axis=1), "lev", 0, 0, tiled=True)
-    return jnp.transpose(returning, (1, 2, 0, 3, 4)).reshape(tracers, depth, rows, cols)
+        ).reshape(2, levels, part_rows, cols)
+        mixed.append(jnp.where(convective_rows[None], both_states[1], both_states[0]))
+    return jnp.stack(mixed)
+
+
+def horizontal_rows(block, rate, wet, codes):
+    count = lax.axis_size("tile")
+    parts = lax.axis_size("lev")
+    part = lax.axis_index("lev")
+    planes, part_rows, cols = block.shape
+    rows = parts * part_rows
+    own = jnp.concatenate(
+        [block[:, 0, :], block[:, -1, :], block[:, :, 0], block[:, :, -1]], axis=-1
+    )
+    gathered = lax.all_gather(own, "lev")
+    first_row = gathered[0, :, :cols]
+    last_row = gathered[parts - 1, :, cols : 2 * cols]
+
+    def column(offset):
+        pieces = gathered[:, :, 2 * cols + offset : 2 * cols + offset + part_rows]
+        return jnp.transpose(pieces, (1, 0, 2)).reshape(planes, rows)
+
+    first_col = column(0)
+    last_col = column(part_rows)
+    corner_set = jnp.stack(
+        [first_row[:, 0], first_row[:, -1], last_row[:, 0], last_row[:, -1]], axis=-1
+    )
+    side = jnp.concatenate([first_col, last_col, corner_set], axis=-1)
+    from_west = lax.ppermute(side, "tile", slot_pairs(count, 2))
+    from_east = lax.ppermute(side, "tile", slot_pairs(count, 3))
+    span = 2 * rows
+    upright = jnp.concatenate(
+        [first_row, last_row, from_west[..., span:], from_east[..., span:]], axis=-1
+    )
+    from_south = lax.ppermute(upright, "tile", slot_pairs(count, 0))
+    from_north = lax.ppermute(upright, "tile", slot_pairs(count, 1))
+
+    def strips(got, length):
+        return jnp.stack([got[..., :length], got[..., length : 2 * length]], axis=-2)
+
+    def corner(got, first, code):
+        cell = got[..., first : first + 4]
+        return jnp.where(
+            code == 0,
+            cell[..., 0],
+            jnp.where(code == 1, cell[..., 1], jnp.where(code == 2, cell[..., 2], cell[..., 3])),
+        )
+
+    south = pick(strips(from_south, cols), codes[0])
+    north = pick(strips(from_north, cols), codes[1])
+    west = pick(strips(from_west, rows), codes[2])
+    east = pick(strips(from_east, rows), codes[3])
+    base = 2 * cols
+    west_full = jnp.concatenate(
+        [corner(from_south, base, codes[4])[:, None], west, corner(from_north, base, codes[6])[:, None]],
+        axis=-1,
+    )
+    east_full = jnp.concatenate(
+        [corner(from_south, base + 4, codes[5])[:, None], east, corner(from_north, base + 4, codes[7])[:, None]],
+        axis=-1,
+    )
+    west_part = lax.dynamic_slice_in_dim(west_full, part * part_rows, part_rows + 2, axis=1)
+    east_part = lax.dynamic_slice_in_dim(east_full, part * part_rows, part_rows + 2, axis=1)
+    before = lax.dynamic_index_in_dim(gathered, (part + parts - 1) % parts, axis=0, keepdims=False)
+    after = lax.dynamic_index_in_dim(gathered, (part + 1) % parts, axis=0, keepdims=False)
+    above = jnp.where(part == 0, south, before[:, cols : 2 * cols])
+    below = jnp.where(part == parts - 1, north, after[:, :cols])
+    middle = jnp.concatenate([above[:, None, :], block, below[:, None, :]], axis=1)
+    extended = jnp.concatenate([west_part[:, :, None], middle, east_part[:, :, None]], axis=2)
+    return stencil(extended, block, rate, wet)
 
 
 def local(forcing, lateral_mix, sea_mask, convective, mixing_inverse, seam_links):
+    tracers, depth, rows, cols = forcing.shape
+    parts = lax.axis_size("lev")
+    part_rows = rows // parts
+    part = lax.axis_index("lev")
+    codes = seam_links[0] % 4
     wet = sea_mask.astype(jnp.float32)[None]
-    plane_rate = jnp.tile(lateral_mix, forcing.shape[0])[:, None, None]
-    codes = seam_links[0] % 4
-    parts = lax.axis_size("lev")
-    rows = forcing.shape[2] // parts
-    lev_here = lax.axis_index("lev")
-    convective_rows = lax.dynamic_slice_in_dim(convective, lev_here * rows, rows, axis=0) == 1
+    plane_rate = jnp.tile(lateral_mix, tracers)[:, None, None]
+    all_rates = lax.all_gather(lateral_mix, "lev", tiled=True)
+    block_rate = jnp.tile(all_rates, tracers)[:, None, None]
+    wet_rows = lax.dynamic_slice_in_dim(wet, part * part_rows, part_rows, axis=1)
+    convective_rows = lax.dynamic_slice_in_dim(convective, part * part_rows, part_rows, axis=0) == 1
     stacked_inverse = jnp.swapaxes(mixing_inverse, 2, 3).reshape(
         mixing_inverse.shape[0], -1, mixing_inverse.shape[2]
     )
-    tracers, depth, rows, cols = forcing.shape
-    adjoint = forcing
-    for step in range(STEPS):
-        planes = adjoint.reshape(tracers * depth, rows, cols)
-        lateral = horizontal(planes, plane_rate, wet, codes)
-        adjoint = column_mix(lateral.reshape(tracers, depth, rows, cols), stacked_inverse, convective_rows)
-    return adjoint
+    lateral = horizontal(forcing.reshape(tracers * depth, rows, cols), plane_rate, wet, codes)
+    block = column_mix(to_rows(lateral.reshape(tracers, depth, rows, cols)), stacked_inverse, convective_rows)
+    levels = block.shape[1]
+    for step in range(1, STEPS):
+        lateral = horizontal_rows(block.reshape(tracers * levels, part_rows, cols), block_rate, wet_rows, codes)
+        block = column_mix(lateral.reshape(tracers, levels, part_rows, cols), stacked_inverse, convective_rows)
+    return to_levels(block)
 
 
 def solution(mesh):

time: 152 us -> 138 us (0.908)
  blocking collectives: 40.1 us -> 32 us
  waiting for transfers between devices: 20.2 us -> 14.4 us
    all_to_all x3 -> x1, blocking collectives: 40.1 us -> 15.2 us  [to_levels(): returning = lax.all_to_all(outgoing, 'lev', 0, 0, tiled=True)]
    ppermute x0 -> x4, starting transfers between devices: none -> 16.4 us  [the longest x1 8.09 us: horizontal_rows(): from_east = lax.ppermute(side, 'tile', slot_pairs(count, 3))]
    ppermute x0 -> x4, waiting for transfers between devices: none -> 10.7 us  [the longest x1 7.4 us: horizontal_rows(): from_west = lax.ppermute(side, 'tile', slot_pairs(count, 2))]
    all_gather x0 -> x1, blocking collectives: none -> 8.46 us  [horizontal_rows(): gathered = lax.all_gather(own, 'lev')]
    all_to_all x1, waiting for transfers between devices: 8.28 us -> 0.01 us  [to_rows(): columns = lax.all_to_all(outgoing, 'lev', 0, 0, tiled=True)]
    unnamed x0 -> x1, blocking collectives: none -> 8.27 us
    ppermute x2 -> x1, starting transfers between devices: 17.3 us -> 9.2 us  [horizontal(): from_east = lax.ppermute(side, 'tile', slot_pairs(count, 3))]
    ppermute x2 -> x1, waiting for transfers between devices: 6.94 us -> 0.01 us  [horizontal(): from_west = lax.ppermute(side, 'tile', slot_pairs(count, 2))]
  transfers between devices with their start and end apart: 9 -> 9, of which waited for: 4 -> 4; matrix products, arithmetic and copies ran while one was open for 3% -> 4% of each run, Pallas kernels for 0% -> 0%
where the time goes in v5:
time: 138 us; the launch traced here: 137 us
  starting transfers between devices  45.9 us (33%)
  blocking collectives  32 us (23%)
  between operations  19.1 us (14%)
  local copies, waits for them, and re-layouts  15.5 us (11%)
  waiting for transfers between devices  14.4 us (10%)
  other arithmetic  7.08 us (5%)
  matrix products  2.84 us (2%)
    all_to_all x1, blocking collectives, to_levels(): returning = lax.all_to_all(outgoing, 'lev', 0, 0, tiled=True)  15.2 us
    ppermute x1, starting transfers between devices, horizontal(): from_north = lax.ppermute(upright, 'tile', slot_pairs(count, 1))  10.7 us
    ppermute x1, starting transfers between devices, horizontal(): from_east = lax.ppermute(side, 'tile', slot_pairs(count, 3))  9.2 us
    all_gather x1, blocking collectives, horizontal_rows(): gathered = lax.all_gather(own, 'lev')  8.46 us
    unnamed x1, blocking collectives  8.27 us
    ppermute x1, starting transfers between devices, horizontal_rows(): from_east = lax.ppermute(side, 'tile', slot_pairs(count, 3))  8.09 us
    ppermute x1, waiting for transfers between devices, horizontal_rows(): from_west = lax.ppermute(side, 'tile', slot_pairs(count, 2))  7.4 us
    all_to_all x1, starting transfers between devices, to_rows(): columns = lax.all_to_all(outgoing, 'lev', 0, 0, tiled=True)  5.83 us
  transfers between devices with their start and end apart: 9, of which 4 were waited for; matrix products, arithmetic and copies ran while one was open for 4% of the time, Pallas kernels for 0%

profile of v5, /device:TPU:1, one launch (start us, length us, event | category | flops | bytes accessed | tf_op | source)
XLA Modules:
  0.0 136.8 jit_solution(659664326400294473)
XLA Ops:
  0.0 1.2 fusion.38
  1.2 1.6 %fusion.39 = (f32[26,48,1]{2,1,0:T(8,128)S(1)}, f32[26,48,1]{2,1,0:T(8,128)S(1)}) fusion(f32[26,48,128]{2,1,0:T(8,128)} %bitcast.117), kind=kLoop, calls=%fused_computation.132 | loop fusion | bytes 19968 | tf_op jit(solution)/shard_map/slice | solution.py:49
  3.5 9.2 %collective-permute-start.1 = (f32[26,100]{1,0:T(8,128)S(1)}, f32[26,100]{1,0:T(8,128)S(1)}, u32[]{:S(2)}, u32[]{:S(2)}) collective-permute-start(f32[26,100]{1,0:T(8,128)S(1)} %concatenate.68), channel_id=1, source_target_pairs={{4,0},{8,4},{12,8},{16,12},{20,16},{24,20},{28,24},{32,28},{36,32}... | collective-permute-start | bytes 31208 | tf_op jit(solution)/shard_map/ppermute | solution.py:51
  12.7 1.9 %collective-permute-start = (f32[26,100]{1,0:T(8,128)S(1)}, f32[26,100]{1,0:T(8,128)S(1)}, u32[]{:S(2)}, u32[]{:S(2)}) collective-permute-start(f32[26,100]{1,0:T(8,128)S(1)} %concatenate.68), channel_id=1, source_target_pairs={{60,0},{0,4},{4,8},{8,12},{12,16},{16,20},{20,24},{24,28},{28,32},... | collective-permute-start | bytes 31208 | tf_op jit(solution)/shard_map/ppermute | solution.py:50
  33.4 10.7 %collective-permute-start.3 = (f32[26,264]{1,0:T(8,128)S(1)}, f32[26,264]{1,0:T(8,128)S(1)}, u32[]{:S(2)}, u32[]{:S(2)}) collective-permute-start(f32[26,264]{1,0:T(8,128)S(1)} %pad_maximum_fusion.8), channel_id=1, source_target_pairs={{64,0},{68,4},{72,8},{76,12},{80,16},{84,20},{88,24},{92,28},{96,3... | collective-permute-start | bytes 82376 | tf_op jit(solution)/shard_map/ppermute | solution.py:59
  44.1 1.9 %collective-permute-start.2 = (f32[26,264]{1,0:T(8,128)S(1)}, f32[26,264]{1,0:T(8,128)S(1)}, u32[]{:S(2)}, u32[]{:S(2)}) collective-permute-start(f32[26,264]{1,0:T(8,128)S(1)} %pad_maximum_fusion.8), channel_id=1, source_target_pairs={{448,0},{452,4},{456,8},{460,12},{464,16},{468,20},{472,24},{476,2... | collective-permute-start | bytes 82376 | tf_op jit(solution)/shard_map/ppermute | solution.py:58
  47.4 3.7 %collective-permute-done.2 = f32[26,264]{1,0:T(8,128)S(1)} collective-permute-done((f32[26,264]{1,0:T(8,128)S(1)}, f32[26,264]{1,0:T(8,128)S(1)}, u32[]{:S(2)}, u32[]{:S(2)}) %collective-permute-start.2) | collective-permute-done | bytes 27488 | tf_op jit(solution)/shard_map/ppermute | solution.py:58
  52.5 1.3 fusion.8
  54.0 1.3 copy.120
  55.3 5.8 %all-to-all-start = ((f32[4,2,13,12,128]{4,1,3,2,0:T(2,128)}), f32[4,2,13,12,128]{4,1,3,2,0:T(2,128)S(1)}, u32[]{:S(2)}, u32[]{:S(2)}) async-start(f32[4,2,13,12,128]{4,1,3,2,0:T(2,128)} %copy.120), calls=%async_computation | async-start | bytes 1277952 | tf_op jit(solution)/shard_map/all_to_all | solution.py:99
  61.2 1.3 dynamic-slice.4
  63.4 8.3 %all-reduce = f32[52]{0:T(128)S(1)} all-reduce(f32[52]{0:T(128)S(1)} %dynamic-update-slice), channel_id=1, replica_groups=mesh['tile'=128,'lev'=4] {'lev'}, use_global_device_ids=true, to_apply=%add | all-reduce | flops 52 | bytes 416
  72.7 1.7 %slice_reduce_fusion.1 = (f32[4,13,12,128]{3,2,1,0:T(8,128)S(1)}, f32[4,13,12,128]{3,2,1,0:T(8,128)S(1)}) fusion(f32[2,4,13,12,128]{4,0,3,2,1:T(2,128)S(1)} %bitcast.122), kind=kLoop, calls=%fused_computation.37 | loop fusion | bytes 1277952 | tf_op jit(solution)/shard_map/slice | solution.py:116
  78.0 8.5 %all-gather.1 = f32[4,104,280]{1,2,0:T(8,128)S(1)} all-gather(f32[1,104,280]{1,2,0:T(8,128)S(1)} %maximum_bitcast_fusion.1), channel_id=2, replica_groups=mesh['tile'=128,'lev'=4] {'lev'}, dimensions={0}, use_global_device_ids=true | all-gather | bytes 582400 | tf_op jit(solution)/shard_map/all_gather | solution.py:133
  86.6 8.1 %collective-permute-start.5 = (f32[104,100]{0,1:T(8,128)S(1)}, f32[104,100]{0,1:T(8,128)S(1)}, u32[]{:S(2)}, u32[]{:S(2)}) collective-permute-start(f32[104,100]{0,1:T(8,128)S(1)} %concatenate.78), channel_id=1, source_target_pairs={{4,0},{8,4},{12,8},{16,12},{20,16},{24,20},{28,24},{32,28},{36,32}... | collective-permute-start | bytes 124808 | tf_op jit(solution)/shard_map/ppermute | solution.py:148
  94.7 1.9 %collective-permute-start.4 = (f32[104,100]{0,1:T(8,128)S(1)}, f32[104,100]{0,1:T(8,128)S(1)}, u32[]{:S(2)}, u32[]{:S(2)}) collective-permute-start(f32[104,100]{0,1:T(8,128)S(1)} %concatenate.78), channel_id=1, source_target_pairs={{60,0},{0,4},{4,8},{8,12},{12,16},{16,20},{20,24},{24,28},{28,32},... | collective-permute-start | bytes 124808 | tf_op jit(solution)/shard_map/ppermute | solution.py:147
  96.6 7.4 %collective-permute-done.4 = f32[104,100]{0,1:T(8,128)S(1)} collective-permute-done((f32[104,100]{0,1:T(8,128)S(1)}, f32[104,100]{0,1:T(8,128)S(1)}, u32[]{:S(2)}, u32[]{:S(2)}) %collective-permute-start.4) | collective-permute-done | bytes 41632 | tf_op jit(solution)/shard_map/ppermute | solution.py:147
  104.1 1.9 %collective-permute-start.7 = (f32[104,264]{0,1:T(8,128)S(1)}, f32[104,264]{0,1:T(8,128)S(1)}, u32[]{:S(2)}, u32[]{:S(2)}) collective-permute-start(f32[104,264]{0,1:T(8,128)S(1)} %pad_maximum_fusion.7), channel_id=1, source_target_pairs={{64,0},{68,4},{72,8},{76,12},{80,16},{84,20},{88,24},{92,28},{96,3... | collective-permute-start | bytes 329480 | tf_op jit(solution)/shard_map/ppermute | solution.py:154
  106.0 4.4 %collective-permute-start.6 = (f32[104,264]{0,1:T(8,128)S(1)}, f32[104,264]{0,1:T(8,128)S(1)}, u32[]{:S(2)}, u32[]{:S(2)}) collective-permute-start(f32[104,264]{0,1:T(8,128)S(1)} %pad_maximum_fusion.7), channel_id=1, source_target_pairs={{448,0},{452,4},{456,8},{460,12},{464,16},{468,20},{472,24},{476,2... | collective-permute-start | bytes 329480 | tf_op jit(solution)/shard_map/ppermute | solution.py:153
  110.5 1.4 collective-permute-done.7
  112.0 1.9 %collective-permute-done.6 = f32[104,264]{0,1:T(8,128)S(1)} collective-permute-done((f32[104,264]{0,1:T(8,128)S(1)}, f32[104,264]{0,1:T(8,128)S(1)}, u32[]{:S(2)}, u32[]{:S(2)}) %collective-permute-start.6) | collective-permute-done | bytes 109856 | tf_op jit(solution)/shard_map/ppermute | solution.py:153
  115.1 1.2 maximum_maximum_fusion
  116.3 1.4 %fusion.2 = f32[104,12,128]{2,1,0:T(8,128)S(1)} fusion(f32[104,14,129]{2,1,0:T(8,128)S(1)} %get-tuple-element.10, f32[104,14,129]{2,1,0:T(8,128)S(1)} %get-tuple-element.9, f32[104,1,128]{2,1,0:T(1,128)S(1)} %copy.126, f32[104,12,128]{2,1,0:T(8,128)S(1)} %bitcast.115, f32[104,1,128]{2,1,0:T(1,128)S(1)} %copy.125, f32[104]{0:T(128)S(1)} %get-tuple-element.58, ...), kind=kLoop, calls=%fused_computation.11 | loop fusion | flops 2236416 | bytes 5225696 | tf_op jit(solution)/shard_map/mul | solution.py:41
  120.6 15.2 %all_to_all.10 = f32[4,2,13,12,128]{4,1,3,2,0:T(2,128)S(1)} all-to-all(f32[4,2,13,12,128]{4,1,3,2,0:T(2,128)S(1)} %copy.131), channel_id=1, replica_groups=mesh['tile'=128,'lev'=4] {'lev'}, dimensions={0} | all-to-all | bytes 1277952 | tf_op jit(solution)/shard_map/all_to_all | solution.py:108
  (133 shorter events, 14.5 us)
Async XLA Ops:
  1.2 13.5 %copy-start = (f32[2,13,48,128]{3,2,1,0:T(8,128)S(1)}, f32[2,13,48,128]{3,2,1,0:T(8,128)}, u32[]{:S(2)}) copy-start(f32[2,13,48,128]{3,2,1,0:T(8,128)} %param.6) | copy-start | bytes 1916932
  1.2 13.5 %copy-start.3 = (s32[1,8]{1,0:T(1,128)S(1)}, s32[1,8]{1,0:T(1,128)}, u32[]{:S(2)}) copy-start(s32[1,8]{1,0:T(1,128)} %param.11) | copy-start | bytes 100
  1.2 13.5 %copy-start.4 = (f32[13]{0:T(128)S(1)}, f32[13]{0:T(128)}, u32[]{:S(2)}) copy-start(f32[13]{0:T(128)} %param.7) | copy-start | bytes 160
  1.2 31.9 %copy-start.2 = (s32[48,128]{1,0:T(8,128)S(1)}, s32[48,128]{1,0:T(8,128)}, u32[]{:S(2)}) copy-start(s32[48,128]{1,0:T(8,128)} %param.8) | copy-start | bytes 73732
  3.5 29.6 %collective-permute-start.1 = (f32[26,100]{1,0:T(8,128)S(1)}, f32[26,100]{1,0:T(8,128)S(1)}, u32[]{:S(2)}, u32[]{:S(2)}) collective-permute-start(f32[26,100]{1,0:T(8,128)S(1)} %concatenate.68), channel_id=1, source_target_pairs={{4,0},{8,4},{12,8},{16,12},{20,16},{24,20},{28,24},{32,28},{36,32}... | collective-permute-start | bytes 31208 | tf_op jit(solution)/shard_map/ppermute | solution.py:51
  12.7 20.5 %collective-permute-start = (f32[26,100]{1,0:T(8,128)S(1)}, f32[26,100]{1,0:T(8,128)S(1)}, u32[]{:S(2)}, u32[]{:S(2)}) collective-permute-start(f32[26,100]{1,0:T(8,128)S(1)} %concatenate.68), channel_id=1, source_target_pairs={{60,0},{0,4},{4,8},{8,12},{12,16},{16,20},{20,24},{24,28},{28,32},... | collective-permute-start | bytes 31208 | tf_op jit(solution)/shard_map/ppermute | solution.py:50
  33.4 13.6 %collective-permute-start.3 = (f32[26,264]{1,0:T(8,128)S(1)}, f32[26,264]{1,0:T(8,128)S(1)}, u32[]{:S(2)}, u32[]{:S(2)}) collective-permute-start(f32[26,264]{1,0:T(8,128)S(1)} %pad_maximum_fusion.8), channel_id=1, source_target_pairs={{64,0},{68,4},{72,8},{76,12},{80,16},{84,20},{88,24},{92,28},{96,3... | collective-permute-start | bytes 82376 | tf_op jit(solution)/shard_map/ppermute | solution.py:59
  44.1 7.0 %collective-permute-start.2 = (f32[26,264]{1,0:T(8,128)S(1)}, f32[26,264]{1,0:T(8,128)S(1)}, u32[]{:S(2)}, u32[]{:S(2)}) collective-permute-start(f32[26,264]{1,0:T(8,128)S(1)} %pad_maximum_fusion.8), channel_id=1, source_target_pairs={{448,0},{452,4},{456,8},{460,12},{464,16},{468,20},{472,24},{476,2... | collective-permute-start | bytes 82376 | tf_op jit(solution)/shard_map/ppermute | solution.py:58
  53.9 7.2 %copy-start.1 = (f32[2,2,52,52]{3,1,2,0:T(2,128)S(1)}, f32[2,2,52,52]{3,1,2,0:T(2,128)}, u32[]{:S(2)}) copy-start(f32[2,2,52,52]{3,1,2,0:T(2,128)} %param.10) | copy-start | bytes 129796
  55.3 17.4 %all-to-all-start = ((f32[4,2,13,12,128]{4,1,3,2,0:T(2,128)}), f32[4,2,13,12,128]{4,1,3,2,0:T(2,128)S(1)}, u32[]{:S(2)}, u32[]{:S(2)}) async-start(f32[4,2,13,12,128]{4,1,3,2,0:T(2,128)} %copy.120), calls=%async_computation | async-start | bytes 1277952 | tf_op jit(solution)/shard_map/all_to_all | solution.py:99
  86.6 10.1 %collective-permute-start.5 = (f32[104,100]{0,1:T(8,128)S(1)}, f32[104,100]{0,1:T(8,128)S(1)}, u32[]{:S(2)}, u32[]{:S(2)}) collective-permute-start(f32[104,100]{0,1:T(8,128)S(1)} %concatenate.78), channel_id=1, source_target_pairs={{4,0},{8,4},{12,8},{16,12},{20,16},{24,20},{28,24},{32,28},{36,32}... | collective-permute-start | bytes 124808 | tf_op jit(solution)/shard_map/ppermute | solution.py:148
  94.7 9.4 %collective-permute-start.4 = (f32[104,100]{0,1:T(8,128)S(1)}, f32[104,100]{0,1:T(8,128)S(1)}, u32[]{:S(2)}, u32[]{:S(2)}) collective-permute-start(f32[104,100]{0,1:T(8,128)S(1)} %concatenate.78), channel_id=1, source_target_pairs={{60,0},{0,4},{4,8},{8,12},{12,16},{16,20},{20,24},{24,28},{28,32},... | collective-permute-start | bytes 124808 | tf_op jit(solution)/shard_map/ppermute | solution.py:147
  104.1 7.8 %collective-permute-start.7 = (f32[104,264]{0,1:T(8,128)S(1)}, f32[104,264]{0,1:T(8,128)S(1)}, u32[]{:S(2)}, u32[]{:S(2)}) collective-permute-start(f32[104,264]{0,1:T(8,128)S(1)} %pad_maximum_fusion.7), channel_id=1, source_target_pairs={{64,0},{68,4},{72,8},{76,12},{80,16},{84,20},{88,24},{92,28},{96,3... | collective-permute-start | bytes 329480 | tf_op jit(solution)/shard_map/ppermute | solution.py:154
  106.0 8.0 %collective-permute-start.6 = (f32[104,264]{0,1:T(8,128)S(1)}, f32[104,264]{0,1:T(8,128)S(1)}, u32[]{:S(2)}, u32[]{:S(2)}) collective-permute-start(f32[104,264]{0,1:T(8,128)S(1)} %pad_maximum_fusion.7), channel_id=1, source_target_pairs={{448,0},{452,4},{456,8},{460,12},{464,16},{468,20},{472,24},{476,2... | collective-permute-start | bytes 329480 | tf_op jit(solution)/shard_map/ppermute | solution.py:153

commit v6 on v5

--- a/solution.py
+++ b/solution.py
@@ -93,11 +93,18 @@
     parts = lax.axis_size("lev")
     tracers, depth, rows, cols = lateral.shape
     part_rows = rows // parts
-    outgoing = jnp.transpose(
-        lateral.reshape(tracers, depth, parts, part_rows, cols), (2, 0, 1, 3, 4)
-    )
-    columns = lax.all_to_all(outgoing, "lev", 0, 0, tiled=True)
-    return jnp.transpose(columns, (1, 0, 2, 3, 4)).reshape(tracers, parts * depth, part_rows, cols)
+    padded = jnp.pad(lateral, ((0, 0), (0, 0), (1, 1), (0, 0)))
+    edges = jnp.concatenate(
+        [lateral[..., :, 0], lateral[..., :, -1], lateral[..., 0, :], lateral[..., -1, :]], axis=-1
+    )
+    outgoing = []
+    for dest in range(parts):
+        window = padded[:, :, dest * part_rows : dest * part_rows + part_rows + 2, :]
+        outgoing.append(
+            jnp.concatenate([window.reshape(tracers, depth, (part_rows + 2) * cols), edges], axis=-1)
+        )
+    columns = lax.all_to_all(jnp.stack(outgoing), "lev", 0, 0, tiled=True)
+    return jnp.transpose(columns, (1, 0, 2, 3)).reshape(tracers, parts * depth, -1)
 
 
 def to_levels(block):
@@ -109,37 +116,29 @@
     return jnp.transpose(returning, (1, 2, 0, 3, 4)).reshape(tracers, depth, parts * part_rows, cols)
 
 
-def column_mix(block, stacked_inverse, convective_rows):
-    tracers, levels, part_rows, cols = block.shape
+def column_mix(block, stacked_inverse, convective_map):
+    tracers, levels, width = block.shape
     mixed = []
     for tracer in range(tracers):
-        flat = block[tracer].reshape(levels, part_rows * cols)
         both_states = jnp.dot(
-            stacked_inverse[tracer], flat, precision=lax.Precision.HIGHEST
-        ).reshape(2, levels, part_rows, cols)
-        mixed.append(jnp.where(convective_rows[None], both_states[1], both_states[0]))
+            stacked_inverse[tracer], block[tracer], precision=lax.Precision.HIGHEST
+        ).reshape(2, levels, width)
+        mixed.append(jnp.where(convective_map[None], both_states[1], both_states[0]))
     return jnp.stack(mixed)
 
 
-def horizontal_rows(block, rate, wet, codes):
+def horizontal_rows(halo_block, edges, rate, wet, codes):
     count = lax.axis_size("tile")
     parts = lax.axis_size("lev")
     part = lax.axis_index("lev")
-    planes, part_rows, cols = block.shape
+    planes, halo_rows, cols = halo_block.shape
+    part_rows = halo_rows - 2
     rows = parts * part_rows
-    own = jnp.concatenate(
-        [block[:, 0, :], block[:, -1, :], block[:, :, 0], block[:, :, -1]], axis=-1
-    )
-    gathered = lax.all_gather(own, "lev")
-    first_row = gathered[0, :, :cols]
-    last_row = gathered[parts - 1, :, cols : 2 * cols]
-
-    def column(offset):
-        pieces = gathered[:, :, 2 * cols + offset : 2 * cols + offset + part_rows]
-        return jnp.transpose(pieces, (1, 0, 2)).reshape(planes, rows)
-
-    first_col = column(0)
-    last_col = column(part_rows)
+    block = halo_block[:, 1:-1, :]
+    first_col = edges[:, :rows]
+    last_col = edges[:, rows : 2 * rows]
+    first_row = edges[:, 2 * rows : 2 * rows + cols]
+    last_row = edges[:, 2 * rows + cols :]
     corner_set = jnp.stack(
         [first_row[:, 0], first_row[:, -1], last_row[:, 0], last_row[:, -1]], axis=-1
     )
@@ -179,10 +178,8 @@
     )
     west_part = lax.dynamic_slice_in_dim(west_full, part * part_rows, part_rows + 2, axis=1)
     east_part = lax.dynamic_slice_in_dim(east_full, part * part_rows, part_rows + 2, axis=1)
-    before = lax.dynamic_index_in_dim(gathered, (part + parts - 1) % parts, axis=0, keepdims=False)
-    after = lax.dynamic_index_in_dim(gathered, (part + 1) % parts, axis=0, keepdims=False)
-    above = jnp.where(part == 0, south, before[:, cols : 2 * cols])
-    below = jnp.where(part == parts - 1, north, after[:, :cols])
+    above = jnp.where(part == 0, south, halo_block[:, 0, :])
+    below = jnp.where(part == parts - 1, north, halo_block[:, -1, :])
     middle = jnp.concatenate([above[:, None, :], block, below[:, None, :]], axis=1)
     extended = jnp.concatenate([west_part[:, :, None], middle, east_part[:, :, None]], axis=2)
     return stencil(extended, block, rate, wet)
@@ -199,17 +196,36 @@
     all_rates = lax.all_gather(lateral_mix, "lev", tiled=True)
     block_rate = jnp.tile(all_rates, tracers)[:, None, None]
     wet_rows = lax.dynamic_slice_in_dim(wet, part * part_rows, part_rows, axis=1)
-    convective_rows = lax.dynamic_slice_in_dim(convective, part * part_rows, part_rows, axis=0) == 1
+    is_convective = convective == 1
+    halo_convective = lax.dynamic_slice_in_dim(
+        jnp.pad(is_convective, ((1, 1), (0, 0))), part * part_rows, part_rows + 2, axis=0
+    )
+    first_map = jnp.concatenate(
+        [
+            halo_convective.reshape(-1),
+            is_convective[:, 0],
+            is_convective[:, -1],
+            is_convective[0, :],
+            is_convective[-1, :],
+        ]
+    )
+    convective_rows = lax.dynamic_slice_in_dim(
+        is_convective, part * part_rows, part_rows, axis=0
+    ).reshape(-1)
     stacked_inverse = jnp.swapaxes(mixing_inverse, 2, 3).reshape(
         mixing_inverse.shape[0], -1, mixing_inverse.shape[2]
     )
     lateral = horizontal(forcing.reshape(tracers * depth, rows, cols), plane_rate, wet, codes)
-    block = column_mix(to_rows(lateral.reshape(tracers, depth, rows, cols)), stacked_inverse, convective_rows)
-    levels = block.shape[1]
-    for step in range(1, STEPS):
-        lateral = horizontal_rows(block.reshape(tracers * levels, part_rows, cols), block_rate, wet_rows, codes)
-        block = column_mix(lateral.reshape(tracers, levels, part_rows, cols), stacked_inverse, convective_rows)
-    return to_levels(block)
+    mixed = column_mix(to_rows(lateral.reshape(tracers, depth, rows, cols)), stacked_inverse, first_map)
+    levels = mixed.shape[1]
+    halo_width = (part_rows + 2) * cols
+    halo_block = mixed[:, :, :halo_width].reshape(tracers * levels, part_rows + 2, cols)
+    edges = mixed[:, :, halo_width:].reshape(tracers * levels, -1)
+    lateral = horizontal_rows(halo_block, edges, block_rate, wet_rows, codes)
+    block = column_mix(
+        lateral.reshape(tracers, levels, part_rows * cols), stacked_inverse, convective_rows
+    )
+    return to_levels(block.reshape(tracers, levels, part_rows, cols))
 
 
 def solution(mesh):

time: 138 us -> 145 us (1.051)
  waiting for transfers between devices: 14.4 us -> 28.5 us
  blocking collectives: 32 us -> 21.4 us
  local copies, waits for them, and re-layouts: 15.5 us -> 17.6 us
  other arithmetic: 7.08 us -> 8.72 us
    all_to_all x1, waiting for transfers between devices: 0.01 us -> 11.9 us  [to_rows(): columns = lax.all_to_all(jnp.stack(outgoing), 'lev', 0, 0, tiled=True)]
    all_gather x1 -> x0, blocking collectives: 8.46 us -> none  [horizontal_rows(): gathered = lax.all_gather(own, 'lev')]
    slice x4 -> x14, local copies, waits for them, and re-layouts: 2.09 us -> 3.82 us  [the longest x2 2.47 us: column_mix(): block[tracer]]
    unnamed x1, blocking collectives: 8.27 us -> 6.58 us
    ppermute x1, waiting for transfers between devices: 1.35 us -> 2.81 us  [horizontal_rows(): from_north = lax.ppermute(upright, 'tile', slot_pairs(count, 1))]
    unnamed x29 -> x23, local copies, waits for them, and re-layouts: 3.7 us -> 2.46 us
  transfers between devices with their start and end apart: 9 -> 9, of which waited for: 4 -> 5; matrix products, arithmetic and copies ran while one was open for 4% -> 4% of each run, Pallas kernels for 0% -> 0%
where the time goes in v6:
time: 145 us; the launch traced here: 144 us
  starting transfers between devices  45.5 us (31%)
  waiting for transfers between devices  28.5 us (20%)
  blocking collectives  21.4 us (15%)
  between operations  19.2 us (13%)
  local copies, waits for them, and re-layouts  17.6 us (12%)
  other arithmetic  8.72 us (6%)
  matrix products  3.35 us (2%)
    all_to_all x1, blocking collectives, to_levels(): returning = lax.all_to_all(outgoing, 'lev', 0, 0, tiled=True)  14.8 us
    all_to_all x1, waiting for transfers between devices, to_rows(): columns = lax.all_to_all(jnp.stack(outgoing), 'lev', 0, 0, tiled=True)  11.9 us
    ppermute x1, starting transfers between devices, horizontal(): from_north = lax.ppermute(upright, 'tile', slot_pairs(count, 1))  10 us
    ppermute x1, starting transfers between devices, horizontal(): from_east = lax.ppermute(side, 'tile', slot_pairs(count, 3))  9.2 us
    ppermute x1, starting transfers between devices, horizontal_rows(): from_east = lax.ppermute(side, 'tile', slot_pairs(count, 3))  8.83 us
    ppermute x1, waiting for transfers between devices, horizontal_rows(): from_west = lax.ppermute(side, 'tile', slot_pairs(count, 2))  6.96 us
    unnamed x1, blocking collectives  6.58 us
    all_to_all x1, starting transfers between devices, to_rows(): columns = lax.all_to_all(jnp.stack(outgoing), 'lev', 0, 0, tiled=True)  5.48 us
  transfers between devices with their start and end apart: 9, of which 5 were waited for; matrix products, arithmetic and copies ran while one was open for 4% of the time, Pallas kernels for 0%

profile of v6, /device:TPU:1, one launch (start us, length us, event | category | flops | bytes accessed | tf_op | source)
XLA Modules:
  0.0 144.1 jit_solution(17953933433191036981)
XLA Ops:
  0.0 1.2 fusion.43
  1.3 1.6 %fusion.44 = (f32[26,48,1]{2,1,0:T(8,128)S(1)}, f32[26,48,1]{2,1,0:T(8,128)S(1)}) fusion(f32[26,48,128]{2,1,0:T(8,128)} %bitcast.115), kind=kLoop, calls=%fused_computation.134 | loop fusion | bytes 19968 | tf_op jit(solution)/shard_map/slice | solution.py:49
  3.6 9.2 %collective-permute-start.1 = (f32[26,100]{1,0:T(8,128)S(1)}, f32[26,100]{1,0:T(8,128)S(1)}, u32[]{:S(2)}, u32[]{:S(2)}) collective-permute-start(f32[26,100]{1,0:T(8,128)S(1)} %concatenate.88), channel_id=1, source_target_pairs={{4,0},{8,4},{12,8},{16,12},{20,16},{24,20},{28,24},{32,28},{36,32}... | collective-permute-start | bytes 31208 | tf_op jit(solution)/shard_map/ppermute | solution.py:51
  12.8 1.9 %collective-permute-start = (f32[26,100]{1,0:T(8,128)S(1)}, f32[26,100]{1,0:T(8,128)S(1)}, u32[]{:S(2)}, u32[]{:S(2)}) collective-permute-start(f32[26,100]{1,0:T(8,128)S(1)} %concatenate.88), channel_id=1, source_target_pairs={{60,0},{0,4},{4,8},{8,12},{12,16},{16,20},{20,24},{24,28},{28,32},... | collective-permute-start | bytes 31208 | tf_op jit(solution)/shard_map/ppermute | solution.py:50
  33.5 1.3 dynamic-slice.4
  35.7 6.6 %all-reduce.2 = f32[52]{0:T(128)S(1)} all-reduce(f32[52]{0:T(128)S(1)} %dynamic-update-slice), channel_id=1, replica_groups=mesh['tile'=128,'lev'=4] {'lev'}, use_global_device_ids=true, to_apply=%add.2 | all-reduce | flops 52 | bytes 416
  42.9 10.0 %collective-permute-start.3 = (f32[26,264]{1,0:T(8,128)S(1)}, f32[26,264]{1,0:T(8,128)S(1)}, u32[]{:S(2)}, u32[]{:S(2)}) collective-permute-start(f32[26,264]{1,0:T(8,128)S(1)} %pad_maximum_fusion.10), channel_id=1, source_target_pairs={{64,0},{68,4},{72,8},{76,12},{80,16},{84,20},{88,24},{92,28},{96,3... | collective-permute-start | bytes 82376 | tf_op jit(solution)/shard_map/ppermute | solution.py:59
  52.9 1.9 %collective-permute-start.2 = (f32[26,264]{1,0:T(8,128)S(1)}, f32[26,264]{1,0:T(8,128)S(1)}, u32[]{:S(2)}, u32[]{:S(2)}) collective-permute-start(f32[26,264]{1,0:T(8,128)S(1)} %pad_maximum_fusion.10), channel_id=1, source_target_pairs={{448,0},{452,4},{456,8},{460,12},{464,16},{468,20},{472,24},{476,2... | collective-permute-start | bytes 82376 | tf_op jit(solution)/shard_map/ppermute | solution.py:58
  56.2 3.7 %collective-permute-done.2 = f32[26,264]{1,0:T(8,128)S(1)} collective-permute-done((f32[26,264]{1,0:T(8,128)S(1)}, f32[26,264]{1,0:T(8,128)S(1)}, u32[]{:S(2)}, u32[]{:S(2)}) %collective-permute-start.2) | collective-permute-done | bytes 27488 | tf_op jit(solution)/shard_map/ppermute | solution.py:58
  61.4 1.3 fusion.9
  65.7 1.3 pad_maximum_fusion.2
  67.0 5.5 %all-to-all-start = ((f32[4,2,13,2144]{3,1,2,0:T(2,128)}), f32[4,2,13,2144]{3,1,2,0:T(2,128)S(1)}, u32[]{:S(2)}, u32[]{:S(2)}) async-start(f32[4,2,13,2144]{3,1,2,0:T(2,128)} %pad_maximum_fusion.2), calls=%async_computation | async-start | bytes 1810432 | tf_op jit(solution)/shard_map/all_to_all | solution.py:106
  72.7 11.9 %all-to-all-done = f32[4,2,13,2144]{3,1,2,0:T(2,128)S(1)} async-done(((f32[4,2,13,2144]{3,1,2,0:T(2,128)}), f32[4,2,13,2144]{3,1,2,0:T(2,128)S(1)}, u32[]{:S(2)}, u32[]{:S(2)}) %all-to-all-start) | async-done | bytes 891936 | tf_op jit(solution)/shard_map/all_to_all | solution.py:106
  84.6 2.4 %slice_reduce_fusion.1 = (f32[4,13,2144]{2,1,0:T(8,128)S(1)}, f32[4,13,2144]{2,1,0:T(8,128)S(1)}) fusion(f32[2,4,13,2144]{3,0,2,1:T(2,128)S(1)} %bitcast.119), kind=kLoop, calls=%fused_computation.46 | loop fusion | bytes 1783808 | tf_op jit(solution)/shard_map/slice | solution.py:124
  89.6 8.8 %collective-permute-start.5 = (f32[104,100]{1,0:T(8,128)S(1)}, f32[104,100]{1,0:T(8,128)S(1)}, u32[]{:S(2)}, u32[]{:S(2)}) collective-permute-start(f32[104,100]{1,0:T(8,128)S(1)} %pad_maximum_fusion.9), channel_id=1, source_target_pairs={{4,0},{8,4},{12,8},{16,12},{20,16},{24,20},{28,24},{32,28},{36,32}... | collective-permute-start | bytes 124808 | tf_op jit(solution)/shard_map/ppermute | solution.py:147
  98.5 1.9 %collective-permute-start.4 = (f32[104,100]{1,0:T(8,128)S(1)}, f32[104,100]{1,0:T(8,128)S(1)}, u32[]{:S(2)}, u32[]{:S(2)}) collective-permute-start(f32[104,100]{1,0:T(8,128)S(1)} %pad_maximum_fusion.9), channel_id=1, source_target_pairs={{60,0},{0,4},{4,8},{8,12},{12,16},{16,20},{20,24},{24,28},{28,32},... | collective-permute-start | bytes 124808 | tf_op jit(solution)/shard_map/ppermute | solution.py:146
  100.9 7.0 %collective-permute-done.4 = f32[104,100]{1,0:T(8,128)S(1)} collective-permute-done((f32[104,100]{1,0:T(8,128)S(1)}, f32[104,100]{1,0:T(8,128)S(1)}, u32[]{:S(2)}, u32[]{:S(2)}) %collective-permute-start.4) | collective-permute-done | bytes 41632 | tf_op jit(solution)/shard_map/ppermute | solution.py:146
  108.0 1.9 %collective-permute-start.7 = (f32[104,264]{1,0:T(8,128)S(1)}, f32[104,264]{1,0:T(8,128)S(1)}, u32[]{:S(2)}, u32[]{:S(2)}) collective-permute-start(f32[104,264]{1,0:T(8,128)S(1)} %pad_maximum_fusion.8), channel_id=1, source_target_pairs={{64,0},{68,4},{72,8},{76,12},{80,16},{84,20},{88,24},{92,28},{96,3... | collective-permute-start | bytes 329480 | tf_op jit(solution)/shard_map/ppermute | solution.py:153
  110.0 4.3 %collective-permute-start.6 = (f32[104,264]{1,0:T(8,128)S(1)}, f32[104,264]{1,0:T(8,128)S(1)}, u32[]{:S(2)}, u32[]{:S(2)}) collective-permute-start(f32[104,264]{1,0:T(8,128)S(1)} %pad_maximum_fusion.8), channel_id=1, source_target_pairs={{448,0},{452,4},{456,8},{460,12},{464,16},{468,20},{472,24},{476,2... | collective-permute-start | bytes 329480 | tf_op jit(solution)/shard_map/ppermute | solution.py:152
  114.8 2.8 %collective-permute-done.7 = f32[104,264]{1,0:T(8,128)S(1)} collective-permute-done((f32[104,264]{1,0:T(8,128)S(1)}, f32[104,264]{1,0:T(8,128)S(1)}, u32[]{:S(2)}, u32[]{:S(2)}) %collective-permute-start.7) | collective-permute-done | bytes 109856 | tf_op jit(solution)/shard_map/ppermute | solution.py:153
  117.7 3.1 %collective-permute-done.6 = f32[104,264]{1,0:T(8,128)S(1)} collective-permute-done((f32[104,264]{1,0:T(8,128)S(1)}, f32[104,264]{1,0:T(8,128)S(1)}, u32[]{:S(2)}, u32[]{:S(2)}) %collective-permute-start.6) | collective-permute-done | bytes 109856 | tf_op jit(solution)/shard_map/ppermute | solution.py:152
  122.9 1.2 maximum_maximum_fusion
  124.1 1.4 fusion.2
  128.4 14.8 %all_to_all.10 = f32[4,2,13,12,128]{4,1,3,2,0:T(2,128)S(1)} all-to-all(f32[4,2,13,12,128]{4,1,3,2,0:T(2,128)S(1)} %copy.150), channel_id=1, replica_groups=mesh['tile'=128,'lev'=4] {'lev'}, dimensions={0} | all-to-all | bytes 1277952 | tf_op jit(solution)/shard_map/all_to_all | solution.py:115
  (142 shorter events, 17.9 us)
Async XLA Ops:
  1.2 13.5 %copy-start = (f32[2,13,48,128]{3,2,1,0:T(8,128)S(1)}, f32[2,13,48,128]{3,2,1,0:T(8,128)}, u32[]{:S(2)}) copy-start(f32[2,13,48,128]{3,2,1,0:T(8,128)} %param.6) | copy-start | bytes 1916932
  1.2 13.5 %copy-start.4 = (s32[1,8]{1,0:T(1,128)S(1)}, s32[1,8]{1,0:T(1,128)}, u32[]{:S(2)}) copy-start(s32[1,8]{1,0:T(1,128)} %param.11) | copy-start | bytes 100
  1.2 13.6 %copy-start.5 = (f32[13]{0:T(128)S(1)}, f32[13]{0:T(128)}, u32[]{:S(2)}) copy-start(f32[13]{0:T(128)} %param.7) | copy-start | bytes 160
  1.3 14.3 %copy-start.3 = (s32[48,128]{1,0:T(8,128)S(1)}, s32[48,128]{1,0:T(8,128)}, u32[]{:S(2)}) copy-start(s32[48,128]{1,0:T(8,128)} %param.9) | copy-start | bytes 73732
  1.3 14.5 %copy-start.1 = (f32[2,2,52,52]{3,1,2,0:T(2,128)S(1)}, f32[2,2,52,52]{3,1,2,0:T(2,128)}, u32[]{:S(2)}) copy-start(f32[2,2,52,52]{3,1,2,0:T(2,128)} %param.10) | copy-start | bytes 129796
  2.8 39.6 %copy-start.2 = (s32[48,128]{1,0:T(8,128)S(1)}, s32[48,128]{1,0:T(8,128)}, u32[]{:S(2)}) copy-start(s32[48,128]{1,0:T(8,128)} %param.8) | copy-start | bytes 73732
  3.6 39.0 %collective-permute-start.1 = (f32[26,100]{1,0:T(8,128)S(1)}, f32[26,100]{1,0:T(8,128)S(1)}, u32[]{:S(2)}, u32[]{:S(2)}) collective-permute-start(f32[26,100]{1,0:T(8,128)S(1)} %concatenate.88), channel_id=1, source_target_pairs={{4,0},{8,4},{12,8},{16,12},{20,16},{24,20},{28,24},{32,28},{36,32}... | collective-permute-start | bytes 31208 | tf_op jit(solution)/shard_map/ppermute | solution.py:51
  12.8 29.9 %collective-permute-start = (f32[26,100]{1,0:T(8,128)S(1)}, f32[26,100]{1,0:T(8,128)S(1)}, u32[]{:S(2)}, u32[]{:S(2)}) collective-permute-start(f32[26,100]{1,0:T(8,128)S(1)} %concatenate.88), channel_id=1, source_target_pairs={{60,0},{0,4},{4,8},{8,12},{12,16},{16,20},{20,24},{24,28},{28,32},... | collective-permute-start | bytes 31208 | tf_op jit(solution)/shard_map/ppermute | solution.py:50
  42.9 13.0 %collective-permute-start.3 = (f32[26,264]{1,0:T(8,128)S(1)}, f32[26,264]{1,0:T(8,128)S(1)}, u32[]{:S(2)}, u32[]{:S(2)}) collective-permute-start(f32[26,264]{1,0:T(8,128)S(1)} %pad_maximum_fusion.10), channel_id=1, source_target_pairs={{64,0},{68,4},{72,8},{76,12},{80,16},{84,20},{88,24},{92,28},{96,3... | collective-permute-start | bytes 82376 | tf_op jit(solution)/shard_map/ppermute | solution.py:59
  52.9 7.0 %collective-permute-start.2 = (f32[26,264]{1,0:T(8,128)S(1)}, f32[26,264]{1,0:T(8,128)S(1)}, u32[]{:S(2)}, u32[]{:S(2)}) collective-permute-start(f32[26,264]{1,0:T(8,128)S(1)} %pad_maximum_fusion.10), channel_id=1, source_target_pairs={{448,0},{452,4},{456,8},{460,12},{464,16},{468,20},{472,24},{476,2... | collective-permute-start | bytes 82376 | tf_op jit(solution)/shard_map/ppermute | solution.py:58
  67.0 17.5 %all-to-all-start = ((f32[4,2,13,2144]{3,1,2,0:T(2,128)}), f32[4,2,13,2144]{3,1,2,0:T(2,128)S(1)}, u32[]{:S(2)}, u32[]{:S(2)}) async-start(f32[4,2,13,2144]{3,1,2,0:T(2,128)} %pad_maximum_fusion.2), calls=%async_computation | async-start | bytes 1810432 | tf_op jit(solution)/shard_map/all_to_all | solution.py:106
  89.6 11.2 %collective-permute-start.5 = (f32[104,100]{1,0:T(8,128)S(1)}, f32[104,100]{1,0:T(8,128)S(1)}, u32[]{:S(2)}, u32[]{:S(2)}) collective-permute-start(f32[104,100]{1,0:T(8,128)S(1)} %pad_maximum_fusion.9), channel_id=1, source_target_pairs={{4,0},{8,4},{12,8},{16,12},{20,16},{24,20},{28,24},{32,28},{36,32}... | collective-permute-start | bytes 124808 | tf_op jit(solution)/shard_map/ppermute | solution.py:147
  98.5 9.4 %collective-permute-start.4 = (f32[104,100]{1,0:T(8,128)S(1)}, f32[104,100]{1,0:T(8,128)S(1)}, u32[]{:S(2)}, u32[]{:S(2)}) collective-permute-start(f32[104,100]{1,0:T(8,128)S(1)} %pad_maximum_fusion.9), channel_id=1, source_target_pairs={{60,0},{0,4},{4,8},{8,12},{12,16},{16,20},{20,24},{24,28},{28,32},... | collective-permute-start | bytes 124808 | tf_op jit(solution)/shard_map/ppermute | solution.py:146
  108.0 9.5 %collective-permute-start.7 = (f32[104,264]{1,0:T(8,128)S(1)}, f32[104,264]{1,0:T(8,128)S(1)}, u32[]{:S(2)}, u32[]{:S(2)}) collective-permute-start(f32[104,264]{1,0:T(8,128)S(1)} %pad_maximum_fusion.8), channel_id=1, source_target_pairs={{64,0},{68,4},{72,8},{76,12},{80,16},{84,20},{88,24},{92,28},{96,3... | collective-permute-start | bytes 329480 | tf_op jit(solution)/shard_map/ppermute | solution.py:153
  110.0 10.7 %collective-permute-start.6 = (f32[104,264]{1,0:T(8,128)S(1)}, f32[104,264]{1,0:T(8,128)S(1)}, u32[]{:S(2)}, u32[]{:S(2)}) collective-permute-start(f32[104,264]{1,0:T(8,128)S(1)} %pad_maximum_fusion.8), channel_id=1, source_target_pairs={{448,0},{452,4},{456,8},{460,12},{464,16},{468,20},{472,24},{476,2... | collective-permute-start | bytes 329480 | tf_op jit(solution)/shard_map/ppermute | solution.py:152

commit v7 on v6

--- a/solution.py
+++ b/solution.py
@@ -89,13 +89,15 @@
     return stencil(extended, field, rate, wet)
 
 
-def to_rows(lateral):
+def to_rows(lateral, rate):
     parts = lax.axis_size("lev")
     tracers, depth, rows, cols = lateral.shape
     part_rows = rows // parts
     padded = jnp.pad(lateral, ((0, 0), (0, 0), (1, 1), (0, 0)))
+    rate_column = jnp.broadcast_to(rate[None, :, None], (tracers, depth, 1))
     edges = jnp.concatenate(
-        [lateral[..., :, 0], lateral[..., :, -1], lateral[..., 0, :], lateral[..., -1, :]], axis=-1
+        [lateral[..., :, 0], lateral[..., :, -1], lateral[..., 0, :], lateral[..., -1, :], rate_column],
+        axis=-1,
     )
     outgoing = []
     for dest in range(parts):
@@ -104,7 +106,8 @@
             jnp.concatenate([window.reshape(tracers, depth, (part_rows + 2) * cols), edges], axis=-1)
         )
     columns = lax.all_to_all(jnp.stack(outgoing), "lev", 0, 0, tiled=True)
-    return jnp.transpose(columns, (1, 0, 2, 3)).reshape(tracers, parts * depth, -1)
+    gathered = jnp.transpose(columns, (1, 0, 2, 3)).reshape(tracers, parts * depth, -1)
+    return gathered[..., :-1], gathered[0, :, -1]
 
 
 def to_levels(block):
@@ -193,8 +196,6 @@
     codes = seam_links[0] % 4
     wet = sea_mask.astype(jnp.float32)[None]
     plane_rate = jnp.tile(lateral_mix, tracers)[:, None, None]
-    all_rates = lax.all_gather(lateral_mix, "lev", tiled=True)
-    block_rate = jnp.tile(all_rates, tracers)[:, None, None]
     wet_rows = lax.dynamic_slice_in_dim(wet, part * part_rows, part_rows, axis=1)
     is_convective = convective == 1
     halo_convective = lax.dynamic_slice_in_dim(
@@ -216,7 +217,9 @@
         mixing_inverse.shape[0], -1, mixing_inverse.shape[2]
     )
     lateral = horizontal(forcing.reshape(tracers * depth, rows, cols), plane_rate, wet, codes)
-    mixed = column_mix(to_rows(lateral.reshape(tracers, depth, rows, cols)), stacked_inverse, first_map)
+    gathered, all_rates = to_rows(lateral.reshape(tracers, depth, rows, cols), lateral_mix)
+    block_rate = jnp.tile(all_rates, tracers)[:, None, None]
+    mixed = column_mix(gathered, stacked_inverse, first_map)
     levels = mixed.shape[1]
     halo_width = (part_rows + 2) * cols
     halo_block = mixed[:, :, :halo_width].reshape(tracers * levels, part_rows + 2, cols)

time: 145 us -> 134 us (0.924)
  blocking collectives: 21.4 us -> 16.7 us
  waiting for transfers between devices: 28.5 us -> 25.5 us
  local copies, waits for them, and re-layouts: 17.6 us -> 15.1 us
    unnamed x1 -> x0, blocking collectives: 6.58 us -> none
    ppermute x1, waiting for transfers between devices: 3.06 us -> 0.51 us  [horizontal_rows(): from_south = lax.ppermute(upright, 'tile', slot_pairs(count, 0))]
    all_to_all x1, blocking collectives: 14.8 us -> 16.7 us  [to_levels(): returning = lax.all_to_all(outgoing, 'lev', 0, 0, tiled=True)]
    slice x2, local copies, waits for them, and re-layouts: 2.47 us -> 0.77 us  [column_mix(): block[tracer]]
    unnamed x23 -> x20, local copies, waits for them, and re-layouts: 2.46 us -> 0.94 us
  transfers between devices with their start and end apart: 9 -> 9, of which waited for: 5 -> 5; matrix products, arithmetic and copies ran while one was open for 4% -> 3% of each run, Pallas kernels for 0% -> 0%
where the time goes in v7:
time: 134 us
  starting transfers between devices  45.9 us (34%)
  waiting for transfers between devices  25.5 us (19%)
  between operations  18.5 us (14%)
  blocking collectives  16.7 us (12%)
  local copies, waits for them, and re-layouts  15.1 us (11%)
  other arithmetic  8.73 us (7%)
  matrix products  3.35 us (2%)
    all_to_all x1, blocking collectives, to_levels(): returning = lax.all_to_all(outgoing, 'lev', 0, 0, tiled=True)  16.7 us
    all_to_all x1, waiting for transfers between devices, to_rows(): columns = lax.all_to_all(jnp.stack(outgoing), 'lev', 0, 0, tiled=True)  11.7 us
    ppermute x1, starting transfers between devices, horizontal(): from_north = lax.ppermute(upright, 'tile', slot_pairs(count, 1))  10.7 us
    ppermute x1, starting transfers between devices, horizontal(): from_east = lax.ppermute(side, 'tile', slot_pairs(count, 3))  9.2 us
    ppermute x1, starting transfers between devices, horizontal_rows(): from_east = lax.ppermute(side, 'tile', slot_pairs(count, 3))  8.1 us
    ppermute x1, waiting for transfers between devices, horizontal_rows(): from_west = lax.ppermute(side, 'tile', slot_pairs(count, 2))  6.86 us
    all_to_all x1, starting transfers between devices, to_rows(): columns = lax.all_to_all(jnp.stack(outgoing), 'lev', 0, 0, tiled=True)  5.85 us
    ppermute x1, starting transfers between devices, horizontal_rows(): from_south = lax.ppermute(upright, 'tile', slot_pairs(count, 0))  4.44 us
  transfers between devices with their start and end apart: 9, of which 5 were waited for; matrix products, arithmetic and copies ran while one was open for 3% of the time, Pallas kernels for 0%

profile of v7, /device:TPU:1, one launch (start us, length us, event | category | flops | bytes accessed | tf_op | source)
XLA Modules:
  0.0 133.7 jit_solution(2718079776047551904)
XLA Ops:
  0.0 1.2 fusion.48
  1.2 1.6 %fusion.49 = (f32[26,48,1]{2,1,0:T(8,128)S(1)}, f32[26,48,1]{2,1,0:T(8,128)S(1)}) fusion(f32[26,48,128]{2,1,0:T(8,128)} %bitcast.120), kind=kLoop, calls=%fused_computation.138 | loop fusion | bytes 19968 | tf_op jit(solution)/shard_map/slice | solution.py:49
  3.5 9.2 %collective-permute-start.1 = (f32[26,100]{1,0:T(8,128)S(1)}, f32[26,100]{1,0:T(8,128)S(1)}, u32[]{:S(2)}, u32[]{:S(2)}) collective-permute-start(f32[26,100]{1,0:T(8,128)S(1)} %concatenate.87), channel_id=1, source_target_pairs={{4,0},{8,4},{12,8},{16,12},{20,16},{24,20},{28,24},{32,28},{36,32}... | collective-permute-start | bytes 31208 | tf_op jit(solution)/shard_map/ppermute | solution.py:51
  12.8 1.9 %collective-permute-start = (f32[26,100]{1,0:T(8,128)S(1)}, f32[26,100]{1,0:T(8,128)S(1)}, u32[]{:S(2)}, u32[]{:S(2)}) collective-permute-start(f32[26,100]{1,0:T(8,128)S(1)} %concatenate.87), channel_id=1, source_target_pairs={{60,0},{0,4},{4,8},{8,12},{12,16},{16,20},{20,24},{24,28},{28,32},... | collective-permute-start | bytes 31208 | tf_op jit(solution)/shard_map/ppermute | solution.py:50
  33.7 10.7 %collective-permute-start.3 = (f32[26,264]{1,0:T(8,128)S(1)}, f32[26,264]{1,0:T(8,128)S(1)}, u32[]{:S(2)}, u32[]{:S(2)}) collective-permute-start(f32[26,264]{1,0:T(8,128)S(1)} %pad_maximum_fusion.10), channel_id=1, source_target_pairs={{64,0},{68,4},{72,8},{76,12},{80,16},{84,20},{88,24},{92,28},{96,3... | collective-permute-start | bytes 82376 | tf_op jit(solution)/shard_map/ppermute | solution.py:59
  44.4 1.9 %collective-permute-start.2 = (f32[26,264]{1,0:T(8,128)S(1)}, f32[26,264]{1,0:T(8,128)S(1)}, u32[]{:S(2)}, u32[]{:S(2)}) collective-permute-start(f32[26,264]{1,0:T(8,128)S(1)} %pad_maximum_fusion.10), channel_id=1, source_target_pairs={{448,0},{452,4},{456,8},{460,12},{464,16},{468,20},{472,24},{476,2... | collective-permute-start | bytes 82376 | tf_op jit(solution)/shard_map/ppermute | solution.py:58
  47.7 3.7 %collective-permute-done.2 = f32[26,264]{1,0:T(8,128)S(1)} collective-permute-done((f32[26,264]{1,0:T(8,128)S(1)}, f32[26,264]{1,0:T(8,128)S(1)}, u32[]{:S(2)}, u32[]{:S(2)}) %collective-permute-start.2) | collective-permute-done | bytes 27488 | tf_op jit(solution)/shard_map/ppermute | solution.py:58
  51.7 1.1 maximum_maximum_fusion.1
  52.8 1.3 fusion.9
  57.3 1.4 %pad_maximum_fusion.2 = f32[4,2,13,2145]{3,1,2,0:T(2,128)} fusion(f32[1,2,13,2145]{3,1,2,0:T(2,128)S(1)} %bitcast.132, f32[1,2,13,2145]{3,1,2,0:T(2,128)S(1)} %bitcast.133, f32[1,2,13,2145]{3,1,2,0:T(2,128)S(1)} %bitcast.134, f32[1,2,13,2145]{3,1,2,0:T(2,128)S(1)} %bitcast.135), kind=kLoop, calls=%fused_computation.10 | loop fusion | flops 669240 | bytes 1784640 | tf_op jit(solution)/shard_map/stack | solution.py:108
  58.7 5.9 %all-to-all-start = ((f32[4,2,13,2145]{3,1,2,0:T(2,128)}), f32[4,2,13,2145]{3,1,2,0:T(2,128)S(1)}, u32[]{:S(2)}, u32[]{:S(2)}) async-start(f32[4,2,13,2145]{3,1,2,0:T(2,128)} %pad_maximum_fusion.2), calls=%async_computation | async-start | bytes 1810432 | tf_op jit(solution)/shard_map/all_to_all | solution.py:108
  64.9 11.7 %all-to-all-done = f32[4,2,13,2145]{3,1,2,0:T(2,128)S(1)} async-done(((f32[4,2,13,2145]{3,1,2,0:T(2,128)}), f32[4,2,13,2145]{3,1,2,0:T(2,128)S(1)}, u32[]{:S(2)}, u32[]{:S(2)}) %all-to-all-start) | async-done | bytes 892352 | tf_op jit(solution)/shard_map/all_to_all | solution.py:108
  78.1 1.0 convolution_bitcast_fusion.1
  79.0 1.0 convolution_bitcast_fusion
  80.6 8.1 %collective-permute-start.5 = (f32[104,100]{1,0:T(8,128)S(1)}, f32[104,100]{1,0:T(8,128)S(1)}, u32[]{:S(2)}, u32[]{:S(2)}) collective-permute-start(f32[104,100]{1,0:T(8,128)S(1)} %pad_maximum_fusion.9), channel_id=1, source_target_pairs={{4,0},{8,4},{12,8},{16,12},{20,16},{24,20},{28,24},{32,28},{36,32}... | collective-permute-start | bytes 124808 | tf_op jit(solution)/shard_map/ppermute | solution.py:150
  88.7 1.9 %collective-permute-start.4 = (f32[104,100]{1,0:T(8,128)S(1)}, f32[104,100]{1,0:T(8,128)S(1)}, u32[]{:S(2)}, u32[]{:S(2)}) collective-permute-start(f32[104,100]{1,0:T(8,128)S(1)} %pad_maximum_fusion.9), channel_id=1, source_target_pairs={{60,0},{0,4},{4,8},{8,12},{12,16},{16,20},{20,24},{24,28},{28,32},... | collective-permute-start | bytes 124808 | tf_op jit(solution)/shard_map/ppermute | solution.py:149
  91.2 6.9 %collective-permute-done.4 = f32[104,100]{1,0:T(8,128)S(1)} collective-permute-done((f32[104,100]{1,0:T(8,128)S(1)}, f32[104,100]{1,0:T(8,128)S(1)}, u32[]{:S(2)}, u32[]{:S(2)}) %collective-permute-start.4) | collective-permute-done | bytes 41632 | tf_op jit(solution)/shard_map/ppermute | solution.py:149
  98.2 1.9 %collective-permute-start.7 = (f32[104,264]{1,0:T(8,128)S(1)}, f32[104,264]{1,0:T(8,128)S(1)}, u32[]{:S(2)}, u32[]{:S(2)}) collective-permute-start(f32[104,264]{1,0:T(8,128)S(1)} %pad_maximum_fusion.8), channel_id=1, source_target_pairs={{64,0},{68,4},{72,8},{76,12},{80,16},{84,20},{88,24},{92,28},{96,3... | collective-permute-start | bytes 329480 | tf_op jit(solution)/shard_map/ppermute | solution.py:156
  100.1 4.4 %collective-permute-start.6 = (f32[104,264]{1,0:T(8,128)S(1)}, f32[104,264]{1,0:T(8,128)S(1)}, u32[]{:S(2)}, u32[]{:S(2)}) collective-permute-start(f32[104,264]{1,0:T(8,128)S(1)} %pad_maximum_fusion.8), channel_id=1, source_target_pairs={{448,0},{452,4},{456,8},{460,12},{464,16},{468,20},{472,24},{476,2... | collective-permute-start | bytes 329480 | tf_op jit(solution)/shard_map/ppermute | solution.py:155
  105.1 2.7 %collective-permute-done.7 = f32[104,264]{1,0:T(8,128)S(1)} collective-permute-done((f32[104,264]{1,0:T(8,128)S(1)}, f32[104,264]{1,0:T(8,128)S(1)}, u32[]{:S(2)}, u32[]{:S(2)}) %collective-permute-start.7) | collective-permute-done | bytes 109856 | tf_op jit(solution)/shard_map/ppermute | solution.py:156
  110.6 1.2 maximum_maximum_fusion
  111.8 1.4 %fusion.2 = f32[104,12,128]{2,1,0:T(8,128)S(1)} fusion(f32[104,14,129]{2,1,0:T(8,128)S(1)} %get-tuple-element.10, f32[104,14,129]{2,1,0:T(8,128)S(1)} %get-tuple-element.9, f32[104,1,128]{2,1,0:T(1,128)S(1)} %bitcast.137, f32[104,12,128]{2,1,0:T(8,128)S(1)} %slice.635, f32[104,1,128]{2,1,0:T(1,128)S(1)} %bitcast.139, f32[104]{0:T(128)S(1)} %get-tuple-element.54, ...), kind=kLoop, calls=%fused_computation.14 | loop fusion | flops 2236416 | bytes 5225696 | tf_op jit(solution)/shard_map/mul | solution.py:41
  116.1 16.7 %all_to_all.10 = f32[4,2,13,12,128]{4,1,3,2,0:T(2,128)S(1)} all-to-all(f32[4,2,13,12,128]{4,1,3,2,0:T(2,128)S(1)} %copy.171), channel_id=1, replica_groups=mesh['tile'=128,'lev'=4] {'lev'}, dimensions={0} | all-to-all | bytes 1277952 | tf_op jit(solution)/shard_map/all_to_all | solution.py:118
  132.8 0.9 copy.173
  (138 shorter events, 15.7 us)
Async XLA Ops:
  1.2 13.5 %copy-start = (f32[2,13,48,128]{3,2,1,0:T(8,128)S(1)}, f32[2,13,48,128]{3,2,1,0:T(8,128)}, u32[]{:S(2)}) copy-start(f32[2,13,48,128]{3,2,1,0:T(8,128)} %param.6) | copy-start | bytes 1916932
  1.2 13.5 %copy-start.5 = (s32[1,8]{1,0:T(1,128)S(1)}, s32[1,8]{1,0:T(1,128)}, u32[]{:S(2)}) copy-start(s32[1,8]{1,0:T(1,128)} %param.11) | copy-start | bytes 100
  1.2 13.5 %copy-start.4 = (f32[13]{0:T(128)S(1)}, f32[13]{0:T(128)}, u32[]{:S(2)}) copy-start(f32[13]{0:T(128)} %param.7) | copy-start | bytes 160
  1.2 13.6 %copy-start.3 = (s32[48,128]{1,0:T(8,128)S(1)}, s32[48,128]{1,0:T(8,128)}, u32[]{:S(2)}) copy-start(s32[48,128]{1,0:T(8,128)} %param.9) | copy-start | bytes 73732
  1.2 13.6 %copy-start.1 = (f32[2,2,52,52]{3,1,2,0:T(2,128)S(1)}, f32[2,2,52,52]{3,1,2,0:T(2,128)}, u32[]{:S(2)}) copy-start(f32[2,2,52,52]{3,1,2,0:T(2,128)} %param.10) | copy-start | bytes 129796
  2.8 30.5 %copy-start.2 = (s32[48,128]{1,0:T(8,128)S(1)}, s32[48,128]{1,0:T(8,128)}, u32[]{:S(2)}) copy-start(s32[48,128]{1,0:T(8,128)} %param.8) | copy-start | bytes 73732
  3.5 29.9 %collective-permute-start.1 = (f32[26,100]{1,0:T(8,128)S(1)}, f32[26,100]{1,0:T(8,128)S(1)}, u32[]{:S(2)}, u32[]{:S(2)}) collective-permute-start(f32[26,100]{1,0:T(8,128)S(1)} %concatenate.87), channel_id=1, source_target_pairs={{4,0},{8,4},{12,8},{16,12},{20,16},{24,20},{28,24},{32,28},{36,32}... | collective-permute-start | bytes 31208 | tf_op jit(solution)/shard_map/ppermute | solution.py:51
  12.8 20.8 %collective-permute-start = (f32[26,100]{1,0:T(8,128)S(1)}, f32[26,100]{1,0:T(8,128)S(1)}, u32[]{:S(2)}, u32[]{:S(2)}) collective-permute-start(f32[26,100]{1,0:T(8,128)S(1)} %concatenate.87), channel_id=1, source_target_pairs={{60,0},{0,4},{4,8},{8,12},{12,16},{16,20},{20,24},{24,28},{28,32},... | collective-permute-start | bytes 31208 | tf_op jit(solution)/shard_map/ppermute | solution.py:50
  33.7 13.6 %collective-permute-start.3 = (f32[26,264]{1,0:T(8,128)S(1)}, f32[26,264]{1,0:T(8,128)S(1)}, u32[]{:S(2)}, u32[]{:S(2)}) collective-permute-start(f32[26,264]{1,0:T(8,128)S(1)} %pad_maximum_fusion.10), channel_id=1, source_target_pairs={{64,0},{68,4},{72,8},{76,12},{80,16},{84,20},{88,24},{92,28},{96,3... | collective-permute-start | bytes 82376 | tf_op jit(solution)/shard_map/ppermute | solution.py:59
  44.4 7.0 %collective-permute-start.2 = (f32[26,264]{1,0:T(8,128)S(1)}, f32[26,264]{1,0:T(8,128)S(1)}, u32[]{:S(2)}, u32[]{:S(2)}) collective-permute-start(f32[26,264]{1,0:T(8,128)S(1)} %pad_maximum_fusion.10), channel_id=1, source_target_pairs={{448,0},{452,4},{456,8},{460,12},{464,16},{468,20},{472,24},{476,2... | collective-permute-start | bytes 82376 | tf_op jit(solution)/shard_map/ppermute | solution.py:58
  58.7 17.9 %all-to-all-start = ((f32[4,2,13,2145]{3,1,2,0:T(2,128)}), f32[4,2,13,2145]{3,1,2,0:T(2,128)S(1)}, u32[]{:S(2)}, u32[]{:S(2)}) async-start(f32[4,2,13,2145]{3,1,2,0:T(2,128)} %pad_maximum_fusion.2), calls=%async_computation | async-start | bytes 1810432 | tf_op jit(solution)/shard_map/all_to_all | solution.py:108
  80.6 10.5 %collective-permute-start.5 = (f32[104,100]{1,0:T(8,128)S(1)}, f32[104,100]{1,0:T(8,128)S(1)}, u32[]{:S(2)}, u32[]{:S(2)}) collective-permute-start(f32[104,100]{1,0:T(8,128)S(1)} %pad_maximum_fusion.9), channel_id=1, source_target_pairs={{4,0},{8,4},{12,8},{16,12},{20,16},{24,20},{28,24},{32,28},{36,32}... | collective-permute-start | bytes 124808 | tf_op jit(solution)/shard_map/ppermute | solution.py:150
  88.7 9.4 %collective-permute-start.4 = (f32[104,100]{1,0:T(8,128)S(1)}, f32[104,100]{1,0:T(8,128)S(1)}, u32[]{:S(2)}, u32[]{:S(2)}) collective-permute-start(f32[104,100]{1,0:T(8,128)S(1)} %pad_maximum_fusion.9), channel_id=1, source_target_pairs={{60,0},{0,4},{4,8},{8,12},{12,16},{16,20},{20,24},{24,28},{28,32},... | collective-permute-start | bytes 124808 | tf_op jit(solution)/shard_map/ppermute | solution.py:149
  98.2 9.6 %collective-permute-start.7 = (f32[104,264]{1,0:T(8,128)S(1)}, f32[104,264]{1,0:T(8,128)S(1)}, u32[]{:S(2)}, u32[]{:S(2)}) collective-permute-start(f32[104,264]{1,0:T(8,128)S(1)} %pad_maximum_fusion.8), channel_id=1, source_target_pairs={{64,0},{68,4},{72,8},{76,12},{80,16},{84,20},{88,24},{92,28},{96,3... | collective-permute-start | bytes 329480 | tf_op jit(solution)/shard_map/ppermute | solution.py:156
  100.1 8.2 %collective-permute-start.6 = (f32[104,264]{1,0:T(8,128)S(1)}, f32[104,264]{1,0:T(8,128)S(1)}, u32[]{:S(2)}, u32[]{:S(2)}) collective-permute-start(f32[104,264]{1,0:T(8,128)S(1)} %pad_maximum_fusion.8), channel_id=1, source_target_pairs={{448,0},{452,4},{456,8},{460,12},{464,16},{468,20},{472,24},{476,2... | collective-permute-start | bytes 329480 | tf_op jit(solution)/shard_map/ppermute | solution.py:155

commit v8 on v7

--- a/solution.py
+++ b/solution.py
@@ -145,40 +145,40 @@
     corner_set = jnp.stack(
         [first_row[:, 0], first_row[:, -1], last_row[:, 0], last_row[:, -1]], axis=-1
     )
-    side = jnp.concatenate([first_col, last_col, corner_set], axis=-1)
-    from_west = lax.ppermute(side, "tile", slot_pairs(count, 2))
-    from_east = lax.ppermute(side, "tile", slot_pairs(count, 3))
-    span = 2 * rows
-    upright = jnp.concatenate(
-        [first_row, last_row, from_west[..., span:], from_east[..., span:]], axis=-1
-    )
-    from_south = lax.ppermute(upright, "tile", slot_pairs(count, 0))
-    from_north = lax.ppermute(upright, "tile", slot_pairs(count, 1))
+    row_pair = jnp.concatenate([first_row, last_row], axis=-1)
+    col_pair = jnp.pad(jnp.concatenate([first_col, last_col], axis=-1), ((0, 0), (0, 2 * (cols - rows))))
+    strip_pair = jnp.where(part < 2, row_pair, col_pair)
+    both = ("tile", "lev")
+
+    def lifted(slot_of_part):
+        return [
+            (source * parts + lev, target * parts + lev)
+            for lev in range(parts)
+            for source, target in slot_pairs(count, slot_of_part(lev))
+        ]
+
+    got_strips = lax.ppermute(strip_pair, both, lifted(lambda lev: lev))
+    got_corners = lax.ppermute(corner_set, both, lifted(lambda lev: 4 + lev))
+    shared = lax.all_gather(jnp.concatenate([got_strips, got_corners], axis=-1), "lev")
 
     def strips(got, length):
         return jnp.stack([got[..., :length], got[..., length : 2 * length]], axis=-2)
 
-    def corner(got, first, code):
-        cell = got[..., first : first + 4]
+    def corner(slot):
+        cell = shared[slot - 4, :, 2 * cols : 2 * cols + 4]
+        code = codes[slot]
         return jnp.where(
             code == 0,
             cell[..., 0],
             jnp.where(code == 1, cell[..., 1], jnp.where(code == 2, cell[..., 2], cell[..., 3])),
         )
 
-    south = pick(strips(from_south, cols), codes[0])
-    north = pick(strips(from_north, cols), codes[1])
-    west = pick(strips(from_west, rows), codes[2])
-    east = pick(strips(from_east, rows), codes[3])
-    base = 2 * cols
-    west_full = jnp.concatenate(
-        [corner(from_south, base, codes[4])[:, None], west, corner(from_north, base, codes[6])[:, None]],
-        axis=-1,
-    )
-    east_full = jnp.concatenate(
-        [corner(from_south, base + 4, codes[5])[:, None], east, corner(from_north, base + 4, codes[7])[:, None]],
-        axis=-1,
-    )
+    south = pick(strips(shared[0], cols), codes[0])
+    north = pick(strips(shared[1], cols), codes[1])
+    west = pick(strips(shared[2], rows), codes[2])
+    east = pick(strips(shared[3], rows), codes[3])
+    west_full = jnp.concatenate([corner(4)[:, None], west, corner(6)[:, None]], axis=-1)
+    east_full = jnp.concatenate([corner(5)[:, None], east, corner(7)[:, None]], axis=-1)
     west_part = lax.dynamic_slice_in_dim(west_full, part * part_rows, part_rows + 2, axis=1)
     east_part = lax.dynamic_slice_in_dim(east_full, part * part_rows, part_rows + 2, axis=1)
     above = jnp.where(part == 0, south, halo_block[:, 0, :])

time: 134 us -> 125 us (0.933)
  waiting for transfers between devices: 25.5 us -> 17.7 us
  starting transfers between devices: 45.9 us -> 42.9 us
  blocking collectives: 16.7 us -> 18.2 us
    ppermute x4 -> x2, waiting for transfers between devices: 10 us -> 2.29 us  [the longest x1 2.28 us: horizontal_rows(): got_strips = lax.ppermute(strip_pair, both, lifted(lambda lev: lev))]
    all_gather x0 -> x1, blocking collectives: none -> 5.59 us  [horizontal_rows(): lax.all_gather(jnp.concatenate([got_strips, got_corners], axis=-1), 'lev')]
    all_to_all x1, blocking collectives: 16.7 us -> 12.6 us  [to_levels(): returning = lax.all_to_all(outgoing, 'lev', 0, 0, tiled=True)]
    ppermute x4 -> x2, starting transfers between devices: 16.4 us -> 13.3 us  [the longest x1 6.96 us: horizontal_rows(): got_strips = lax.ppermute(strip_pair, both, lifted(lambda lev: lev))]
  transfers between devices with their start and end apart: 9 -> 7, of which waited for: 5 -> 3; matrix products, arithmetic and copies ran while one was open for 3% -> 2% of each run, Pallas kernels for 0% -> 0%
where the time goes in v8:
time: 125 us
  starting transfers between devices  42.9 us (34%)
  between operations  18.7 us (15%)
  blocking collectives  18.2 us (15%)
  waiting for transfers between devices  17.7 us (14%)
  local copies, waits for them, and re-layouts  15.2 us (12%)
  other arithmetic  8.61 us (7%)
  matrix products  3.35 us (3%)
    all_to_all x1, blocking collectives, to_levels(): returning = lax.all_to_all(outgoing, 'lev', 0, 0, tiled=True)  12.6 us
    all_to_all x1, waiting for transfers between devices, to_rows(): columns = lax.all_to_all(jnp.stack(outgoing), 'lev', 0, 0, tiled=True)  11.7 us
    ppermute x1, starting transfers between devices, horizontal(): from_north = lax.ppermute(upright, 'tile', slot_pairs(count, 1))  10.7 us
    ppermute x1, starting transfers between devices, horizontal(): from_east = lax.ppermute(side, 'tile', slot_pairs(count, 3))  9.2 us
    ppermute x1, starting transfers between devices, horizontal_rows(): got_strips = lax.ppermute(strip_pair, both, lifted(lambda lev: lev))  6.96 us
    ppermute x1, starting transfers between devices, horizontal_rows(): got_corners = lax.ppermute(corner_set, both, lifted(lambda lev: 4 + lev))  6.33 us
    all_to_all x1, starting transfers between devices, to_rows(): columns = lax.all_to_all(jnp.stack(outgoing), 'lev', 0, 0, tiled=True)  5.85 us
    all_gather x1, blocking collectives, horizontal_rows(): lax.all_gather(jnp.concatenate([got_strips, got_corners], axis=-1), 'lev')  5.59 us
  transfers between devices with their start and end apart: 7, of which 3 were waited for; matrix products, arithmetic and copies ran while one was open for 2% of the time, Pallas kernels for 0%

profile of v8, /device:TPU:1, one launch (start us, length us, event | category | flops | bytes accessed | tf_op | source)
XLA Modules:
  0.0 124.7 jit_solution(11264716675576933696)
XLA Ops:
  0.0 1.2 fusion.49
  1.2 1.6 %fusion.50 = (f32[26,48,1]{2,1,0:T(8,128)S(1)}, f32[26,48,1]{2,1,0:T(8,128)S(1)}) fusion(f32[26,48,128]{2,1,0:T(8,128)} %bitcast.131), kind=kLoop, calls=%fused_computation.144 | loop fusion | bytes 19968 | tf_op jit(solution)/shard_map/slice | solution.py:49
  3.5 9.2 %collective-permute-start.1 = (f32[26,100]{1,0:T(8,128)S(1)}, f32[26,100]{1,0:T(8,128)S(1)}, u32[]{:S(2)}, u32[]{:S(2)}) collective-permute-start(f32[26,100]{1,0:T(8,128)S(1)} %concatenate.86), channel_id=1, source_target_pairs={{4,0},{8,4},{12,8},{16,12},{20,16},{24,20},{28,24},{32,28},{36,32}... | collective-permute-start | bytes 31208 | tf_op jit(solution)/shard_map/ppermute | solution.py:51
  12.8 1.9 %collective-permute-start = (f32[26,100]{1,0:T(8,128)S(1)}, f32[26,100]{1,0:T(8,128)S(1)}, u32[]{:S(2)}, u32[]{:S(2)}) collective-permute-start(f32[26,100]{1,0:T(8,128)S(1)} %concatenate.86), channel_id=1, source_target_pairs={{60,0},{0,4},{4,8},{8,12},{12,16},{16,20},{20,24},{24,28},{28,32},... | collective-permute-start | bytes 31208 | tf_op jit(solution)/shard_map/ppermute | solution.py:50
  33.9 10.7 %collective-permute-start.3 = (f32[26,264]{1,0:T(8,128)S(1)}, f32[26,264]{1,0:T(8,128)S(1)}, u32[]{:S(2)}, u32[]{:S(2)}) collective-permute-start(f32[26,264]{1,0:T(8,128)S(1)} %pad_maximum_fusion.9), channel_id=1, source_target_pairs={{64,0},{68,4},{72,8},{76,12},{80,16},{84,20},{88,24},{92,28},{96,3... | collective-permute-start | bytes 82376 | tf_op jit(solution)/shard_map/ppermute | solution.py:59
  44.6 1.9 %collective-permute-start.2 = (f32[26,264]{1,0:T(8,128)S(1)}, f32[26,264]{1,0:T(8,128)S(1)}, u32[]{:S(2)}, u32[]{:S(2)}) collective-permute-start(f32[26,264]{1,0:T(8,128)S(1)} %pad_maximum_fusion.9), channel_id=1, source_target_pairs={{448,0},{452,4},{456,8},{460,12},{464,16},{468,20},{472,24},{476,2... | collective-permute-start | bytes 82376 | tf_op jit(solution)/shard_map/ppermute | solution.py:58
  47.9 3.7 %collective-permute-done.2 = f32[26,264]{1,0:T(8,128)S(1)} collective-permute-done((f32[26,264]{1,0:T(8,128)S(1)}, f32[26,264]{1,0:T(8,128)S(1)}, u32[]{:S(2)}, u32[]{:S(2)}) %collective-permute-start.2) | collective-permute-done | bytes 27488 | tf_op jit(solution)/shard_map/ppermute | solution.py:58
  51.9 1.1 maximum_maximum_fusion.1
  53.1 1.3 %fusion.9 = f32[26,48,128]{2,1,0:T(8,128)S(1)} fusion(f32[26,49,130]{2,1,0:T(8,128)S(1)} %get-tuple-element.8, f32[26,49,130]{2,1,0:T(8,128)S(1)} %get-tuple-element.7, f32[26,48,1]{2,1,0:T(8,128)S(1)} %copy.192, f32[26,48,128]{2,1,0:T(8,128)S(1)} %bitcast.134, f32[26,48,1]{2,1,0:T(8,128)S(1)} %copy.191, f32[26]{0:T(128)S(1)} %get-tuple-element.62, ...), kind=kLoop, calls=%fused_computation.31 | loop fusion | flops 2236416 | bytes 5146680 | tf_op jit(solution)/shard_map/mul | solution.py:41
  57.6 1.3 %pad_maximum_fusion.2 = f32[4,2,13,2145]{3,1,2,0:T(2,128)} fusion(f32[1,2,13,2145]{3,1,2,0:T(2,128)S(1)} %bitcast.145, f32[1,2,13,2145]{3,1,2,0:T(2,128)S(1)} %bitcast.146, f32[1,2,13,2145]{3,1,2,0:T(2,128)S(1)} %bitcast.147, f32[1,2,13,2145]{3,1,2,0:T(2,128)S(1)} %bitcast.148), kind=kLoop, calls=%fused_computation.10 | loop fusion | flops 669240 | bytes 1784640 | tf_op jit(solution)/shard_map/stack | solution.py:108
  58.9 5.9 %all-to-all-start = ((f32[4,2,13,2145]{3,1,2,0:T(2,128)}), f32[4,2,13,2145]{3,1,2,0:T(2,128)S(1)}, u32[]{:S(2)}, u32[]{:S(2)}) async-start(f32[4,2,13,2145]{3,1,2,0:T(2,128)} %pad_maximum_fusion.2), calls=%async_computation | async-start | bytes 1810432 | tf_op jit(solution)/shard_map/all_to_all | solution.py:108
  65.1 11.7 %all-to-all-done = f32[4,2,13,2145]{3,1,2,0:T(2,128)S(1)} async-done(((f32[4,2,13,2145]{3,1,2,0:T(2,128)}), f32[4,2,13,2145]{3,1,2,0:T(2,128)S(1)}, u32[]{:S(2)}, u32[]{:S(2)}) %all-to-all-start) | async-done | bytes 892352 | tf_op jit(solution)/shard_map/all_to_all | solution.py:108
  76.8 0.8 slice_reduce_fusion
  78.3 1.0 convolution_bitcast_fusion.1
  79.3 1.0 convolution_bitcast_fusion
  81.1 6.3 %collective-permute-start.5 = (f32[104,4]{1,0:T(8,128)S(1)}, f32[104,4]{1,0:T(8,128)S(1)}, u32[]{:S(2)}, u32[]{:S(2)}) collective-permute-start(f32[104,4]{1,0:T(8,128)S(1)} %pad_maximum_fusion.8), channel_id=1, source_target_pairs={{508,0},{448,4},{452,8},{456,12},{460,16},{464,20},{468,24},{472,2... | collective-permute-start | bytes 5000 | tf_op jit(solution)/shard_map/ppermute | solution.py:161
  87.6 7.0 %collective-permute-start.4 = (f32[104,256]{1,0:T(8,128)S(1)}, f32[104,256]{1,0:T(8,128)S(1)}, u32[]{:S(2)}, u32[]{:S(2)}) collective-permute-start(f32[104,256]{1,0:T(8,128)S(1)} %fusion.20), channel_id=1, source_target_pairs={{448,0},{452,4},{456,8},{460,12},{464,16},{468,20},{472,24},{476,2... | collective-permute-start | bytes 319496 | tf_op jit(solution)/shard_map/ppermute | solution.py:160
  94.7 2.3 %collective-permute-done.4 = f32[104,256]{1,0:T(8,128)S(1)} collective-permute-done((f32[104,256]{1,0:T(8,128)S(1)}, f32[104,256]{1,0:T(8,128)S(1)}, u32[]{:S(2)}, u32[]{:S(2)}) %collective-permute-start.4) | collective-permute-done | bytes 106528 | tf_op jit(solution)/shard_map/ppermute | solution.py:160
  97.1 5.6 %all-gather.1 = f32[4,104,260]{1,2,0:T(8,128)S(1)} all-gather(f32[1,104,260]{1,2,0:T(8,128)S(1)} %copy.204), channel_id=2, replica_groups=mesh['tile'=128,'lev'=4] {'lev'}, dimensions={0}, use_global_device_ids=true | all-gather | bytes 540800 | tf_op jit(solution)/shard_map/all_gather | solution.py:162
  104.9 0.7 copy.218
  105.7 1.2 maximum_maximum_fusion
  106.9 1.4 %fusion.2 = f32[104,12,128]{2,1,0:T(8,128)S(1)} fusion(f32[104,14,129]{2,1,0:T(8,128)S(1)} %get-tuple-element.10, f32[104,14,129]{2,1,0:T(8,128)S(1)} %get-tuple-element.9, f32[104,1,128]{2,1,0:T(1,128)S(1)} %bitcast.152, f32[104,12,128]{2,1,0:T(8,128)S(1)} %slice.652, f32[104,1,128]{2,1,0:T(1,128)S(1)} %bitcast.150, f32[104]{0:T(128)S(1)} %get-tuple-element.60, ...), kind=kLoop, calls=%fused_computation.14 | loop fusion | flops 2236416 | bytes 5225696 | tf_op jit(solution)/shard_map/mul | solution.py:41
  111.2 12.6 %all_to_all.10 = f32[4,2,13,12,128]{4,1,3,2,0:T(2,128)S(1)} all-to-all(f32[4,2,13,12,128]{4,1,3,2,0:T(2,128)S(1)} %copy.219), channel_id=1, replica_groups=mesh['tile'=128,'lev'=4] {'lev'}, dimensions={0} | all-to-all | bytes 1277952 | tf_op jit(solution)/shard_map/all_to_all | solution.py:118
  123.8 0.9 copy.221
  (137 shorter events, 13.7 us)
Async XLA Ops:
  1.2 13.5 %copy-start = (f32[2,13,48,128]{3,2,1,0:T(8,128)S(1)}, f32[2,13,48,128]{3,2,1,0:T(8,128)}, u32[]{:S(2)}) copy-start(f32[2,13,48,128]{3,2,1,0:T(8,128)} %param.6) | copy-start | bytes 1916932
  1.2 13.5 %copy-start.6 = (s32[1,8]{1,0:T(1,128)S(1)}, s32[1,8]{1,0:T(1,128)}, u32[]{:S(2)}) copy-start(s32[1,8]{1,0:T(1,128)} %param.11) | copy-start | bytes 100
  1.2 13.5 %copy-start.5 = (f32[13]{0:T(128)S(1)}, f32[13]{0:T(128)}, u32[]{:S(2)}) copy-start(f32[13]{0:T(128)} %param.7) | copy-start | bytes 160
  1.2 13.6 %copy-start.3 = (s32[48,128]{1,0:T(8,128)S(1)}, s32[48,128]{1,0:T(8,128)}, u32[]{:S(2)}) copy-start(s32[48,128]{1,0:T(8,128)} %param.9) | copy-start | bytes 73732
  1.2 13.6 %copy-start.1 = (f32[2,2,52,52]{3,1,2,0:T(2,128)S(1)}, f32[2,2,52,52]{3,1,2,0:T(2,128)}, u32[]{:S(2)}) copy-start(f32[2,2,52,52]{3,1,2,0:T(2,128)} %param.10) | copy-start | bytes 129796
  2.8 30.7 %copy-start.2 = (s32[48,128]{1,0:T(8,128)S(1)}, s32[48,128]{1,0:T(8,128)}, u32[]{:S(2)}) copy-start(s32[48,128]{1,0:T(8,128)} %param.8) | copy-start | bytes 73732
  3.5 30.2 %collective-permute-start.1 = (f32[26,100]{1,0:T(8,128)S(1)}, f32[26,100]{1,0:T(8,128)S(1)}, u32[]{:S(2)}, u32[]{:S(2)}) collective-permute-start(f32[26,100]{1,0:T(8,128)S(1)} %concatenate.86), channel_id=1, source_target_pairs={{4,0},{8,4},{12,8},{16,12},{20,16},{24,20},{28,24},{32,28},{36,32}... | collective-permute-start | bytes 31208 | tf_op jit(solution)/shard_map/ppermute | solution.py:51
  12.8 21.0 %collective-permute-start = (f32[26,100]{1,0:T(8,128)S(1)}, f32[26,100]{1,0:T(8,128)S(1)}, u32[]{:S(2)}, u32[]{:S(2)}) collective-permute-start(f32[26,100]{1,0:T(8,128)S(1)} %concatenate.86), channel_id=1, source_target_pairs={{60,0},{0,4},{4,8},{8,12},{12,16},{16,20},{20,24},{24,28},{28,32},... | collective-permute-start | bytes 31208 | tf_op jit(solution)/shard_map/ppermute | solution.py:50
  33.9 13.6 %collective-permute-start.3 = (f32[26,264]{1,0:T(8,128)S(1)}, f32[26,264]{1,0:T(8,128)S(1)}, u32[]{:S(2)}, u32[]{:S(2)}) collective-permute-start(f32[26,264]{1,0:T(8,128)S(1)} %pad_maximum_fusion.9), channel_id=1, source_target_pairs={{64,0},{68,4},{72,8},{76,12},{80,16},{84,20},{88,24},{92,28},{96,3... | collective-permute-start | bytes 82376 | tf_op jit(solution)/shard_map/ppermute | solution.py:59
  44.6 7.0 %collective-permute-start.2 = (f32[26,264]{1,0:T(8,128)S(1)}, f32[26,264]{1,0:T(8,128)S(1)}, u32[]{:S(2)}, u32[]{:S(2)}) collective-permute-start(f32[26,264]{1,0:T(8,128)S(1)} %pad_maximum_fusion.9), channel_id=1, source_target_pairs={{448,0},{452,4},{456,8},{460,12},{464,16},{468,20},{472,24},{476,2... | collective-permute-start | bytes 82376 | tf_op jit(solution)/shard_map/ppermute | solution.py:58
  58.9 17.9 %all-to-all-start = ((f32[4,2,13,2145]{3,1,2,0:T(2,128)}), f32[4,2,13,2145]{3,1,2,0:T(2,128)S(1)}, u32[]{:S(2)}, u32[]{:S(2)}) async-start(f32[4,2,13,2145]{3,1,2,0:T(2,128)} %pad_maximum_fusion.2), calls=%async_computation | async-start | bytes 1810432 | tf_op jit(solution)/shard_map/all_to_all | solution.py:108
  80.5 7.0 %copy-start.4 = (pred[256]{0:T(512)(128)(4,1)S(1)}, pred[256]{0:T(512)(128)(4,1)}, u32[]{:S(2)}) copy-start(pred[256]{0:T(512)(128)(4,1)} %constant.132.clone.1) | copy-start | bytes 772
  81.1 13.6 %collective-permute-start.5 = (f32[104,4]{1,0:T(8,128)S(1)}, f32[104,4]{1,0:T(8,128)S(1)}, u32[]{:S(2)}, u32[]{:S(2)}) collective-permute-start(f32[104,4]{1,0:T(8,128)S(1)} %pad_maximum_fusion.8), channel_id=1, source_target_pairs={{508,0},{448,4},{452,8},{456,12},{460,16},{464,20},{468,24},{472,2... | collective-permute-start | bytes 5000 | tf_op jit(solution)/shard_map/ppermute | solution.py:161
  87.6 9.4 %collective-permute-start.4 = (f32[104,256]{1,0:T(8,128)S(1)}, f32[104,256]{1,0:T(8,128)S(1)}, u32[]{:S(2)}, u32[]{:S(2)}) collective-permute-start(f32[104,256]{1,0:T(8,128)S(1)} %fusion.20), channel_id=1, source_target_pairs={{448,0},{452,4},{456,8},{460,12},{464,16},{468,20},{472,24},{476,2... | collective-permute-start | bytes 319496 | tf_op jit(solution)/shard_map/ppermute | solution.py:160

commit v9 on v8

--- a/solution.py
+++ b/solution.py
@@ -41,47 +41,66 @@
     return wet * ((1.0 - 6.0 * rate) * field + rate * edge_sum + 0.5 * rate * diag_sum)
 
 
-def horizontal(field, rate, wet, codes):
+def fetch_seams(strip_pair, corner_set):
     count = lax.axis_size("tile")
-    corner_set = jnp.stack(
-        [field[..., 0, 0], field[..., 0, -1], field[..., -1, 0], field[..., -1, -1]], axis=-1
-    )
-    side = jnp.concatenate([field[..., :, 0], field[..., :, -1], corner_set], axis=-1)
-    from_west = lax.ppermute(side, "tile", slot_pairs(count, 2))
-    from_east = lax.ppermute(side, "tile", slot_pairs(count, 3))
-    cols = field.shape[-1]
-    rows = field.shape[-2]
-    span = 2 * rows
-    upright = jnp.concatenate(
-        [field[..., 0, :], field[..., -1, :], from_west[..., span:], from_east[..., span:]], axis=-1
-    )
-    from_south = lax.ppermute(upright, "tile", slot_pairs(count, 0))
-    from_north = lax.ppermute(upright, "tile", slot_pairs(count, 1))
-
+    parts = lax.axis_size("lev")
+    both = ("tile", "lev")
+
+    def lifted(slot_of_part):
+        return [
+            (source * parts + lev, target * parts + lev)
+            for lev in range(parts)
+            for source, target in slot_pairs(count, slot_of_part(lev))
+        ]
+
+    got_strips = lax.ppermute(strip_pair, both, lifted(lambda lev: lev))
+    got_corners = lax.ppermute(corner_set, both, lifted(lambda lev: 4 + lev))
+    return jnp.concatenate([got_strips, got_corners], axis=-1)
+
+
+def seam_pieces(shared, codes, rows, cols):
     def strips(got, length):
         return jnp.stack([got[..., :length], got[..., length : 2 * length]], axis=-2)
 
-    south = pick(strips(from_south, cols), codes[0])
-    north = pick(strips(from_north, cols), codes[1])
-    west = pick(strips(from_west, rows), codes[2])
-    east = pick(strips(from_east, rows), codes[3])
-    base = 2 * cols
-    sources = [
-        (from_south, base),
-        (from_south, base + 4),
-        (from_north, base),
-        (from_north, base + 4),
-    ]
-    corners = []
-    for slot, (got, first) in zip(range(4, 8), sources):
+    def corner(slot):
+        cell = shared[slot - 4, :, 2 * cols : 2 * cols + 4]
         code = codes[slot]
-        cell = got[..., first : first + 4]
-        value = jnp.where(
+        return jnp.where(
             code == 0,
             cell[..., 0],
             jnp.where(code == 1, cell[..., 1], jnp.where(code == 2, cell[..., 2], cell[..., 3])),
         )
-        corners.append(value)
+
+    south = pick(strips(shared[0], cols), codes[0])
+    north = pick(strips(shared[1], cols), codes[1])
+    west = pick(strips(shared[2], rows), codes[2])
+    east = pick(strips(shared[3], rows), codes[3])
+    return south, north, west, east, [corner(slot) for slot in range(4, 8)]
+
+
+def horizontal(field, rate, wet, codes, tracers):
+    parts = lax.axis_size("lev")
+    part = lax.axis_index("lev")
+    planes, rows, cols = field.shape
+    depth = planes // tracers
+    own = jnp.concatenate(
+        [
+            field[:, 0, :],
+            field[:, -1, :],
+            jnp.pad(jnp.concatenate([field[:, :, 0], field[:, :, -1]], axis=-1), ((0, 0), (0, 2 * (cols - rows)))),
+            jnp.stack([field[:, 0, 0], field[:, 0, -1], field[:, -1, 0], field[:, -1, -1]], axis=-1),
+        ],
+        axis=-1,
+    )
+    gathered = lax.all_gather(own, "lev")
+    every = jnp.transpose(gathered.reshape(parts, tracers, depth, -1), (1, 0, 2, 3)).reshape(
+        tracers * parts * depth, -1
+    )
+    strip_pair = jnp.where(part < 2, every[:, : 2 * cols], every[:, 2 * cols : 4 * cols])
+    fetched = fetch_seams(strip_pair, every[:, 4 * cols :])
+    outgoing = jnp.transpose(fetched.reshape(tracers, parts, depth, -1), (1, 0, 2, 3))
+    shared = lax.all_to_all(outgoing, "lev", 0, 0, tiled=True).reshape(parts, planes, -1)
+    south, north, west, east, corners = seam_pieces(shared, codes, rows, cols)
     middle = jnp.concatenate([west[..., None], field, east[..., None]], axis=-1)
     top_row = jnp.concatenate([corners[0][..., None], south, corners[1][..., None]], axis=-1)
     bottom_row = jnp.concatenate([corners[2][..., None], north, corners[3][..., None]], axis=-1)
@@ -147,38 +166,11 @@
     )
     row_pair = jnp.concatenate([first_row, last_row], axis=-1)
     col_pair = jnp.pad(jnp.concatenate([first_col, last_col], axis=-1), ((0, 0), (0, 2 * (cols - rows))))
-    strip_pair = jnp.where(part < 2, row_pair, col_pair)
-    both = ("tile", "lev")
-
-    def lifted(slot_of_part):
-        return [
-            (source * parts + lev, target * parts + lev)
-            for lev in range(parts)
-            for source, target in slot_pairs(count, slot_of_part(lev))
-        ]
-
-    got_strips = lax.ppermute(strip_pair, both, lifted(lambda lev: lev))
-    got_corners = lax.ppermute(corner_set, both, lifted(lambda lev: 4 + lev))
-    shared = lax.all_gather(jnp.concatenate([got_strips, got_corners], axis=-1), "lev")
-
-    def strips(got, length):
-        return jnp.stack([got[..., :length], got[..., length : 2 * length]], axis=-2)
-
-    def corner(slot):
-        cell = shared[slot - 4, :, 2 * cols : 2 * cols + 4]
-        code = codes[slot]
-        return jnp.where(
-            code == 0,
-            cell[..., 0],
-            jnp.where(code == 1, cell[..., 1], jnp.where(code == 2, cell[..., 2], cell[..., 3])),
-        )
-
-    south = pick(strips(shared[0], cols), codes[0])
-    north = pick(strips(shared[1], cols), codes[1])
-    west = pick(strips(shared[2], rows), codes[2])
-    east = pick(strips(shared[3], rows), codes[3])
-    west_full = jnp.concatenate([corner(4)[:, None], west, corner(6)[:, None]], axis=-1)
-    east_full = jnp.concatenate([corner(5)[:, None], east, corner(7)[:, None]], axis=-1)
+    fetched = fetch_seams(jnp.where(part < 2, row_pair, col_pair), corner_set)
+    shared = lax.all_gather(fetched, "lev")
+    south, north, west, east, corners = seam_pieces(shared, codes, rows, cols)
+    west_full = jnp.concatenate([corners[0][:, None], west, corners[2][:, None]], axis=-1)
+    east_full = jnp.concatenate([corners[1][:, None], east, corners[3][:, None]], axis=-1)
     west_part = lax.dynamic_slice_in_dim(west_full, part * part_rows, part_rows + 2, axis=1)
     east_part = lax.dynamic_slice_in_dim(east_full, part * part_rows, part_rows + 2, axis=1)
     above = jnp.where(part == 0, south, halo_block[:, 0, :])
@@ -216,7 +208,7 @@
     stacked_inverse = jnp.swapaxes(mixing_inverse, 2, 3).reshape(
         mixing_inverse.shape[0], -1, mixing_inverse.shape[2]
     )
-    lateral = horizontal(forcing.reshape(tracers * depth, rows, cols), plane_rate, wet, codes)
+    lateral = horizontal(forcing.reshape(tracers * depth, rows, cols), plane_rate, wet, codes, tracers)
     gathered, all_rates = to_rows(lateral.reshape(tracers, depth, rows, cols), lateral_mix)
     block_rate = jnp.tile(all_rates, tracers)[:, None, None]
     mixed = column_mix(gathered, stacked_inverse, first_map)

time: 125 us -> 132 us (1.056)
  blocking collectives: 18.2 us -> 32 us
  starting transfers between devices: 42.9 us -> 30.3 us
  local copies, waits for them, and re-layouts: 15.2 us -> 19 us
  waiting for transfers between devices: 17.7 us -> 19.4 us
    ppermute x6 -> x4, starting transfers between devices: 37 us -> 19.2 us  [the longest x2 11.5 us: fetch_seams(): got_strips = lax.ppermute(strip_pair, both, lifted(lambda lev: lev))]
    all_gather x1 -> x2, blocking collectives: 5.59 us -> 20.3 us  [the longest x1 12.7 us: horizontal(): gathered = lax.all_gather(own, 'lev')]
    all_to_all x0 -> x1, starting transfers between devices: none -> 7.46 us  [horizontal(): lax.all_to_all(outgoing, 'lev', 0, 0, tiled=True).reshape(parts, planes, -1)]
    all_to_all x1, starting transfers between devices: 5.85 us -> 3.67 us  [to_rows(): columns = lax.all_to_all(jnp.stack(outgoing), 'lev', 0, 0, tiled=True)]
    ppermute x6 -> x4, waiting for transfers between devices: 6.02 us -> 7.75 us  [the longest x2 7.13 us: fetch_seams(): got_strips = lax.ppermute(strip_pair, both, lifted(lambda lev: lev))]
    slice x6 -> x19, local copies, waits for them, and re-layouts: 3.59 us -> 5.21 us  [the longest x1 1.86 us: horizontal(): field[:, :, 0]]
  transfers between devices with their start and end apart: 7 -> 6, of which waited for: 3 -> 4; matrix products, arithmetic and copies ran while one was open for 2% -> 1% of each run, Pallas kernels for 0% -> 0%
where the time goes in v9:
time: 132 us; the launch traced here: 131 us
  blocking collectives  32 us (24%)
  starting transfers between devices  30.3 us (23%)
  waiting for transfers between devices  19.4 us (15%)
  local copies, waits for them, and re-layouts  19 us (14%)
  between operations  18.2 us (14%)
  other arithmetic  8.48 us (6%)
  matrix products  3.35 us (3%)
    all_gather x1, blocking collectives, horizontal(): gathered = lax.all_gather(own, 'lev')  12.7 us
    all_to_all x1, blocking collectives, to_levels(): returning = lax.all_to_all(outgoing, 'lev', 0, 0, tiled=True)  11.6 us
    all_to_all x1, waiting for transfers between devices, to_rows(): columns = lax.all_to_all(jnp.stack(outgoing), 'lev', 0, 0, tiled=True)  11.6 us
    ppermute x2, starting transfers between devices, fetch_seams(): got_strips = lax.ppermute(strip_pair, both, lifted(lambda lev: lev))  11.5 us
    all_gather x1, blocking collectives, horizontal_rows(): shared = lax.all_gather(fetched, 'lev')  7.68 us
    ppermute x2, starting transfers between devices, fetch_seams(): got_corners = lax.ppermute(corner_set, both, lifted(lambda lev: 4 + lev))  7.63 us
    all_to_all x1, starting transfers between devices, horizontal(): lax.all_to_all(outgoing, 'lev', 0, 0, tiled=True).reshape(parts, planes, -1)  7.46 us
    ppermute x2, waiting for transfers between devices, fetch_seams(): got_strips = lax.ppermute(strip_pair, both, lifted(lambda lev: lev))  7.13 us
  transfers between devices with their start and end apart: 6, of which 4 were waited for; matrix products, arithmetic and copies ran while one was open for 1% of the time, Pallas kernels for 0%

profile of v9, /device:TPU:1, one launch (start us, length us, event | category | flops | bytes accessed | tf_op | source)
XLA Modules:
  0.0 130.7 jit_solution(2106301065624429648)
XLA Ops:
  0.0 1.0 fusion.41
  1.0 1.9 %slice_reduce_fusion.1 = (f32[26,48]{1,0:T(8,128)S(1)}, f32[26,48]{1,0:T(8,128)S(1)}) fusion(f32[26,48,128]{2,1,0:T(8,128)} %bitcast.137), kind=kLoop, calls=%fused_computation.42 | loop fusion | bytes 19968 | tf_op jit(solution)/shard_map/slice | solution.py:90
  2.9 1.2 fusion.40
  4.3 12.7 %all-gather.2 = f32[4,26,516]{2,1,0:T(8,128)S(1)} all-gather(f32[1,26,516]{2,1,0:T(8,128)S(1)} %bitcast.177), channel_id=2, replica_groups=mesh['tile'=128,'lev'=4] {'lev'}, dimensions={0}, use_global_device_ids=true | all-gather | bytes 268320 | tf_op jit(solution)/shard_map/all_gather | solution.py:95
  17.3 5.7 %collective-permute-start.1 = (f32[104,4]{1,0:T(8,128)S(1)}, f32[104,4]{1,0:T(8,128)S(1)}, u32[]{:S(2)}, u32[]{:S(2)}) collective-permute-start(f32[104,4]{1,0:T(8,128)S(1)} %slice.621), channel_id=1, source_target_pairs={{508,0},{448,4},{452,8},{456,12},{460,16},{464,20},{468,24},{472,2... | collective-permute-start | bytes 5000 | tf_op jit(solution)/shard_map/ppermute | solution.py:57
  23.0 2.6 %collective-permute-start = (f32[104,256]{1,0:T(8,128)S(1)}, f32[104,256]{1,0:T(8,128)S(1)}, u32[]{:S(2)}, u32[]{:S(2)}) collective-permute-start(f32[104,256]{1,0:T(8,128)S(1)} %slice_select_fusion.3), channel_id=1, source_target_pairs={{448,0},{452,4},{456,8},{460,12},{464,16},{468,20},{472,24},{476,2... | collective-permute-start | bytes 319496 | tf_op jit(solution)/shard_map/ppermute | solution.py:56
  26.4 4.9 %collective-permute-done = f32[104,256]{1,0:T(8,128)S(1)} collective-permute-done((f32[104,256]{1,0:T(8,128)S(1)}, f32[104,256]{1,0:T(8,128)S(1)}, u32[]{:S(2)}, u32[]{:S(2)}) %collective-permute-start) | collective-permute-done | bytes 106528 | tf_op jit(solution)/shard_map/ppermute | solution.py:56
  31.4 0.8 copy.279
  32.2 7.5 %all-to-all-start = ((f32[4,2,13,260]{3,1,2,0:T(2,128)}), f32[4,2,13,260]{3,1,2,0:T(2,128)S(1)}, u32[]{:S(2)}, u32[]{:S(2)}) async-start(f32[4,2,13,260]{3,1,2,0:T(2,128)} %copy.279), calls=%async_computation | async-start | bytes 319488 | tf_op jit(solution)/shard_map/all_to_all | solution.py:102
  61.5 1.1 maximum_maximum_fusion.1
  62.7 1.3 %fusion.9 = f32[26,48,128]{2,1,0:T(8,128)S(1)} fusion(f32[26,49,130]{2,1,0:T(8,128)S(1)} %get-tuple-element.10, f32[26,49,130]{2,1,0:T(8,128)S(1)} %get-tuple-element.9, f32[26,48,1]{2,1,0:T(8,128)S(1)} %copy.295, f32[26,48,128]{2,1,0:T(8,128)S(1)} %bitcast.140, f32[26,48,1]{2,1,0:T(8,128)S(1)} %copy.294, f32[26]{0:T(128)S(1)} %get-tuple-element.82, ...), kind=kLoop, calls=%fused_computation.31 | loop fusion | flops 2236416 | bytes 5146680 | tf_op jit(solution)/shard_map/mul | solution.py:41
  67.1 1.3 %pad_maximum_fusion.2 = f32[4,2,13,2145]{3,1,2,0:T(2,128)} fusion(f32[1,2,13,2145]{3,1,2,0:T(2,128)S(1)} %bitcast.152, f32[1,2,13,2145]{3,1,2,0:T(2,128)S(1)} %bitcast.153, f32[1,2,13,2145]{3,1,2,0:T(2,128)S(1)} %bitcast.154, f32[1,2,13,2145]{3,1,2,0:T(2,128)S(1)} %bitcast.155), kind=kLoop, calls=%fused_computation.10 | loop fusion | flops 669240 | bytes 1784640 | tf_op jit(solution)/shard_map/stack | solution.py:127
  68.5 3.7 %all-to-all-start.1 = ((f32[4,2,13,2145]{3,1,2,0:T(2,128)}), f32[4,2,13,2145]{3,1,2,0:T(2,128)S(1)}, u32[]{:S(2)}, u32[]{:S(2)}) async-start(f32[4,2,13,2145]{3,1,2,0:T(2,128)} %pad_maximum_fusion.2), calls=%async_computation.1 | async-start | bytes 1810432 | tf_op jit(solution)/shard_map/all_to_all | solution.py:127
  72.5 11.6 %all-to-all-done.1 = f32[4,2,13,2145]{3,1,2,0:T(2,128)S(1)} async-done(((f32[4,2,13,2145]{3,1,2,0:T(2,128)}), f32[4,2,13,2145]{3,1,2,0:T(2,128)S(1)}, u32[]{:S(2)}, u32[]{:S(2)}) %all-to-all-start.1) | async-done | bytes 892352 | tf_op jit(solution)/shard_map/all_to_all | solution.py:127
  85.6 1.0 convolution_bitcast_fusion.1
  86.6 1.0 convolution_bitcast_fusion
  88.6 1.9 %collective-permute-start.3 = (f32[104,4]{1,0:T(8,128)S(1)}, f32[104,4]{1,0:T(8,128)S(1)}, u32[]{:S(2)}, u32[]{:S(2)}) collective-permute-start(f32[104,4]{1,0:T(8,128)S(1)} %pad_maximum_fusion.9), channel_id=1, source_target_pairs={{508,0},{448,4},{452,8},{456,12},{460,16},{464,20},{468,24},{472,2... | collective-permute-start | bytes 5000 | tf_op jit(solution)/shard_map/ppermute | solution.py:57
  90.6 8.9 %collective-permute-start.2 = (f32[104,256]{1,0:T(8,128)S(1)}, f32[104,256]{1,0:T(8,128)S(1)}, u32[]{:S(2)}, u32[]{:S(2)}) collective-permute-start(f32[104,256]{1,0:T(8,128)S(1)} %fusion.20), channel_id=1, source_target_pairs={{448,0},{452,4},{456,8},{460,12},{464,16},{468,20},{472,24},{476,2... | collective-permute-start | bytes 319496 | tf_op jit(solution)/shard_map/ppermute | solution.py:56
  99.6 2.2 %collective-permute-done.2 = f32[104,256]{1,0:T(8,128)S(1)} collective-permute-done((f32[104,256]{1,0:T(8,128)S(1)}, f32[104,256]{1,0:T(8,128)S(1)}, u32[]{:S(2)}, u32[]{:S(2)}) %collective-permute-start.2) | collective-permute-done | bytes 106528 | tf_op jit(solution)/shard_map/ppermute | solution.py:56
  101.9 7.7 %all-gather.3 = f32[4,104,260]{1,2,0:T(8,128)S(1)} all-gather(f32[1,104,260]{1,2,0:T(8,128)S(1)} %copy.317), channel_id=3, replica_groups=mesh['tile'=128,'lev'=4] {'lev'}, dimensions={0}, use_global_device_ids=true | all-gather | bytes 540800 | tf_op jit(solution)/shard_map/all_gather | solution.py:170
  112.6 1.2 maximum_maximum_fusion
  113.8 1.4 %fusion.2 = f32[104,12,128]{2,1,0:T(8,128)S(1)} fusion(f32[104,14,129]{2,1,0:T(8,128)S(1)} %get-tuple-element.12, f32[104,14,129]{2,1,0:T(8,128)S(1)} %get-tuple-element.11, f32[104,1,128]{2,1,0:T(1,128)S(1)} %bitcast.160, f32[104,12,128]{2,1,0:T(8,128)S(1)} %slice.665, f32[104,1,128]{2,1,0:T(1,128)S(1)} %bitcast.158, f32[104]{0:T(128)S(1)} %get-tuple-element.80, ...), kind=kLoop, calls=%fused_computation.14 | loop fusion | flops 2236416 | bytes 5225696 | tf_op jit(solution)/shard_map/mul | solution.py:41
  118.1 11.6 %all_to_all.15 = f32[4,2,13,12,128]{4,1,3,2,0:T(2,128)S(1)} all-to-all(f32[4,2,13,12,128]{4,1,3,2,0:T(2,128)S(1)} %copy.332), channel_id=1, replica_groups=mesh['tile'=128,'lev'=4] {'lev'}, dimensions={0} | all-to-all | bytes 1277952 | tf_op jit(solution)/shard_map/all_to_all | solution.py:137
  129.8 0.9 copy.334
  (177 shorter events, 17.5 us)
Async XLA Ops:
  2.8 22.8 %copy-start.5 = (f32[13]{0:T(128)S(1)}, f32[13]{0:T(128)}, u32[]{:S(2)}) copy-start(f32[13]{0:T(128)} %param.7) | copy-start | bytes 160
  2.9 22.9 %copy-start.3 = (s32[48,128]{1,0:T(8,128)S(1)}, s32[48,128]{1,0:T(8,128)}, u32[]{:S(2)}) copy-start(s32[48,128]{1,0:T(8,128)} %param.9) | copy-start | bytes 73732
  2.9 22.9 %copy-start.1 = (f32[2,2,52,52]{3,1,2,0:T(2,128)S(1)}, f32[2,2,52,52]{3,1,2,0:T(2,128)}, u32[]{:S(2)}) copy-start(f32[2,2,52,52]{3,1,2,0:T(2,128)} %param.10) | copy-start | bytes 129796
  4.1 21.7 %copy-start.6 = (s32[1,8]{1,0:T(1,128)S(1)}, s32[1,8]{1,0:T(1,128)}, u32[]{:S(2)}) copy-start(s32[1,8]{1,0:T(1,128)} %param.11) | copy-start | bytes 100
  17.1 40.4 %copy-start.2 = (s32[48,128]{1,0:T(8,128)S(1)}, s32[48,128]{1,0:T(8,128)}, u32[]{:S(2)}) copy-start(s32[48,128]{1,0:T(8,128)} %param.8) | copy-start | bytes 73732
  17.3 9.2 %collective-permute-start.1 = (f32[104,4]{1,0:T(8,128)S(1)}, f32[104,4]{1,0:T(8,128)S(1)}, u32[]{:S(2)}, u32[]{:S(2)}) collective-permute-start(f32[104,4]{1,0:T(8,128)S(1)} %slice.621), channel_id=1, source_target_pairs={{508,0},{448,4},{452,8},{456,12},{460,16},{464,20},{468,24},{472,2... | collective-permute-start | bytes 5000 | tf_op jit(solution)/shard_map/ppermute | solution.py:57
  23.0 8.4 %collective-permute-start = (f32[104,256]{1,0:T(8,128)S(1)}, f32[104,256]{1,0:T(8,128)S(1)}, u32[]{:S(2)}, u32[]{:S(2)}) collective-permute-start(f32[104,256]{1,0:T(8,128)S(1)} %slice_select_fusion.3), channel_id=1, source_target_pairs={{448,0},{452,4},{456,8},{460,12},{464,16},{468,20},{472,24},{476,2... | collective-permute-start | bytes 319496 | tf_op jit(solution)/shard_map/ppermute | solution.py:56
  32.2 25.6 %all-to-all-start = ((f32[4,2,13,260]{3,1,2,0:T(2,128)}), f32[4,2,13,260]{3,1,2,0:T(2,128)S(1)}, u32[]{:S(2)}, u32[]{:S(2)}) async-start(f32[4,2,13,260]{3,1,2,0:T(2,128)} %copy.279), calls=%async_computation | async-start | bytes 319488 | tf_op jit(solution)/shard_map/all_to_all | solution.py:102
  58.3 3.2 %copy-start = (f32[2,13,48,128]{3,2,1,0:T(8,128)S(1)}, f32[2,13,48,128]{3,2,1,0:T(8,128)}, u32[]{:S(2)}) copy-start(f32[2,13,48,128]{3,2,1,0:T(8,128)} %param.6) | copy-start | bytes 1916932
  68.5 15.7 %all-to-all-start.1 = ((f32[4,2,13,2145]{3,1,2,0:T(2,128)}), f32[4,2,13,2145]{3,1,2,0:T(2,128)S(1)}, u32[]{:S(2)}, u32[]{:S(2)}) async-start(f32[4,2,13,2145]{3,1,2,0:T(2,128)} %pad_maximum_fusion.2), calls=%async_computation.1 | async-start | bytes 1810432 | tf_op jit(solution)/shard_map/all_to_all | solution.py:127
  87.7 0.7 copy-start.4
  88.6 11.0 %collective-permute-start.3 = (f32[104,4]{1,0:T(8,128)S(1)}, f32[104,4]{1,0:T(8,128)S(1)}, u32[]{:S(2)}, u32[]{:S(2)}) collective-permute-start(f32[104,4]{1,0:T(8,128)S(1)} %pad_maximum_fusion.9), channel_id=1, source_target_pairs={{508,0},{448,4},{452,8},{456,12},{460,16},{464,20},{468,24},{472,2... | collective-permute-start | bytes 5000 | tf_op jit(solution)/shard_map/ppermute | solution.py:57
  90.6 11.2 %collective-permute-start.2 = (f32[104,256]{1,0:T(8,128)S(1)}, f32[104,256]{1,0:T(8,128)S(1)}, u32[]{:S(2)}, u32[]{:S(2)}) collective-permute-start(f32[104,256]{1,0:T(8,128)S(1)} %fusion.20), channel_id=1, source_target_pairs={{448,0},{452,4},{456,8},{460,12},{464,16},{468,20},{472,24},{476,2... | collective-permute-start | bytes 319496 | tf_op jit(solution)/shard_map/ppermute | solution.py:56

commit v10 on v8

--- a/solution.py
+++ b/solution.py
@@ -159,24 +159,35 @@
 
     got_strips = lax.ppermute(strip_pair, both, lifted(lambda lev: lev))
     got_corners = lax.ppermute(corner_set, both, lifted(lambda lev: 4 + lev))
-    shared = lax.all_gather(jnp.concatenate([got_strips, got_corners], axis=-1), "lev")
 
     def strips(got, length):
         return jnp.stack([got[..., :length], got[..., length : 2 * length]], axis=-2)
 
+    code = codes[part]
+    picked_row = pick(strips(got_strips, cols), code)
+    picked_col = jnp.pad(pick(strips(got_strips, rows), code), ((0, 0), (0, cols - rows)))
+    corner_code = codes[4 + part]
+    picked_corner = jnp.where(
+        corner_code == 0,
+        got_corners[:, 0],
+        jnp.where(
+            corner_code == 1,
+            got_corners[:, 1],
+            jnp.where(corner_code == 2, got_corners[:, 2], got_corners[:, 3]),
+        ),
+    )
+    mine = jnp.concatenate(
+        [jnp.where(part < 2, picked_row, picked_col), picked_corner[:, None]], axis=-1
+    )
+    shared = lax.all_gather(mine, "lev")
+    south = shared[0, :, :cols]
+    north = shared[1, :, :cols]
+    west = shared[2, :, :rows]
+    east = shared[3, :, :rows]
+
     def corner(slot):
-        cell = shared[slot - 4, :, 2 * cols : 2 * cols + 4]
-        code = codes[slot]
-        return jnp.where(
-            code == 0,
-            cell[..., 0],
-            jnp.where(code == 1, cell[..., 1], jnp.where(code == 2, cell[..., 2], cell[..., 3])),
-        )
-
-    south = pick(strips(shared[0], cols), codes[0])
-    north = pick(strips(shared[1], cols), codes[1])
-    west = pick(strips(shared[2], rows), codes[2])
-    east = pick(strips(shared[3], rows), codes[3])
+        return shared[slot - 4, :, cols]
+
     west_full = jnp.concatenate([corner(4)[:, None], west, corner(6)[:, None]], axis=-1)
     east_full = jnp.concatenate([corner(5)[:, None], east, corner(7)[:, None]], axis=-1)
     west_part = lax.dynamic_slice_in_dim(west_full, part * part_rows, part_rows + 2, axis=1)

time: 125 us -> 128 us (1.024)
  between operations: 18.7 us -> 22.6 us
where the time goes in v10:
time: 128 us; the launch traced here: 127 us
  starting transfers between devices  42.9 us (34%)
  between operations  22.6 us (18%)
  waiting for transfers between devices  17.6 us (14%)
  blocking collectives  17.5 us (14%)
  local copies, waits for them, and re-layouts  14.9 us (12%)
  other arithmetic  8.28 us (6%)
  matrix products  3.35 us (3%)
    all_to_all x1, blocking collectives, to_levels(): returning = lax.all_to_all(outgoing, 'lev', 0, 0, tiled=True)  12.6 us
    all_to_all x1, waiting for transfers between devices, to_rows(): columns = lax.all_to_all(jnp.stack(outgoing), 'lev', 0, 0, tiled=True)  11.7 us
    ppermute x1, starting transfers between devices, horizontal(): from_north = lax.ppermute(upright, 'tile', slot_pairs(count, 1))  10.7 us
    ppermute x1, starting transfers between devices, horizontal(): from_east = lax.ppermute(side, 'tile', slot_pairs(count, 3))  9.2 us
    ppermute x1, starting transfers between devices, horizontal_rows(): got_strips = lax.ppermute(strip_pair, both, lifted(lambda lev: lev))  6.96 us
    ppermute x1, starting transfers between devices, horizontal_rows(): got_corners = lax.ppermute(corner_set, both, lifted(lambda lev: 4 + lev))  6.33 us
    all_to_all x1, starting transfers between devices, to_rows(): columns = lax.all_to_all(jnp.stack(outgoing), 'lev', 0, 0, tiled=True)  5.85 us
    all_gather x1, blocking collectives, horizontal_rows(): shared = lax.all_gather(mine, 'lev')  4.86 us
  transfers between devices with their start and end apart: 7, of which 3 were waited for; matrix products, arithmetic and copies ran while one was open for 2% of the time, Pallas kernels for 0%

profile of v10, /device:TPU:1, one launch (start us, length us, event | category | flops | bytes accessed | tf_op | source)
XLA Modules:
  0.0 127.1 jit_solution(1501263731800375963)
XLA Ops:
  0.0 1.2 fusion.46
  1.2 1.6 %fusion.47 = (f32[26,48,1]{2,1,0:T(8,128)S(1)}, f32[26,48,1]{2,1,0:T(8,128)S(1)}) fusion(f32[26,48,128]{2,1,0:T(8,128)} %bitcast.128), kind=kLoop, calls=%fused_computation.140 | loop fusion | bytes 19968 | tf_op jit(solution)/shard_map/slice | solution.py:49
  3.5 9.2 %collective-permute-start.1 = (f32[26,100]{1,0:T(8,128)S(1)}, f32[26,100]{1,0:T(8,128)S(1)}, u32[]{:S(2)}, u32[]{:S(2)}) collective-permute-start(f32[26,100]{1,0:T(8,128)S(1)} %concatenate.86), channel_id=1, source_target_pairs={{4,0},{8,4},{12,8},{16,12},{20,16},{24,20},{28,24},{32,28},{36,32}... | collective-permute-start | bytes 31208 | tf_op jit(solution)/shard_map/ppermute | solution.py:51
  12.8 1.9 %collective-permute-start = (f32[26,100]{1,0:T(8,128)S(1)}, f32[26,100]{1,0:T(8,128)S(1)}, u32[]{:S(2)}, u32[]{:S(2)}) collective-permute-start(f32[26,100]{1,0:T(8,128)S(1)} %concatenate.86), channel_id=1, source_target_pairs={{60,0},{0,4},{4,8},{8,12},{12,16},{16,20},{20,24},{24,28},{28,32},... | collective-permute-start | bytes 31208 | tf_op jit(solution)/shard_map/ppermute | solution.py:50
  37.9 10.7 %collective-permute-start.3 = (f32[26,264]{1,0:T(8,128)S(1)}, f32[26,264]{1,0:T(8,128)S(1)}, u32[]{:S(2)}, u32[]{:S(2)}) collective-permute-start(f32[26,264]{1,0:T(8,128)S(1)} %pad_maximum_fusion.9), channel_id=1, source_target_pairs={{64,0},{68,4},{72,8},{76,12},{80,16},{84,20},{88,24},{92,28},{96,3... | collective-permute-start | bytes 82376 | tf_op jit(solution)/shard_map/ppermute | solution.py:59
  48.5 1.9 %collective-permute-start.2 = (f32[26,264]{1,0:T(8,128)S(1)}, f32[26,264]{1,0:T(8,128)S(1)}, u32[]{:S(2)}, u32[]{:S(2)}) collective-permute-start(f32[26,264]{1,0:T(8,128)S(1)} %pad_maximum_fusion.9), channel_id=1, source_target_pairs={{448,0},{452,4},{456,8},{460,12},{464,16},{468,20},{472,24},{476,2... | collective-permute-start | bytes 82376 | tf_op jit(solution)/shard_map/ppermute | solution.py:58
  51.8 3.7 %collective-permute-done.2 = f32[26,264]{1,0:T(8,128)S(1)} collective-permute-done((f32[26,264]{1,0:T(8,128)S(1)}, f32[26,264]{1,0:T(8,128)S(1)}, u32[]{:S(2)}, u32[]{:S(2)}) %collective-permute-start.2) | collective-permute-done | bytes 27488 | tf_op jit(solution)/shard_map/ppermute | solution.py:58
  55.9 1.1 maximum_maximum_fusion.1
  57.0 1.3 %fusion.9 = f32[26,48,128]{2,1,0:T(8,128)S(1)} fusion(f32[26,49,130]{2,1,0:T(8,128)S(1)} %get-tuple-element.8, f32[26,49,130]{2,1,0:T(8,128)S(1)} %get-tuple-element.7, f32[26,48,1]{2,1,0:T(8,128)S(1)} %copy.194, f32[26,48,128]{2,1,0:T(8,128)S(1)} %bitcast.131, f32[26,48,1]{2,1,0:T(8,128)S(1)} %copy.193, f32[26]{0:T(128)S(1)} %get-tuple-element.72, ...), kind=kLoop, calls=%fused_computation.31 | loop fusion | flops 2236416 | bytes 5146680 | tf_op jit(solution)/shard_map/mul | solution.py:41
  61.5 1.3 %pad_maximum_fusion.2 = f32[4,2,13,2145]{3,1,2,0:T(2,128)} fusion(f32[1,2,13,2145]{3,1,2,0:T(2,128)S(1)} %bitcast.140, f32[1,2,13,2145]{3,1,2,0:T(2,128)S(1)} %bitcast.141, f32[1,2,13,2145]{3,1,2,0:T(2,128)S(1)} %bitcast.142, f32[1,2,13,2145]{3,1,2,0:T(2,128)S(1)} %bitcast.143), kind=kLoop, calls=%fused_computation.10 | loop fusion | flops 669240 | bytes 1784640 | tf_op jit(solution)/shard_map/stack | solution.py:108
  62.8 5.9 %all-to-all-start = ((f32[4,2,13,2145]{3,1,2,0:T(2,128)}), f32[4,2,13,2145]{3,1,2,0:T(2,128)S(1)}, u32[]{:S(2)}, u32[]{:S(2)}) async-start(f32[4,2,13,2145]{3,1,2,0:T(2,128)} %pad_maximum_fusion.2), calls=%async_computation | async-start | bytes 1810432 | tf_op jit(solution)/shard_map/all_to_all | solution.py:108
  69.0 11.7 %all-to-all-done = f32[4,2,13,2145]{3,1,2,0:T(2,128)S(1)} async-done(((f32[4,2,13,2145]{3,1,2,0:T(2,128)}), f32[4,2,13,2145]{3,1,2,0:T(2,128)S(1)}, u32[]{:S(2)}, u32[]{:S(2)}) %all-to-all-start) | async-done | bytes 892352 | tf_op jit(solution)/shard_map/all_to_all | solution.py:108
  80.7 0.8 slice_reduce_fusion
  82.2 1.0 convolution_bitcast_fusion.1
  83.2 1.0 convolution_bitcast_fusion
  84.8 6.3 %collective-permute-start.5 = (f32[104,4]{1,0:T(8,128)S(1)}, f32[104,4]{1,0:T(8,128)S(1)}, u32[]{:S(2)}, u32[]{:S(2)}) collective-permute-start(f32[104,4]{1,0:T(8,128)S(1)} %pad_maximum_fusion.8), channel_id=1, source_target_pairs={{508,0},{448,4},{452,8},{456,12},{460,16},{464,20},{468,24},{472,2... | collective-permute-start | bytes 5000 | tf_op jit(solution)/shard_map/ppermute | solution.py:161
  91.4 7.0 %collective-permute-start.4 = (f32[104,256]{1,0:T(8,128)S(1)}, f32[104,256]{1,0:T(8,128)S(1)}, u32[]{:S(2)}, u32[]{:S(2)}) collective-permute-start(f32[104,256]{1,0:T(8,128)S(1)} %fusion.20), channel_id=1, source_target_pairs={{448,0},{452,4},{456,8},{460,12},{464,16},{468,20},{472,24},{476,2... | collective-permute-start | bytes 319496 | tf_op jit(solution)/shard_map/ppermute | solution.py:160
  98.6 2.2 %collective-permute-done.4 = f32[104,256]{1,0:T(8,128)S(1)} collective-permute-done((f32[104,256]{1,0:T(8,128)S(1)}, f32[104,256]{1,0:T(8,128)S(1)}, u32[]{:S(2)}, u32[]{:S(2)}) %collective-permute-start.4) | collective-permute-done | bytes 106528 | tf_op jit(solution)/shard_map/ppermute | solution.py:160
  101.3 4.9 %all-gather.1 = f32[4,104,129]{1,2,0:T(8,128)S(1)} all-gather(f32[1,104,129]{1,2,0:T(8,128)S(1)} %copy.206), channel_id=2, replica_groups=mesh['tile'=128,'lev'=4] {'lev'}, dimensions={0}, use_global_device_ids=true | all-gather | bytes 268320 | tf_op jit(solution)/shard_map/all_gather | solution.py:182
  106.3 0.7 copy.229
  108.1 1.2 maximum_maximum_fusion
  109.3 1.4 %fusion.2 = f32[104,12,128]{2,1,0:T(8,128)S(1)} fusion(f32[104,14,129]{2,1,0:T(8,128)S(1)} %get-tuple-element.10, f32[104,14,129]{2,1,0:T(8,128)S(1)} %get-tuple-element.9, f32[104,1,128]{2,1,0:T(1,128)S(1)} %get-tuple-element.16, f32[104,12,128]{2,1,0:T(8,128)S(1)} %slice.568, f32[104,1,128]{2,1,0:T(1,128)S(1)} %get-tuple-element.15, ...), kind=kLoop, calls=%fused_computation.14 | loop fusion | flops 2236416 | bytes 5225696 | tf_op jit(solution)/shard_map/mul | solution.py:41
  113.6 12.6 %all_to_all.10 = f32[4,2,13,12,128]{4,1,3,2,0:T(2,128)S(1)} all-to-all(f32[4,2,13,12,128]{4,1,3,2,0:T(2,128)S(1)} %copy.211), channel_id=1, replica_groups=mesh['tile'=128,'lev'=4] {'lev'}, dimensions={0} | all-to-all | bytes 1277952 | tf_op jit(solution)/shard_map/all_to_all | solution.py:118
  126.3 0.9 copy.213
  (133 shorter events, 13.1 us)
Async XLA Ops:
  1.2 13.5 %copy-start = (f32[2,13,48,128]{3,2,1,0:T(8,128)S(1)}, f32[2,13,48,128]{3,2,1,0:T(8,128)}, u32[]{:S(2)}) copy-start(f32[2,13,48,128]{3,2,1,0:T(8,128)} %param.6) | copy-start | bytes 1916932
  1.2 13.5 %copy-start.6 = (s32[1,8]{1,0:T(1,128)S(1)}, s32[1,8]{1,0:T(1,128)}, u32[]{:S(2)}) copy-start(s32[1,8]{1,0:T(1,128)} %param.11) | copy-start | bytes 100
  1.2 13.6 %copy-start.5 = (f32[13]{0:T(128)S(1)}, f32[13]{0:T(128)}, u32[]{:S(2)}) copy-start(f32[13]{0:T(128)} %param.7) | copy-start | bytes 160
  1.2 13.7 %copy-start.3 = (s32[48,128]{1,0:T(8,128)S(1)}, s32[48,128]{1,0:T(8,128)}, u32[]{:S(2)}) copy-start(s32[48,128]{1,0:T(8,128)} %param.9) | copy-start | bytes 73732
  1.2 13.7 %copy-start.1 = (f32[2,2,52,52]{3,1,2,0:T(2,128)S(1)}, f32[2,2,52,52]{3,1,2,0:T(2,128)}, u32[]{:S(2)}) copy-start(f32[2,2,52,52]{3,1,2,0:T(2,128)} %param.10) | copy-start | bytes 129796
  2.8 34.6 %copy-start.2 = (s32[48,128]{1,0:T(8,128)S(1)}, s32[48,128]{1,0:T(8,128)}, u32[]{:S(2)}) copy-start(s32[48,128]{1,0:T(8,128)} %param.8) | copy-start | bytes 73732
  3.5 34.1 %collective-permute-start.1 = (f32[26,100]{1,0:T(8,128)S(1)}, f32[26,100]{1,0:T(8,128)S(1)}, u32[]{:S(2)}, u32[]{:S(2)}) collective-permute-start(f32[26,100]{1,0:T(8,128)S(1)} %concatenate.86), channel_id=1, source_target_pairs={{4,0},{8,4},{12,8},{16,12},{20,16},{24,20},{28,24},{32,28},{36,32}... | collective-permute-start | bytes 31208 | tf_op jit(solution)/shard_map/ppermute | solution.py:51
  12.8 25.0 %collective-permute-start = (f32[26,100]{1,0:T(8,128)S(1)}, f32[26,100]{1,0:T(8,128)S(1)}, u32[]{:S(2)}, u32[]{:S(2)}) collective-permute-start(f32[26,100]{1,0:T(8,128)S(1)} %concatenate.86), channel_id=1, source_target_pairs={{60,0},{0,4},{4,8},{8,12},{12,16},{16,20},{20,24},{24,28},{28,32},... | collective-permute-start | bytes 31208 | tf_op jit(solution)/shard_map/ppermute | solution.py:50
  37.9 13.6 %collective-permute-start.3 = (f32[26,264]{1,0:T(8,128)S(1)}, f32[26,264]{1,0:T(8,128)S(1)}, u32[]{:S(2)}, u32[]{:S(2)}) collective-permute-start(f32[26,264]{1,0:T(8,128)S(1)} %pad_maximum_fusion.9), channel_id=1, source_target_pairs={{64,0},{68,4},{72,8},{76,12},{80,16},{84,20},{88,24},{92,28},{96,3... | collective-permute-start | bytes 82376 | tf_op jit(solution)/shard_map/ppermute | solution.py:59
  48.5 7.0 %collective-permute-start.2 = (f32[26,264]{1,0:T(8,128)S(1)}, f32[26,264]{1,0:T(8,128)S(1)}, u32[]{:S(2)}, u32[]{:S(2)}) collective-permute-start(f32[26,264]{1,0:T(8,128)S(1)} %pad_maximum_fusion.9), channel_id=1, source_target_pairs={{448,0},{452,4},{456,8},{460,12},{464,16},{468,20},{472,24},{476,2... | collective-permute-start | bytes 82376 | tf_op jit(solution)/shard_map/ppermute | solution.py:58
  62.8 17.9 %all-to-all-start = ((f32[4,2,13,2145]{3,1,2,0:T(2,128)}), f32[4,2,13,2145]{3,1,2,0:T(2,128)S(1)}, u32[]{:S(2)}, u32[]{:S(2)}) async-start(f32[4,2,13,2145]{3,1,2,0:T(2,128)} %pad_maximum_fusion.2), calls=%async_computation | async-start | bytes 1810432 | tf_op jit(solution)/shard_map/all_to_all | solution.py:108
  84.3 6.8 %copy-start.4 = (pred[256]{0:T(512)(128)(4,1)S(1)}, pred[256]{0:T(512)(128)(4,1)}, u32[]{:S(2)}) copy-start(pred[256]{0:T(512)(128)(4,1)} %constant.137.clone.1) | copy-start | bytes 772
  84.8 13.7 %collective-permute-start.5 = (f32[104,4]{1,0:T(8,128)S(1)}, f32[104,4]{1,0:T(8,128)S(1)}, u32[]{:S(2)}, u32[]{:S(2)}) collective-permute-start(f32[104,4]{1,0:T(8,128)S(1)} %pad_maximum_fusion.8), channel_id=1, source_target_pairs={{508,0},{448,4},{452,8},{456,12},{460,16},{464,20},{468,24},{472,2... | collective-permute-start | bytes 5000 | tf_op jit(solution)/shard_map/ppermute | solution.py:161
  91.4 9.4 %collective-permute-start.4 = (f32[104,256]{1,0:T(8,128)S(1)}, f32[104,256]{1,0:T(8,128)S(1)}, u32[]{:S(2)}, u32[]{:S(2)}) collective-permute-start(f32[104,256]{1,0:T(8,128)S(1)} %fusion.20), channel_id=1, source_target_pairs={{448,0},{452,4},{456,8},{460,12},{464,16},{468,20},{472,24},{476,2... | collective-permute-start | bytes 319496 | tf_op jit(solution)/shard_map/ppermute | solution.py:160

commit v11 on v8

--- a/solution.py
+++ b/solution.py
@@ -96,7 +96,7 @@
     padded = jnp.pad(lateral, ((0, 0), (0, 0), (1, 1), (0, 0)))
     rate_column = jnp.broadcast_to(rate[None, :, None], (tracers, depth, 1))
     edges = jnp.concatenate(
-        [lateral[..., :, 0], lateral[..., :, -1], lateral[..., 0, :], lateral[..., -1, :], rate_column],
+        [lateral[..., 0, :], lateral[..., -1, :], lateral[..., :, 0], lateral[..., :, -1], rate_column],
         axis=-1,
     )
     outgoing = []
@@ -138,10 +138,10 @@
     part_rows = halo_rows - 2
     rows = parts * part_rows
     block = halo_block[:, 1:-1, :]
-    first_col = edges[:, :rows]
-    last_col = edges[:, rows : 2 * rows]
-    first_row = edges[:, 2 * rows : 2 * rows + cols]
-    last_row = edges[:, 2 * rows + cols :]
+    first_row = edges[:, :cols]
+    last_row = edges[:, cols : 2 * cols]
+    first_col = edges[:, 2 * cols : 2 * cols + rows]
+    last_col = edges[:, 2 * cols + rows :]
     corner_set = jnp.stack(
         [first_row[:, 0], first_row[:, -1], last_row[:, 0], last_row[:, -1]], axis=-1
     )
@@ -204,10 +204,10 @@
     first_map = jnp.concatenate(
         [
             halo_convective.reshape(-1),
+            is_convective[0, :],
+            is_convective[-1, :],
             is_convective[:, 0],
             is_convective[:, -1],
-            is_convective[0, :],
-            is_convective[-1, :],
         ]
     )
     convective_rows = lax.dynamic_slice_in_dim(

time: 125 us -> 125 us (level)
  no operation moved by 1% of the time
where the time goes in v11:
time: 125 us; the launch traced here: 124 us
  starting transfers between devices  42.9 us (34%)
  between operations  18.3 us (15%)
  blocking collectives  18.2 us (15%)
  waiting for transfers between devices  17.7 us (14%)
  local copies, waits for them, and re-layouts  15.1 us (12%)
  other arithmetic  8.54 us (7%)
  matrix products  3.35 us (3%)
    all_to_all x1, blocking collectives, to_levels(): returning = lax.all_to_all(outgoing, 'lev', 0, 0, tiled=True)  12.6 us
    all_to_all x1, waiting for transfers between devices, to_rows(): columns = lax.all_to_all(jnp.stack(outgoing), 'lev', 0, 0, tiled=True)  11.7 us
    ppermute x1, starting transfers between devices, horizontal(): from_north = lax.ppermute(upright, 'tile', slot_pairs(count, 1))  10.7 us
    ppermute x1, starting transfers between devices, horizontal(): from_east = lax.ppermute(side, 'tile', slot_pairs(count, 3))  9.2 us
    ppermute x1, starting transfers between devices, horizontal_rows(): got_strips = lax.ppermute(strip_pair, both, lifted(lambda lev: lev))  6.96 us
    ppermute x1, starting transfers between devices, horizontal_rows(): got_corners = lax.ppermute(corner_set, both, lifted(lambda lev: 4 + lev))  6.33 us
    all_to_all x1, starting transfers between devices, to_rows(): columns = lax.all_to_all(jnp.stack(outgoing), 'lev', 0, 0, tiled=True)  5.85 us
    all_gather x1, blocking collectives, horizontal_rows(): lax.all_gather(jnp.concatenate([got_strips, got_corners], axis=-1), 'lev')  5.59 us
  transfers between devices with their start and end apart: 7, of which 3 were waited for; matrix products, arithmetic and copies ran while one was open for 2% of the time, Pallas kernels for 0%

profile of v11, /device:TPU:1, one launch (start us, length us, event | category | flops | bytes accessed | tf_op | source)
XLA Modules:
  0.0 124.0 jit_solution(12947577643745291063)
XLA Ops:
  0.0 1.2 fusion.48
  1.2 1.6 %fusion.49 = (f32[26,48,1]{2,1,0:T(8,128)S(1)}, f32[26,48,1]{2,1,0:T(8,128)S(1)}) fusion(f32[26,48,128]{2,1,0:T(8,128)} %bitcast.131), kind=kLoop, calls=%fused_computation.143 | loop fusion | bytes 19968 | tf_op jit(solution)/shard_map/slice | solution.py:49
  3.5 9.2 %collective-permute-start.1 = (f32[26,100]{1,0:T(8,128)S(1)}, f32[26,100]{1,0:T(8,128)S(1)}, u32[]{:S(2)}, u32[]{:S(2)}) collective-permute-start(f32[26,100]{1,0:T(8,128)S(1)} %concatenate.88), channel_id=1, source_target_pairs={{4,0},{8,4},{12,8},{16,12},{20,16},{24,20},{28,24},{32,28},{36,32}... | collective-permute-start | bytes 31208 | tf_op jit(solution)/shard_map/ppermute | solution.py:51
  12.8 1.9 %collective-permute-start = (f32[26,100]{1,0:T(8,128)S(1)}, f32[26,100]{1,0:T(8,128)S(1)}, u32[]{:S(2)}, u32[]{:S(2)}) collective-permute-start(f32[26,100]{1,0:T(8,128)S(1)} %concatenate.88), channel_id=1, source_target_pairs={{60,0},{0,4},{4,8},{8,12},{12,16},{16,20},{20,24},{24,28},{28,32},... | collective-permute-start | bytes 31208 | tf_op jit(solution)/shard_map/ppermute | solution.py:50
  33.5 10.7 %collective-permute-start.3 = (f32[26,264]{1,0:T(8,128)S(1)}, f32[26,264]{1,0:T(8,128)S(1)}, u32[]{:S(2)}, u32[]{:S(2)}) collective-permute-start(f32[26,264]{1,0:T(8,128)S(1)} %pad_maximum_fusion.9), channel_id=1, source_target_pairs={{64,0},{68,4},{72,8},{76,12},{80,16},{84,20},{88,24},{92,28},{96,3... | collective-permute-start | bytes 82376 | tf_op jit(solution)/shard_map/ppermute | solution.py:59
  44.2 1.9 %collective-permute-start.2 = (f32[26,264]{1,0:T(8,128)S(1)}, f32[26,264]{1,0:T(8,128)S(1)}, u32[]{:S(2)}, u32[]{:S(2)}) collective-permute-start(f32[26,264]{1,0:T(8,128)S(1)} %pad_maximum_fusion.9), channel_id=1, source_target_pairs={{448,0},{452,4},{456,8},{460,12},{464,16},{468,20},{472,24},{476,2... | collective-permute-start | bytes 82376 | tf_op jit(solution)/shard_map/ppermute | solution.py:58
  47.5 3.7 %collective-permute-done.2 = f32[26,264]{1,0:T(8,128)S(1)} collective-permute-done((f32[26,264]{1,0:T(8,128)S(1)}, f32[26,264]{1,0:T(8,128)S(1)}, u32[]{:S(2)}, u32[]{:S(2)}) %collective-permute-start.2) | collective-permute-done | bytes 27488 | tf_op jit(solution)/shard_map/ppermute | solution.py:58
  51.5 1.1 maximum_maximum_fusion.1
  52.7 1.3 %fusion.9 = f32[26,48,128]{2,1,0:T(8,128)S(1)} fusion(f32[26,49,130]{2,1,0:T(8,128)S(1)} %get-tuple-element.8, f32[26,49,130]{2,1,0:T(8,128)S(1)} %get-tuple-element.7, f32[26,48,1]{2,1,0:T(8,128)S(1)} %copy.192, f32[26,48,128]{2,1,0:T(8,128)S(1)} %bitcast.134, f32[26,48,1]{2,1,0:T(8,128)S(1)} %copy.191, f32[26]{0:T(128)S(1)} %get-tuple-element.62, ...), kind=kLoop, calls=%fused_computation.31 | loop fusion | flops 2236416 | bytes 5146680 | tf_op jit(solution)/shard_map/mul | solution.py:41
  57.0 1.4 %pad_maximum_fusion.2 = f32[4,2,13,2145]{3,1,2,0:T(2,128)} fusion(f32[1,2,13,2145]{3,1,2,0:T(2,128)S(1)} %bitcast.145, f32[1,2,13,2145]{3,1,2,0:T(2,128)S(1)} %bitcast.146, f32[1,2,13,2145]{3,1,2,0:T(2,128)S(1)} %bitcast.147, f32[1,2,13,2145]{3,1,2,0:T(2,128)S(1)} %bitcast.148), kind=kLoop, calls=%fused_computation.10 | loop fusion | flops 669240 | bytes 1784640 | tf_op jit(solution)/shard_map/stack | solution.py:108
  58.4 5.9 %all-to-all-start = ((f32[4,2,13,2145]{3,1,2,0:T(2,128)}), f32[4,2,13,2145]{3,1,2,0:T(2,128)S(1)}, u32[]{:S(2)}, u32[]{:S(2)}) async-start(f32[4,2,13,2145]{3,1,2,0:T(2,128)} %pad_maximum_fusion.2), calls=%async_computation | async-start | bytes 1810432 | tf_op jit(solution)/shard_map/all_to_all | solution.py:108
  64.6 11.7 %all-to-all-done = f32[4,2,13,2145]{3,1,2,0:T(2,128)S(1)} async-done(((f32[4,2,13,2145]{3,1,2,0:T(2,128)}), f32[4,2,13,2145]{3,1,2,0:T(2,128)S(1)}, u32[]{:S(2)}, u32[]{:S(2)}) %all-to-all-start) | async-done | bytes 892352 | tf_op jit(solution)/shard_map/all_to_all | solution.py:108
  76.3 0.8 slice_reduce_fusion
  77.8 1.0 convolution_bitcast_fusion.1
  78.8 1.0 convolution_bitcast_fusion
  80.5 6.3 %collective-permute-start.5 = (f32[104,4]{1,0:T(8,128)S(1)}, f32[104,4]{1,0:T(8,128)S(1)}, u32[]{:S(2)}, u32[]{:S(2)}) collective-permute-start(f32[104,4]{1,0:T(8,128)S(1)} %pad_maximum_fusion.8), channel_id=1, source_target_pairs={{508,0},{448,4},{452,8},{456,12},{460,16},{464,20},{468,24},{472,2... | collective-permute-start | bytes 5000 | tf_op jit(solution)/shard_map/ppermute | solution.py:161
  87.0 7.0 %collective-permute-start.4 = (f32[104,256]{1,0:T(8,128)S(1)}, f32[104,256]{1,0:T(8,128)S(1)}, u32[]{:S(2)}, u32[]{:S(2)}) collective-permute-start(f32[104,256]{1,0:T(8,128)S(1)} %slice_select_fusion.2), channel_id=1, source_target_pairs={{448,0},{452,4},{456,8},{460,12},{464,16},{468,20},{472,24},{476,2... | collective-permute-start | bytes 319496 | tf_op jit(solution)/shard_map/ppermute | solution.py:160
  94.0 2.3 %collective-permute-done.4 = f32[104,256]{1,0:T(8,128)S(1)} collective-permute-done((f32[104,256]{1,0:T(8,128)S(1)}, f32[104,256]{1,0:T(8,128)S(1)}, u32[]{:S(2)}, u32[]{:S(2)}) %collective-permute-start.4) | collective-permute-done | bytes 106528 | tf_op jit(solution)/shard_map/ppermute | solution.py:160
  96.4 5.6 %all-gather.1 = f32[4,104,260]{1,2,0:T(8,128)S(1)} all-gather(f32[1,104,260]{1,2,0:T(8,128)S(1)} %copy.204), channel_id=2, replica_groups=mesh['tile'=128,'lev'=4] {'lev'}, dimensions={0}, use_global_device_ids=true | all-gather | bytes 540800 | tf_op jit(solution)/shard_map/all_gather | solution.py:162
  103.4 0.7 copy.214
  105.0 1.2 maximum_maximum_fusion
  106.2 1.4 %fusion.2 = f32[104,12,128]{2,1,0:T(8,128)S(1)} fusion(f32[104,14,129]{2,1,0:T(8,128)S(1)} %get-tuple-element.10, f32[104,14,129]{2,1,0:T(8,128)S(1)} %get-tuple-element.9, f32[104,1,128]{2,1,0:T(1,128)S(1)} %bitcast.152, f32[104,12,128]{2,1,0:T(8,128)S(1)} %slice.648, f32[104,1,128]{2,1,0:T(1,128)S(1)} %bitcast.150, f32[104]{0:T(128)S(1)} %get-tuple-element.60, ...), kind=kLoop, calls=%fused_computation.14 | loop fusion | flops 2236416 | bytes 5225696 | tf_op jit(solution)/shard_map/mul | solution.py:41
  110.5 12.6 %all_to_all.10 = f32[4,2,13,12,128]{4,1,3,2,0:T(2,128)S(1)} all-to-all(f32[4,2,13,12,128]{4,1,3,2,0:T(2,128)S(1)} %copy.219), channel_id=1, replica_groups=mesh['tile'=128,'lev'=4] {'lev'}, dimensions={0} | all-to-all | bytes 1277952 | tf_op jit(solution)/shard_map/all_to_all | solution.py:118
  123.2 0.9 copy.221
  (136 shorter events, 13.5 us)
Async XLA Ops:
  1.2 13.5 %copy-start = (f32[2,13,48,128]{3,2,1,0:T(8,128)S(1)}, f32[2,13,48,128]{3,2,1,0:T(8,128)}, u32[]{:S(2)}) copy-start(f32[2,13,48,128]{3,2,1,0:T(8,128)} %param.6) | copy-start | bytes 1916932
  1.2 13.5 %copy-start.5 = (s32[1,8]{1,0:T(1,128)S(1)}, s32[1,8]{1,0:T(1,128)}, u32[]{:S(2)}) copy-start(s32[1,8]{1,0:T(1,128)} %param.11) | copy-start | bytes 100
  1.2 13.5 %copy-start.4 = (f32[13]{0:T(128)S(1)}, f32[13]{0:T(128)}, u32[]{:S(2)}) copy-start(f32[13]{0:T(128)} %param.7) | copy-start | bytes 160
  1.2 13.6 %copy-start.3 = (s32[48,128]{1,0:T(8,128)S(1)}, s32[48,128]{1,0:T(8,128)}, u32[]{:S(2)}) copy-start(s32[48,128]{1,0:T(8,128)} %param.9) | copy-start | bytes 73732
  1.2 13.6 %copy-start.1 = (f32[2,2,52,52]{3,1,2,0:T(2,128)S(1)}, f32[2,2,52,52]{3,1,2,0:T(2,128)}, u32[]{:S(2)}) copy-start(f32[2,2,52,52]{3,1,2,0:T(2,128)} %param.10) | copy-start | bytes 129796
  2.8 30.3 %copy-start.2 = (s32[48,128]{1,0:T(8,128)S(1)}, s32[48,128]{1,0:T(8,128)}, u32[]{:S(2)}) copy-start(s32[48,128]{1,0:T(8,128)} %param.8) | copy-start | bytes 73732
  3.5 29.8 %collective-permute-start.1 = (f32[26,100]{1,0:T(8,128)S(1)}, f32[26,100]{1,0:T(8,128)S(1)}, u32[]{:S(2)}, u32[]{:S(2)}) collective-permute-start(f32[26,100]{1,0:T(8,128)S(1)} %concatenate.88), channel_id=1, source_target_pairs={{4,0},{8,4},{12,8},{16,12},{20,16},{24,20},{28,24},{32,28},{36,32}... | collective-permute-start | bytes 31208 | tf_op jit(solution)/shard_map/ppermute | solution.py:51
  12.8 20.6 %collective-permute-start = (f32[26,100]{1,0:T(8,128)S(1)}, f32[26,100]{1,0:T(8,128)S(1)}, u32[]{:S(2)}, u32[]{:S(2)}) collective-permute-start(f32[26,100]{1,0:T(8,128)S(1)} %concatenate.88), channel_id=1, source_target_pairs={{60,0},{0,4},{4,8},{8,12},{12,16},{16,20},{20,24},{24,28},{28,32},... | collective-permute-start | bytes 31208 | tf_op jit(solution)/shard_map/ppermute | solution.py:50
  33.5 13.6 %collective-permute-start.3 = (f32[26,264]{1,0:T(8,128)S(1)}, f32[26,264]{1,0:T(8,128)S(1)}, u32[]{:S(2)}, u32[]{:S(2)}) collective-permute-start(f32[26,264]{1,0:T(8,128)S(1)} %pad_maximum_fusion.9), channel_id=1, source_target_pairs={{64,0},{68,4},{72,8},{76,12},{80,16},{84,20},{88,24},{92,28},{96,3... | collective-permute-start | bytes 82376 | tf_op jit(solution)/shard_map/ppermute | solution.py:59
  44.2 7.0 %collective-permute-start.2 = (f32[26,264]{1,0:T(8,128)S(1)}, f32[26,264]{1,0:T(8,128)S(1)}, u32[]{:S(2)}, u32[]{:S(2)}) collective-permute-start(f32[26,264]{1,0:T(8,128)S(1)} %pad_maximum_fusion.9), channel_id=1, source_target_pairs={{448,0},{452,4},{456,8},{460,12},{464,16},{468,20},{472,24},{476,2... | collective-permute-start | bytes 82376 | tf_op jit(solution)/shard_map/ppermute | solution.py:58
  58.4 17.9 %all-to-all-start = ((f32[4,2,13,2145]{3,1,2,0:T(2,128)}), f32[4,2,13,2145]{3,1,2,0:T(2,128)S(1)}, u32[]{:S(2)}, u32[]{:S(2)}) async-start(f32[4,2,13,2145]{3,1,2,0:T(2,128)} %pad_maximum_fusion.2), calls=%async_computation | async-start | bytes 1810432 | tf_op jit(solution)/shard_map/all_to_all | solution.py:108
  80.5 13.5 %collective-permute-start.5 = (f32[104,4]{1,0:T(8,128)S(1)}, f32[104,4]{1,0:T(8,128)S(1)}, u32[]{:S(2)}, u32[]{:S(2)}) collective-permute-start(f32[104,4]{1,0:T(8,128)S(1)} %pad_maximum_fusion.8), channel_id=1, source_target_pairs={{508,0},{448,4},{452,8},{456,12},{460,16},{464,20},{468,24},{472,2... | collective-permute-start | bytes 5000 | tf_op jit(solution)/shard_map/ppermute | solution.py:161
  87.0 9.4 %collective-permute-start.4 = (f32[104,256]{1,0:T(8,128)S(1)}, f32[104,256]{1,0:T(8,128)S(1)}, u32[]{:S(2)}, u32[]{:S(2)}) collective-permute-start(f32[104,256]{1,0:T(8,128)S(1)} %slice_select_fusion.2), channel_id=1, source_target_pairs={{448,0},{452,4},{456,8},{460,12},{464,16},{468,20},{472,24},{476,2... | collective-permute-start | bytes 319496 | tf_op jit(solution)/shard_map/ppermute | solution.py:160

commit v12 on v11

--- a/solution.py
+++ b/solution.py
@@ -145,9 +145,6 @@
     corner_set = jnp.stack(
         [first_row[:, 0], first_row[:, -1], last_row[:, 0], last_row[:, -1]], axis=-1
     )
-    row_pair = jnp.concatenate([first_row, last_row], axis=-1)
-    col_pair = jnp.pad(jnp.concatenate([first_col, last_col], axis=-1), ((0, 0), (0, 2 * (cols - rows))))
-    strip_pair = jnp.where(part < 2, row_pair, col_pair)
     both = ("tile", "lev")
 
     def lifted(slot_of_part):
@@ -157,28 +154,36 @@
             for source, target in slot_pairs(count, slot_of_part(lev))
         ]
 
-    got_strips = lax.ppermute(strip_pair, both, lifted(lambda lev: lev))
-    got_corners = lax.ppermute(corner_set, both, lifted(lambda lev: 4 + lev))
-    shared = lax.all_gather(jnp.concatenate([got_strips, got_corners], axis=-1), "lev")
+    col_pair = jnp.concatenate([first_col, last_col], axis=-1)
+    row_pair = jnp.concatenate([first_row, last_row], axis=-1)
+    last = parts - 1
+    from_west = lax.ppermute(col_pair, both, lifted(lambda lev: 2))
+    from_east = lax.ppermute(col_pair, both, lifted(lambda lev: 3))
+    from_row = lax.ppermute(row_pair, both, lifted(lambda lev: 1 if lev == last else 0))
+    first_corner = lax.ppermute(corner_set, both, lifted(lambda lev: 6 if lev == last else 4))
+    second_corner = lax.ppermute(corner_set, both, lifted(lambda lev: 7 if lev == last else 5))
 
     def strips(got, length):
         return jnp.stack([got[..., :length], got[..., length : 2 * length]], axis=-2)
 
-    def corner(slot):
-        cell = shared[slot - 4, :, 2 * cols : 2 * cols + 4]
-        code = codes[slot]
+    def choose(cell, code):
         return jnp.where(
             code == 0,
             cell[..., 0],
             jnp.where(code == 1, cell[..., 1], jnp.where(code == 2, cell[..., 2], cell[..., 3])),
         )
 
-    south = pick(strips(shared[0], cols), codes[0])
-    north = pick(strips(shared[1], cols), codes[1])
-    west = pick(strips(shared[2], rows), codes[2])
-    east = pick(strips(shared[3], rows), codes[3])
-    west_full = jnp.concatenate([corner(4)[:, None], west, corner(6)[:, None]], axis=-1)
-    east_full = jnp.concatenate([corner(5)[:, None], east, corner(7)[:, None]], axis=-1)
+    at_end = part == last
+    row_code = jnp.where(at_end, codes[1], codes[0])
+    outer = pick(strips(from_row, cols), row_code)
+    south = outer
+    north = outer
+    west = pick(strips(from_west, rows), codes[2])
+    east = pick(strips(from_east, rows), codes[3])
+    corner_a = choose(first_corner, jnp.where(at_end, codes[6], codes[4]))
+    corner_b = choose(second_corner, jnp.where(at_end, codes[7], codes[5]))
+    west_full = jnp.concatenate([corner_a[:, None], west, corner_a[:, None]], axis=-1)
+    east_full = jnp.concatenate([corner_b[:, None], east, corner_b[:, None]], axis=-1)
     west_part = lax.dynamic_slice_in_dim(west_full, part * part_rows, part_rows + 2, axis=1)
     east_part = lax.dynamic_slice_in_dim(east_full, part * part_rows, part_rows + 2, axis=1)
     above = jnp.where(part == 0, south, halo_block[:, 0, :])

time: 125 us -> 138 us (1.10)
  starting transfers between devices: 42.9 us -> 49.7 us
  waiting for transfers between devices: 17.7 us -> 22.6 us
  between operations: 18.3 us -> 22.3 us
  blocking collectives: 18.2 us -> 16.6 us
    ppermute x2 -> x5, starting transfers between devices: 13.3 us -> 20.1 us  [the longest x1 8.09 us: horizontal_rows(): from_east = lax.ppermute(col_pair, both, lifted(lambda lev: 3))]
    all_gather x1 -> x0, blocking collectives: 5.59 us -> none  [horizontal_rows(): lax.all_gather(jnp.concatenate([got_strips, got_corners], axis=-1), 'lev')]
    ppermute x2 -> x5, waiting for transfers between devices: 2.29 us -> 7.11 us  [the longest x1 6.37 us: horizontal_rows(): lax.ppermute(corner_set, both, lifted(lambda lev: 6 if lev == last else 4))]
    all_to_all x1, blocking collectives: 12.6 us -> 16.6 us  [to_levels(): returning = lax.all_to_all(outgoing, 'lev', 0, 0, tiled=True)]
  transfers between devices with their start and end apart: 7 -> 10, of which waited for: 3 -> 4; matrix products, arithmetic and copies ran while one was open for 2% -> 4% of each run, Pallas kernels for 0% -> 0%
where the time goes in v12:
time: 138 us
  starting transfers between devices  49.7 us (36%)
  waiting for transfers between devices  22.6 us (16%)
  between operations  22.3 us (16%)
  blocking collectives  16.6 us (12%)
  local copies, waits for them, and re-layouts  14.6 us (11%)
  other arithmetic  8.5 us (6%)
  matrix products  3.35 us (2%)
    all_to_all x1, blocking collectives, to_levels(): returning = lax.all_to_all(outgoing, 'lev', 0, 0, tiled=True)  16.6 us
    all_to_all x1, waiting for transfers between devices, to_rows(): columns = lax.all_to_all(jnp.stack(outgoing), 'lev', 0, 0, tiled=True)  11.7 us
    ppermute x1, starting transfers between devices, horizontal(): from_north = lax.ppermute(upright, 'tile', slot_pairs(count, 1))  10.7 us
    ppermute x1, starting transfers between devices, horizontal(): from_east = lax.ppermute(side, 'tile', slot_pairs(count, 3))  9.2 us
    ppermute x1, starting transfers between devices, horizontal_rows(): from_east = lax.ppermute(col_pair, both, lifted(lambda lev: 3))  8.09 us
    ppermute x1, waiting for transfers between devices, horizontal_rows(): lax.ppermute(corner_set, both, lifted(lambda lev: 6 if lev == last else 4))  6.37 us
    ppermute x1, starting transfers between devices, horizontal_rows(): lax.ppermute(corner_set, both, lifted(lambda lev: 7 if lev == last else 5))  6.11 us
    all_to_all x1, starting transfers between devices, to_rows(): columns = lax.all_to_all(jnp.stack(outgoing), 'lev', 0, 0, tiled=True)  5.85 us
  transfers between devices with their start and end apart: 10, of which 4 were waited for; matrix products, arithmetic and copies ran while one was open for 4% of the time, Pallas kernels for 0%

profile of v12, /device:TPU:1, one launch (start us, length us, event | category | flops | bytes accessed | tf_op | source)
XLA Modules:
  0.0 137.7 jit_solution(11708268145279955051)
XLA Ops:
  0.0 1.2 fusion.44
  1.2 1.6 %fusion.45 = (f32[26,48,1]{2,1,0:T(8,128)S(1)}, f32[26,48,1]{2,1,0:T(8,128)S(1)}) fusion(f32[26,48,128]{2,1,0:T(8,128)} %bitcast.112), kind=kLoop, calls=%fused_computation.131 | loop fusion | bytes 19968 | tf_op jit(solution)/shard_map/slice | solution.py:49
  3.5 9.2 %collective-permute-start.1 = (f32[26,100]{1,0:T(8,128)S(1)}, f32[26,100]{1,0:T(8,128)S(1)}, u32[]{:S(2)}, u32[]{:S(2)}) collective-permute-start(f32[26,100]{1,0:T(8,128)S(1)} %concatenate.85), channel_id=1, source_target_pairs={{4,0},{8,4},{12,8},{16,12},{20,16},{24,20},{28,24},{32,28},{36,32}... | collective-permute-start | bytes 31208 | tf_op jit(solution)/shard_map/ppermute | solution.py:51
  12.8 1.9 %collective-permute-start = (f32[26,100]{1,0:T(8,128)S(1)}, f32[26,100]{1,0:T(8,128)S(1)}, u32[]{:S(2)}, u32[]{:S(2)}) collective-permute-start(f32[26,100]{1,0:T(8,128)S(1)} %concatenate.85), channel_id=1, source_target_pairs={{60,0},{0,4},{4,8},{8,12},{12,16},{16,20},{20,24},{24,28},{28,32},... | collective-permute-start | bytes 31208 | tf_op jit(solution)/shard_map/ppermute | solution.py:50
  37.5 10.7 %collective-permute-start.3 = (f32[26,264]{1,0:T(8,128)S(1)}, f32[26,264]{1,0:T(8,128)S(1)}, u32[]{:S(2)}, u32[]{:S(2)}) collective-permute-start(f32[26,264]{1,0:T(8,128)S(1)} %pad_maximum_fusion.9), channel_id=1, source_target_pairs={{64,0},{68,4},{72,8},{76,12},{80,16},{84,20},{88,24},{92,28},{96,3... | collective-permute-start | bytes 82376 | tf_op jit(solution)/shard_map/ppermute | solution.py:59
  48.2 1.9 %collective-permute-start.2 = (f32[26,264]{1,0:T(8,128)S(1)}, f32[26,264]{1,0:T(8,128)S(1)}, u32[]{:S(2)}, u32[]{:S(2)}) collective-permute-start(f32[26,264]{1,0:T(8,128)S(1)} %pad_maximum_fusion.9), channel_id=1, source_target_pairs={{448,0},{452,4},{456,8},{460,12},{464,16},{468,20},{472,24},{476,2... | collective-permute-start | bytes 82376 | tf_op jit(solution)/shard_map/ppermute | solution.py:58
  51.5 3.7 %collective-permute-done.2 = f32[26,264]{1,0:T(8,128)S(1)} collective-permute-done((f32[26,264]{1,0:T(8,128)S(1)}, f32[26,264]{1,0:T(8,128)S(1)}, u32[]{:S(2)}, u32[]{:S(2)}) %collective-permute-start.2) | collective-permute-done | bytes 27488 | tf_op jit(solution)/shard_map/ppermute | solution.py:58
  55.5 1.1 maximum_maximum_fusion.1
  56.7 1.3 fusion.9
  61.0 1.3 pad_maximum_fusion.2
  62.4 5.9 %all-to-all-start = ((f32[4,2,13,2145]{3,1,2,0:T(2,128)}), f32[4,2,13,2145]{3,1,2,0:T(2,128)S(1)}, u32[]{:S(2)}, u32[]{:S(2)}) async-start(f32[4,2,13,2145]{3,1,2,0:T(2,128)} %pad_maximum_fusion.2), calls=%async_computation | async-start | bytes 1810432 | tf_op jit(solution)/shard_map/all_to_all | solution.py:108
  68.6 11.7 %all-to-all-done = f32[4,2,13,2145]{3,1,2,0:T(2,128)S(1)} async-done(((f32[4,2,13,2145]{3,1,2,0:T(2,128)}), f32[4,2,13,2145]{3,1,2,0:T(2,128)S(1)}, u32[]{:S(2)}, u32[]{:S(2)}) %all-to-all-start) | async-done | bytes 892352 | tf_op jit(solution)/shard_map/all_to_all | solution.py:108
  81.8 1.0 convolution_bitcast_fusion.1
  82.7 1.0 convolution_bitcast_fusion
  84.1 8.1 %collective-permute-start.8 = (f32[104,96]{1,0:T(8,128)S(1)}, f32[104,96]{1,0:T(8,128)S(1)}, u32[]{:S(2)}, u32[]{:S(2)}) collective-permute-start(f32[104,96]{1,0:T(8,128)S(1)} %concatenate.109), channel_id=1, source_target_pairs={{4,0},{8,4},{12,8},{16,12},{20,16},{24,20},{28,24},{32,28},{36,32}... | collective-permute-start | bytes 119816 | tf_op jit(solution)/shard_map/ppermute | solution.py:161
  92.2 1.9 %collective-permute-start.6 = (f32[104,96]{1,0:T(8,128)S(1)}, f32[104,96]{1,0:T(8,128)S(1)}, u32[]{:S(2)}, u32[]{:S(2)}) collective-permute-start(f32[104,96]{1,0:T(8,128)S(1)} %concatenate.109), channel_id=1, source_target_pairs={{60,0},{0,4},{4,8},{8,12},{12,16},{16,20},{20,24},{24,28},{28,32},... | collective-permute-start | bytes 119816 | tf_op jit(solution)/shard_map/ppermute | solution.py:160
  94.5 6.1 %collective-permute-start.7 = (f32[104,4]{1,0:T(8,128)S(1)}, f32[104,4]{1,0:T(8,128)S(1)}, u32[]{:S(2)}, u32[]{:S(2)}) collective-permute-start(f32[104,4]{1,0:T(8,128)S(1)} %pad_maximum_fusion.8), channel_id=1, source_target_pairs={{452,0},{456,4},{460,8},{464,12},{468,16},{472,20},{476,24},{480,2... | collective-permute-start | bytes 5000 | tf_op jit(solution)/shard_map/ppermute | solution.py:164
  100.8 1.9 %collective-permute-start.5 = (f32[104,4]{1,0:T(8,128)S(1)}, f32[104,4]{1,0:T(8,128)S(1)}, u32[]{:S(2)}, u32[]{:S(2)}) collective-permute-start(f32[104,4]{1,0:T(8,128)S(1)} %pad_maximum_fusion.8), channel_id=1, source_target_pairs={{508,0},{448,4},{452,8},{456,12},{460,16},{464,20},{468,24},{472,2... | collective-permute-start | bytes 5000 | tf_op jit(solution)/shard_map/ppermute | solution.py:163
  102.8 2.1 %collective-permute-start.4 = (f32[104,256]{1,0:T(8,128)S(1)}, f32[104,256]{1,0:T(8,128)S(1)}, u32[]{:S(2)}, u32[]{:S(2)}) collective-permute-start(f32[104,256]{1,0:T(8,128)S(1)} %concatenate.108), channel_id=1, source_target_pairs={{448,0},{452,4},{456,8},{460,12},{464,16},{468,20},{472,24},{476,2... | collective-permute-start | bytes 319496 | tf_op jit(solution)/shard_map/ppermute | solution.py:162
  105.0 6.4 %collective-permute-done.5 = f32[104,4]{1,0:T(8,128)S(1)} collective-permute-done((f32[104,4]{1,0:T(8,128)S(1)}, f32[104,4]{1,0:T(8,128)S(1)}, u32[]{:S(2)}, u32[]{:S(2)}) %collective-permute-start.5) | collective-permute-done | bytes 1696 | tf_op jit(solution)/shard_map/ppermute | solution.py:163
  114.6 1.2 maximum_maximum_fusion
  115.8 1.4 %fusion.2 = f32[104,12,128]{2,1,0:T(8,128)S(1)} fusion(f32[104,14,129]{2,1,0:T(8,128)S(1)} %get-tuple-element.10, f32[104,14,129]{2,1,0:T(8,128)S(1)} %get-tuple-element.9, f32[104,1,128]{2,1,0:T(1,128)S(1)} %bitcast.131, f32[104,12,128]{2,1,0:T(8,128)S(1)} %slice.564, f32[104,1,128]{2,1,0:T(1,128)S(1)} %bitcast.129, f32[104]{0:T(128)S(1)} %get-tuple-element.54, ...), kind=kLoop, calls=%fused_computation.14 | loop fusion | flops 2236416 | bytes 5225696 | tf_op jit(solution)/shard_map/mul | solution.py:41
  120.1 16.6 %all_to_all.10 = f32[4,2,13,12,128]{4,1,3,2,0:T(2,128)S(1)} all-to-all(f32[4,2,13,12,128]{4,1,3,2,0:T(2,128)S(1)} %copy.209), channel_id=1, replica_groups=mesh['tile'=128,'lev'=4] {'lev'}, dimensions={0} | all-to-all | bytes 1277952 | tf_op jit(solution)/shard_map/all_to_all | solution.py:118
  136.8 0.9 copy.211
  (134 shorter events, 15.3 us)
Async XLA Ops:
  1.2 13.5 %copy-start = (f32[2,13,48,128]{3,2,1,0:T(8,128)S(1)}, f32[2,13,48,128]{3,2,1,0:T(8,128)}, u32[]{:S(2)}) copy-start(f32[2,13,48,128]{3,2,1,0:T(8,128)} %param.6) | copy-start | bytes 1916932
  1.2 13.5 %copy-start.5 = (s32[1,8]{1,0:T(1,128)S(1)}, s32[1,8]{1,0:T(1,128)}, u32[]{:S(2)}) copy-start(s32[1,8]{1,0:T(1,128)} %param.11) | copy-start | bytes 100
  1.2 13.5 %copy-start.4 = (f32[13]{0:T(128)S(1)}, f32[13]{0:T(128)}, u32[]{:S(2)}) copy-start(f32[13]{0:T(128)} %param.7) | copy-start | bytes 160
  1.2 13.6 %copy-start.3 = (s32[48,128]{1,0:T(8,128)S(1)}, s32[48,128]{1,0:T(8,128)}, u32[]{:S(2)}) copy-start(s32[48,128]{1,0:T(8,128)} %param.9) | copy-start | bytes 73732
  1.2 13.6 %copy-start.1 = (f32[2,2,52,52]{3,1,2,0:T(2,128)S(1)}, f32[2,2,52,52]{3,1,2,0:T(2,128)}, u32[]{:S(2)}) copy-start(f32[2,2,52,52]{3,1,2,0:T(2,128)} %param.10) | copy-start | bytes 129796
  2.8 34.3 %copy-start.2 = (s32[48,128]{1,0:T(8,128)S(1)}, s32[48,128]{1,0:T(8,128)}, u32[]{:S(2)}) copy-start(s32[48,128]{1,0:T(8,128)} %param.8) | copy-start | bytes 73732
  3.5 33.8 %collective-permute-start.1 = (f32[26,100]{1,0:T(8,128)S(1)}, f32[26,100]{1,0:T(8,128)S(1)}, u32[]{:S(2)}, u32[]{:S(2)}) collective-permute-start(f32[26,100]{1,0:T(8,128)S(1)} %concatenate.85), channel_id=1, source_target_pairs={{4,0},{8,4},{12,8},{16,12},{20,16},{24,20},{28,24},{32,28},{36,32}... | collective-permute-start | bytes 31208 | tf_op jit(solution)/shard_map/ppermute | solution.py:51
  12.8 24.6 %collective-permute-start = (f32[26,100]{1,0:T(8,128)S(1)}, f32[26,100]{1,0:T(8,128)S(1)}, u32[]{:S(2)}, u32[]{:S(2)}) collective-permute-start(f32[26,100]{1,0:T(8,128)S(1)} %concatenate.85), channel_id=1, source_target_pairs={{60,0},{0,4},{4,8},{8,12},{12,16},{16,20},{20,24},{24,28},{28,32},... | collective-permute-start | bytes 31208 | tf_op jit(solution)/shard_map/ppermute | solution.py:50
  37.5 13.6 %collective-permute-start.3 = (f32[26,264]{1,0:T(8,128)S(1)}, f32[26,264]{1,0:T(8,128)S(1)}, u32[]{:S(2)}, u32[]{:S(2)}) collective-permute-start(f32[26,264]{1,0:T(8,128)S(1)} %pad_maximum_fusion.9), channel_id=1, source_target_pairs={{64,0},{68,4},{72,8},{76,12},{80,16},{84,20},{88,24},{92,28},{96,3... | collective-permute-start | bytes 82376 | tf_op jit(solution)/shard_map/ppermute | solution.py:59
  48.2 7.0 %collective-permute-start.2 = (f32[26,264]{1,0:T(8,128)S(1)}, f32[26,264]{1,0:T(8,128)S(1)}, u32[]{:S(2)}, u32[]{:S(2)}) collective-permute-start(f32[26,264]{1,0:T(8,128)S(1)} %pad_maximum_fusion.9), channel_id=1, source_target_pairs={{448,0},{452,4},{456,8},{460,12},{464,16},{468,20},{472,24},{476,2... | collective-permute-start | bytes 82376 | tf_op jit(solution)/shard_map/ppermute | solution.py:58
  62.4 17.9 %all-to-all-start = ((f32[4,2,13,2145]{3,1,2,0:T(2,128)}), f32[4,2,13,2145]{3,1,2,0:T(2,128)S(1)}, u32[]{:S(2)}, u32[]{:S(2)}) async-start(f32[4,2,13,2145]{3,1,2,0:T(2,128)} %pad_maximum_fusion.2), calls=%async_computation | async-start | bytes 1810432 | tf_op jit(solution)/shard_map/all_to_all | solution.py:108
  84.1 27.4 %collective-permute-start.8 = (f32[104,96]{1,0:T(8,128)S(1)}, f32[104,96]{1,0:T(8,128)S(1)}, u32[]{:S(2)}, u32[]{:S(2)}) collective-permute-start(f32[104,96]{1,0:T(8,128)S(1)} %concatenate.109), channel_id=1, source_target_pairs={{4,0},{8,4},{12,8},{16,12},{20,16},{24,20},{28,24},{32,28},{36,32}... | collective-permute-start | bytes 119816 | tf_op jit(solution)/shard_map/ppermute | solution.py:161
  92.2 19.5 %collective-permute-start.6 = (f32[104,96]{1,0:T(8,128)S(1)}, f32[104,96]{1,0:T(8,128)S(1)}, u32[]{:S(2)}, u32[]{:S(2)}) collective-permute-start(f32[104,96]{1,0:T(8,128)S(1)} %concatenate.109), channel_id=1, source_target_pairs={{60,0},{0,4},{4,8},{8,12},{12,16},{16,20},{20,24},{24,28},{28,32},... | collective-permute-start | bytes 119816 | tf_op jit(solution)/shard_map/ppermute | solution.py:160
  94.5 10.4 %collective-permute-start.7 = (f32[104,4]{1,0:T(8,128)S(1)}, f32[104,4]{1,0:T(8,128)S(1)}, u32[]{:S(2)}, u32[]{:S(2)}) collective-permute-start(f32[104,4]{1,0:T(8,128)S(1)} %pad_maximum_fusion.8), channel_id=1, source_target_pairs={{452,0},{456,4},{460,8},{464,12},{468,16},{472,20},{476,24},{480,2... | collective-permute-start | bytes 5000 | tf_op jit(solution)/shard_map/ppermute | solution.py:164
  100.8 10.6 %collective-permute-start.5 = (f32[104,4]{1,0:T(8,128)S(1)}, f32[104,4]{1,0:T(8,128)S(1)}, u32[]{:S(2)}, u32[]{:S(2)}) collective-permute-start(f32[104,4]{1,0:T(8,128)S(1)} %pad_maximum_fusion.8), channel_id=1, source_target_pairs={{508,0},{448,4},{452,8},{456,12},{460,16},{464,20},{468,24},{472,2... | collective-permute-start | bytes 5000 | tf_op jit(solution)/shard_map/ppermute | solution.py:163
  102.8 11.7 %collective-permute-start.4 = (f32[104,256]{1,0:T(8,128)S(1)}, f32[104,256]{1,0:T(8,128)S(1)}, u32[]{:S(2)}, u32[]{:S(2)}) collective-permute-start(f32[104,256]{1,0:T(8,128)S(1)} %concatenate.108), channel_id=1, source_target_pairs={{448,0},{452,4},{456,8},{460,12},{464,16},{468,20},{472,24},{476,2... | collective-permute-start | bytes 319496 | tf_op jit(solution)/shard_map/ppermute | solution.py:162

commit v13 on v11

--- a/solution.py
+++ b/solution.py
@@ -95,13 +95,20 @@
     part_rows = rows // parts
     padded = jnp.pad(lateral, ((0, 0), (0, 0), (1, 1), (0, 0)))
     rate_column = jnp.broadcast_to(rate[None, :, None], (tracers, depth, 1))
-    edges = jnp.concatenate(
-        [lateral[..., 0, :], lateral[..., -1, :], lateral[..., :, 0], lateral[..., :, -1], rate_column],
+    row_edges = jnp.concatenate([lateral[..., 0, :], lateral[..., -1, :], rate_column], axis=-1)
+    col_edges = jnp.concatenate(
+        [
+            lateral[..., :, 0],
+            lateral[..., :, -1],
+            jnp.zeros((tracers, depth, 2 * (cols - rows)), lateral.dtype),
+            rate_column,
+        ],
         axis=-1,
     )
     outgoing = []
     for dest in range(parts):
         window = padded[:, :, dest * part_rows : dest * part_rows + part_rows + 2, :]
+        edges = row_edges if dest < 2 else col_edges
         outgoing.append(
             jnp.concatenate([window.reshape(tracers, depth, (part_rows + 2) * cols), edges], axis=-1)
         )
@@ -138,16 +145,12 @@
     part_rows = halo_rows - 2
     rows = parts * part_rows
     block = halo_block[:, 1:-1, :]
-    first_row = edges[:, :cols]
-    last_row = edges[:, cols : 2 * cols]
-    first_col = edges[:, 2 * cols : 2 * cols + rows]
-    last_col = edges[:, 2 * cols + rows :]
-    corner_set = jnp.stack(
-        [first_row[:, 0], first_row[:, -1], last_row[:, 0], last_row[:, -1]], axis=-1
-    )
-    row_pair = jnp.concatenate([first_row, last_row], axis=-1)
-    col_pair = jnp.pad(jnp.concatenate([first_col, last_col], axis=-1), ((0, 0), (0, 2 * (cols - rows))))
-    strip_pair = jnp.where(part < 2, row_pair, col_pair)
+    from_rows = jnp.stack([edges[:, 0], edges[:, cols - 1], edges[:, cols], edges[:, 2 * cols - 1]], axis=-1)
+    from_cols = jnp.stack(
+        [edges[:, 0], edges[:, rows], edges[:, rows - 1], edges[:, 2 * rows - 1]], axis=-1
+    )
+    corner_set = jnp.where(part < 2, from_rows, from_cols)
+    strip_pair = edges
     both = ("tile", "lev")
 
     def lifted(slot_of_part):
@@ -201,14 +204,12 @@
     halo_convective = lax.dynamic_slice_in_dim(
         jnp.pad(is_convective, ((1, 1), (0, 0))), part * part_rows, part_rows + 2, axis=0
     )
+    row_map = jnp.concatenate([is_convective[0, :], is_convective[-1, :]])
+    col_map = jnp.concatenate(
+        [is_convective[:, 0], is_convective[:, -1], jnp.zeros((2 * (cols - rows),), bool)]
+    )
     first_map = jnp.concatenate(
-        [
-            halo_convective.reshape(-1),
-            is_convective[0, :],
-            is_convective[-1, :],
-            is_convective[:, 0],
-            is_convective[:, -1],
-        ]
+        [halo_convective.reshape(-1), jnp.where(part < 2, row_map, col_map)]
     )
     convective_rows = lax.dynamic_slice_in_dim(
         is_convective, part * part_rows, part_rows, axis=0

time: 125 us -> 126 us (level)
  blocking collectives: 18.2 us -> 22.3 us
  starting transfers between devices: 42.9 us -> 41.6 us
    all_gather x1, blocking collectives: 5.59 us -> 10.7 us  [horizontal_rows(): lax.all_gather(jnp.concatenate([got_strips, got_corners], axis=-1), 'lev')]
    ppermute x1, starting transfers between devices: 6.96 us -> 1.92 us  [horizontal_rows(): got_strips = lax.ppermute(strip_pair, both, lifted(lambda lev: lev))]
    ppermute x1, starting transfers between devices: 6.33 us -> 10.2 us  [horizontal_rows(): got_corners = lax.ppermute(corner_set, both, lifted(lambda lev: 4 + lev))]
    ppermute x1, waiting for transfers between devices: 2.28 us -> 0.01 us  [horizontal_rows(): got_strips = lax.ppermute(strip_pair, both, lifted(lambda lev: lev))]
  transfers between devices with their start and end apart: 7 -> 7, of which waited for: 3 -> 3; matrix products, arithmetic and copies ran while one was open for 2% -> 3% of each run, Pallas kernels for 0% -> 0%
where the time goes in v13:
time: 126 us; the launch traced here: 125 us
  starting transfers between devices  41.6 us (33%)
  blocking collectives  22.3 us (18%)
  between operations  18.7 us (15%)
  waiting for transfers between devices  16.5 us (13%)
  local copies, waits for them, and re-layouts  14.1 us (11%)
  other arithmetic  8.84 us (7%)
  matrix products  3.28 us (3%)
    all_to_all x1, waiting for transfers between devices, to_rows(): columns = lax.all_to_all(jnp.stack(outgoing), 'lev', 0, 0, tiled=True)  11.7 us
    all_to_all x1, blocking collectives, to_levels(): returning = lax.all_to_all(outgoing, 'lev', 0, 0, tiled=True)  11.6 us
    all_gather x1, blocking collectives, horizontal_rows(): lax.all_gather(jnp.concatenate([got_strips, got_corners], axis=-1), 'lev')  10.7 us
    ppermute x1, starting transfers between devices, horizontal(): from_north = lax.ppermute(upright, 'tile', slot_pairs(count, 1))  10.7 us
    ppermute x1, starting transfers between devices, horizontal_rows(): got_corners = lax.ppermute(corner_set, both, lifted(lambda lev: 4 + lev))  10.2 us
    ppermute x1, starting transfers between devices, horizontal(): from_east = lax.ppermute(side, 'tile', slot_pairs(count, 3))  9.2 us
    all_to_all x1, starting transfers between devices, to_rows(): columns = lax.all_to_all(jnp.stack(outgoing), 'lev', 0, 0, tiled=True)  5.85 us
    ppermute x1, waiting for transfers between devices, horizontal(): from_south = lax.ppermute(upright, 'tile', slot_pairs(count, 0))  3.72 us
  transfers between devices with their start and end apart: 7, of which 3 were waited for; matrix products, arithmetic and copies ran while one was open for 3% of the time, Pallas kernels for 0%

profile of v13, /device:TPU:1, one launch (start us, length us, event | category | flops | bytes accessed | tf_op | source)
XLA Modules:
  0.0 125.5 jit_solution(18217397210567277326)
XLA Ops:
  0.0 1.2 fusion.50
  1.2 1.6 %fusion.51 = (f32[26,48,1]{2,1,0:T(8,128)S(1)}, f32[26,48,1]{2,1,0:T(8,128)S(1)}) fusion(f32[26,48,128]{2,1,0:T(8,128)} %bitcast.133), kind=kLoop, calls=%fused_computation.152 | loop fusion | bytes 19968 | tf_op jit(solution)/shard_map/slice | solution.py:49
  3.5 9.2 %collective-permute-start.1 = (f32[26,100]{1,0:T(8,128)S(1)}, f32[26,100]{1,0:T(8,128)S(1)}, u32[]{:S(2)}, u32[]{:S(2)}) collective-permute-start(f32[26,100]{1,0:T(8,128)S(1)} %concatenate.89), channel_id=1, source_target_pairs={{4,0},{8,4},{12,8},{16,12},{20,16},{24,20},{28,24},{32,28},{36,32}... | collective-permute-start | bytes 31208 | tf_op jit(solution)/shard_map/ppermute | solution.py:51
  12.8 1.9 %collective-permute-start = (f32[26,100]{1,0:T(8,128)S(1)}, f32[26,100]{1,0:T(8,128)S(1)}, u32[]{:S(2)}, u32[]{:S(2)}) collective-permute-start(f32[26,100]{1,0:T(8,128)S(1)} %concatenate.89), channel_id=1, source_target_pairs={{60,0},{0,4},{4,8},{8,12},{12,16},{16,20},{20,24},{24,28},{28,32},... | collective-permute-start | bytes 31208 | tf_op jit(solution)/shard_map/ppermute | solution.py:50
  34.0 10.7 %collective-permute-start.3 = (f32[26,264]{1,0:T(8,128)S(1)}, f32[26,264]{1,0:T(8,128)S(1)}, u32[]{:S(2)}, u32[]{:S(2)}) collective-permute-start(f32[26,264]{1,0:T(8,128)S(1)} %pad_maximum_fusion.14), channel_id=1, source_target_pairs={{64,0},{68,4},{72,8},{76,12},{80,16},{84,20},{88,24},{92,28},{96,3... | collective-permute-start | bytes 82376 | tf_op jit(solution)/shard_map/ppermute | solution.py:59
  44.6 1.9 %collective-permute-start.2 = (f32[26,264]{1,0:T(8,128)S(1)}, f32[26,264]{1,0:T(8,128)S(1)}, u32[]{:S(2)}, u32[]{:S(2)}) collective-permute-start(f32[26,264]{1,0:T(8,128)S(1)} %pad_maximum_fusion.14), channel_id=1, source_target_pairs={{448,0},{452,4},{456,8},{460,12},{464,16},{468,20},{472,24},{476,2... | collective-permute-start | bytes 82376 | tf_op jit(solution)/shard_map/ppermute | solution.py:58
  47.9 3.7 %collective-permute-done.2 = f32[26,264]{1,0:T(8,128)S(1)} collective-permute-done((f32[26,264]{1,0:T(8,128)S(1)}, f32[26,264]{1,0:T(8,128)S(1)}, u32[]{:S(2)}, u32[]{:S(2)}) %collective-permute-start.2) | collective-permute-done | bytes 27488 | tf_op jit(solution)/shard_map/ppermute | solution.py:58
  52.0 1.1 maximum_maximum_fusion.1
  53.1 1.3 %fusion.9 = f32[26,48,128]{2,1,0:T(8,128)S(1)} fusion(f32[26,49,130]{2,1,0:T(8,128)S(1)} %get-tuple-element.8, f32[26,49,130]{2,1,0:T(8,128)S(1)} %get-tuple-element.7, f32[26,48,1]{2,1,0:T(8,128)S(1)} %copy.189, f32[26,48,128]{2,1,0:T(8,128)S(1)} %bitcast.136, f32[26,48,1]{2,1,0:T(8,128)S(1)} %copy.188, f32[26]{0:T(128)S(1)} %get-tuple-element.67, ...), kind=kLoop, calls=%fused_computation.31 | loop fusion | flops 2236416 | bytes 5146680 | tf_op jit(solution)/shard_map/mul | solution.py:41
  57.1 1.3 %pad_maximum_fusion.2 = f32[4,2,13,2049]{3,1,2,0:T(2,128)} fusion(f32[1,2,13,2049]{3,1,2,0:T(2,128)S(1)} %bitcast.147, f32[1,2,13,2049]{3,1,2,0:T(2,128)S(1)} %bitcast.148, f32[1,2,13,2049]{3,1,2,0:T(2,128)S(1)} %get-tuple-element.57, f32[1,2,13,2049]{3,1,2,0:T(2,128)S(1)} %get-tuple-element.56), kind=kLoop, calls=%fused_computation.10 | loop fusion | flops 639288 | bytes 1704768 | tf_op jit(solution)/shard_map/stack | solution.py:115
  58.5 5.9 %all-to-all-start = ((f32[4,2,13,2049]{3,1,2,0:T(2,128)}), f32[4,2,13,2049]{3,1,2,0:T(2,128)S(1)}, u32[]{:S(2)}, u32[]{:S(2)}) async-start(f32[4,2,13,2049]{3,1,2,0:T(2,128)} %pad_maximum_fusion.2), calls=%async_computation | async-start | bytes 1810432 | tf_op jit(solution)/shard_map/all_to_all | solution.py:115
  64.7 11.7 %all-to-all-done = f32[4,2,13,2049]{3,1,2,0:T(2,128)S(1)} async-done(((f32[4,2,13,2049]{3,1,2,0:T(2,128)}), f32[4,2,13,2049]{3,1,2,0:T(2,128)S(1)}, u32[]{:S(2)}, u32[]{:S(2)}) %all-to-all-start) | async-done | bytes 852416 | tf_op jit(solution)/shard_map/all_to_all | solution.py:115
  77.5 0.9 convolution_bitcast_fusion.3
  78.5 0.9 convolution_bitcast_fusion.2
  79.7 1.9 %collective-permute-start.4 = (f32[104,256]{1,0:T(8,128)S(1)}, f32[104,256]{1,0:T(8,128)S(1)}, u32[]{:S(2)}, u32[]{:S(2)}) collective-permute-start(f32[104,256]{1,0:T(8,128)S(1)} %reshape.215), channel_id=1, source_target_pairs={{448,0},{452,4},{456,8},{460,12},{464,16},{468,20},{472,24},{476,2... | collective-permute-start | bytes 319496 | tf_op jit(solution)/shard_map/ppermute | solution.py:163
  82.2 10.2 %collective-permute-start.5 = (f32[104,4]{1,0:T(8,128)S(1)}, f32[104,4]{1,0:T(8,128)S(1)}, u32[]{:S(2)}, u32[]{:S(2)}) collective-permute-start(f32[104,4]{1,0:T(8,128)S(1)} %maximum_select_fusion), channel_id=1, source_target_pairs={{508,0},{448,4},{452,8},{456,12},{460,16},{464,20},{468,24},{472,2... | collective-permute-start | bytes 5000 | tf_op jit(solution)/shard_map/ppermute | solution.py:164
  92.5 1.1 collective-permute-done.5
  93.7 10.7 %all-gather.1 = f32[4,104,260]{1,2,0:T(8,128)S(1)} all-gather(f32[1,104,260]{1,2,0:T(8,128)S(1)} %copy.201), channel_id=2, replica_groups=mesh['tile'=128,'lev'=4] {'lev'}, dimensions={0}, use_global_device_ids=true | all-gather | bytes 540800 | tf_op jit(solution)/shard_map/all_gather | solution.py:165
  105.8 0.7 copy.211
  106.6 0.7 copy.215
  107.4 1.2 maximum_maximum_fusion
  108.6 1.4 %fusion.2 = f32[104,12,128]{2,1,0:T(8,128)S(1)} fusion(f32[104,14,129]{2,1,0:T(8,128)S(1)} %get-tuple-element.10, f32[104,14,129]{2,1,0:T(8,128)S(1)} %get-tuple-element.9, f32[104,1,128]{2,1,0:T(1,128)S(1)} %bitcast.152, f32[104,12,128]{2,1,0:T(8,128)S(1)} %slice.651, f32[104,1,128]{2,1,0:T(1,128)S(1)} %bitcast.150, f32[104]{0:T(128)S(1)} %get-tuple-element.65, ...), kind=kLoop, calls=%fused_computation.14 | loop fusion | flops 2236416 | bytes 5225696 | tf_op jit(solution)/shard_map/mul | solution.py:41
  112.9 11.6 %all_to_all.10 = f32[4,2,13,12,128]{4,1,3,2,0:T(2,128)S(1)} all-to-all(f32[4,2,13,12,128]{4,1,3,2,0:T(2,128)S(1)} %copy.216), channel_id=1, replica_groups=mesh['tile'=128,'lev'=4] {'lev'}, dimensions={0} | all-to-all | bytes 1277952 | tf_op jit(solution)/shard_map/all_to_all | solution.py:125
  124.6 0.9 copy.218
  (136 shorter events, 12.9 us)
Async XLA Ops:
  1.2 13.5 %copy-start = (f32[2,13,48,128]{3,2,1,0:T(8,128)S(1)}, f32[2,13,48,128]{3,2,1,0:T(8,128)}, u32[]{:S(2)}) copy-start(f32[2,13,48,128]{3,2,1,0:T(8,128)} %param.6) | copy-start | bytes 1916932
  1.2 13.5 %copy-start.5 = (s32[1,8]{1,0:T(1,128)S(1)}, s32[1,8]{1,0:T(1,128)}, u32[]{:S(2)}) copy-start(s32[1,8]{1,0:T(1,128)} %param.11) | copy-start | bytes 100
  1.2 13.5 %copy-start.4 = (f32[13]{0:T(128)S(1)}, f32[13]{0:T(128)}, u32[]{:S(2)}) copy-start(f32[13]{0:T(128)} %param.7) | copy-start | bytes 160
  1.2 13.6 %copy-start.3 = (s32[48,128]{1,0:T(8,128)S(1)}, s32[48,128]{1,0:T(8,128)}, u32[]{:S(2)}) copy-start(s32[48,128]{1,0:T(8,128)} %param.9) | copy-start | bytes 73732
  1.2 13.7 %copy-start.1 = (f32[2,2,52,52]{3,1,2,0:T(2,128)S(1)}, f32[2,2,52,52]{3,1,2,0:T(2,128)}, u32[]{:S(2)}) copy-start(f32[2,2,52,52]{3,1,2,0:T(2,128)} %param.10) | copy-start | bytes 129796
  2.8 30.7 %copy-start.2 = (s32[48,128]{1,0:T(8,128)S(1)}, s32[48,128]{1,0:T(8,128)}, u32[]{:S(2)}) copy-start(s32[48,128]{1,0:T(8,128)} %param.8) | copy-start | bytes 73732
  3.5 30.2 %collective-permute-start.1 = (f32[26,100]{1,0:T(8,128)S(1)}, f32[26,100]{1,0:T(8,128)S(1)}, u32[]{:S(2)}, u32[]{:S(2)}) collective-permute-start(f32[26,100]{1,0:T(8,128)S(1)} %concatenate.89), channel_id=1, source_target_pairs={{4,0},{8,4},{12,8},{16,12},{20,16},{24,20},{28,24},{32,28},{36,32}... | collective-permute-start | bytes 31208 | tf_op jit(solution)/shard_map/ppermute | solution.py:51
  12.8 21.1 %collective-permute-start = (f32[26,100]{1,0:T(8,128)S(1)}, f32[26,100]{1,0:T(8,128)S(1)}, u32[]{:S(2)}, u32[]{:S(2)}) collective-permute-start(f32[26,100]{1,0:T(8,128)S(1)} %concatenate.89), channel_id=1, source_target_pairs={{60,0},{0,4},{4,8},{8,12},{12,16},{16,20},{20,24},{24,28},{28,32},... | collective-permute-start | bytes 31208 | tf_op jit(solution)/shard_map/ppermute | solution.py:50
  34.0 13.6 %collective-permute-start.3 = (f32[26,264]{1,0:T(8,128)S(1)}, f32[26,264]{1,0:T(8,128)S(1)}, u32[]{:S(2)}, u32[]{:S(2)}) collective-permute-start(f32[26,264]{1,0:T(8,128)S(1)} %pad_maximum_fusion.14), channel_id=1, source_target_pairs={{64,0},{68,4},{72,8},{76,12},{80,16},{84,20},{88,24},{92,28},{96,3... | collective-permute-start | bytes 82376 | tf_op jit(solution)/shard_map/ppermute | solution.py:59
  44.6 7.0 %collective-permute-start.2 = (f32[26,264]{1,0:T(8,128)S(1)}, f32[26,264]{1,0:T(8,128)S(1)}, u32[]{:S(2)}, u32[]{:S(2)}) collective-permute-start(f32[26,264]{1,0:T(8,128)S(1)} %pad_maximum_fusion.14), channel_id=1, source_target_pairs={{448,0},{452,4},{456,8},{460,12},{464,16},{468,20},{472,24},{476,2... | collective-permute-start | bytes 82376 | tf_op jit(solution)/shard_map/ppermute | solution.py:58
  58.5 17.9 %all-to-all-start = ((f32[4,2,13,2049]{3,1,2,0:T(2,128)}), f32[4,2,13,2049]{3,1,2,0:T(2,128)S(1)}, u32[]{:S(2)}, u32[]{:S(2)}) async-start(f32[4,2,13,2049]{3,1,2,0:T(2,128)} %pad_maximum_fusion.2), calls=%async_computation | async-start | bytes 1810432 | tf_op jit(solution)/shard_map/all_to_all | solution.py:115
  79.7 13.9 %collective-permute-start.4 = (f32[104,256]{1,0:T(8,128)S(1)}, f32[104,256]{1,0:T(8,128)S(1)}, u32[]{:S(2)}, u32[]{:S(2)}) collective-permute-start(f32[104,256]{1,0:T(8,128)S(1)} %reshape.215), channel_id=1, source_target_pairs={{448,0},{452,4},{456,8},{460,12},{464,16},{468,20},{472,24},{476,2... | collective-permute-start | bytes 319496 | tf_op jit(solution)/shard_map/ppermute | solution.py:163
  82.2 11.4 %collective-permute-start.5 = (f32[104,4]{1,0:T(8,128)S(1)}, f32[104,4]{1,0:T(8,128)S(1)}, u32[]{:S(2)}, u32[]{:S(2)}) collective-permute-start(f32[104,4]{1,0:T(8,128)S(1)} %maximum_select_fusion), channel_id=1, source_target_pairs={{508,0},{448,4},{452,8},{456,12},{460,16},{464,20},{468,24},{472,2... | collective-permute-start | bytes 5000 | tf_op jit(solution)/shard_map/ppermute | solution.py:164

commit v14 on v11

--- a/solution.py
+++ b/solution.py
@@ -110,13 +110,10 @@
     return gathered[..., :-1], gathered[0, :, -1]
 
 
-def to_levels(block):
-    parts = lax.axis_size("lev")
-    tracers, levels, part_rows, cols = block.shape
-    depth = levels // parts
-    outgoing = jnp.transpose(block.reshape(tracers, parts, depth, part_rows, cols), (1, 0, 2, 3, 4))
+def to_levels(outgoing, rows, cols):
+    parts, tracers, depth, width = outgoing.shape
     returning = lax.all_to_all(outgoing, "lev", 0, 0, tiled=True)
-    return jnp.transpose(returning, (1, 2, 0, 3, 4)).reshape(tracers, depth, parts * part_rows, cols)
+    return jnp.transpose(returning, (1, 2, 0, 3)).reshape(tracers, depth, rows, cols)
 
 
 def column_mix(block, stacked_inverse, convective_map):
@@ -225,10 +222,14 @@
     halo_block = mixed[:, :, :halo_width].reshape(tracers * levels, part_rows + 2, cols)
     edges = mixed[:, :, halo_width:].reshape(tracers * levels, -1)
     lateral = horizontal_rows(halo_block, edges, block_rate, wet_rows, codes)
-    block = column_mix(
-        lateral.reshape(tracers, levels, part_rows * cols), stacked_inverse, convective_rows
-    )
-    return to_levels(block.reshape(tracers, levels, part_rows, cols))
+    flat = lateral.reshape(tracers, levels, part_rows * cols)
+    outgoing = []
+    for tracer in range(tracers):
+        both_states = jnp.dot(
+            stacked_inverse[tracer], flat[tracer], precision=lax.Precision.HIGHEST
+        ).reshape(2, parts, depth, part_rows * cols)
+        outgoing.append(jnp.where(convective_rows[None, None], both_states[1], both_states[0]))
+    return to_levels(jnp.stack(outgoing, axis=1), rows, cols)
 
 
 def solution(mesh):

time: 125 us -> 125 us (level)
    dot_general x0 -> x2, matrix products: none -> 1.43 us  [local(): jnp.dot(stacked_inverse[tracer], flat[tracer], precision=lax.Precision.HI...]
    dot_general x4 -> x2, matrix products: 3.35 us -> 1.92 us  [column_mix(): jnp.dot(stacked_inverse[tracer], block[tracer], precision=lax.Precision.H...]
where the time goes in v14:
time: 125 us; the launch traced here: 124 us
  starting transfers between devices  42.9 us (34%)
  between operations  18.3 us (15%)
  blocking collectives  18.2 us (15%)
  waiting for transfers between devices  17.7 us (14%)
  local copies, waits for them, and re-layouts  15.3 us (12%)
  other arithmetic  8.52 us (7%)
  matrix products  3.35 us (3%)
    all_to_all x1, blocking collectives, to_levels(): returning = lax.all_to_all(outgoing, 'lev', 0, 0, tiled=True)  12.6 us
    all_to_all x1, waiting for transfers between devices, to_rows(): columns = lax.all_to_all(jnp.stack(outgoing), 'lev', 0, 0, tiled=True)  11.7 us
    ppermute x1, starting transfers between devices, horizontal(): from_north = lax.ppermute(upright, 'tile', slot_pairs(count, 1))  10.7 us
    ppermute x1, starting transfers between devices, horizontal(): from_east = lax.ppermute(side, 'tile', slot_pairs(count, 3))  9.2 us
    ppermute x1, starting transfers between devices, horizontal_rows(): got_strips = lax.ppermute(strip_pair, both, lifted(lambda lev: lev))  6.96 us
    ppermute x1, starting transfers between devices, horizontal_rows(): got_corners = lax.ppermute(corner_set, both, lifted(lambda lev: 4 + lev))  6.33 us
    all_to_all x1, starting transfers between devices, to_rows(): columns = lax.all_to_all(jnp.stack(outgoing), 'lev', 0, 0, tiled=True)  5.85 us
    all_gather x1, blocking collectives, horizontal_rows(): lax.all_gather(jnp.concatenate([got_strips, got_corners], axis=-1), 'lev')  5.59 us
  transfers between devices with their start and end apart: 7, of which 3 were waited for; matrix products, arithmetic and copies ran while one was open for 2% of the time, Pallas kernels for 0%

profile of v14, /device:TPU:1, one launch (start us, length us, event | category | flops | bytes accessed | tf_op | source)
XLA Modules:
  0.0 124.3 jit_solution(16105870713835706603)
XLA Ops:
  0.0 1.2 fusion.48
  1.2 1.6 %fusion.49 = (f32[26,48,1]{2,1,0:T(8,128)S(1)}, f32[26,48,1]{2,1,0:T(8,128)S(1)}) fusion(f32[26,48,128]{2,1,0:T(8,128)} %bitcast.130), kind=kLoop, calls=%fused_computation.143 | loop fusion | bytes 19968 | tf_op jit(solution)/shard_map/slice | solution.py:49
  3.5 9.2 %collective-permute-start.1 = (f32[26,100]{1,0:T(8,128)S(1)}, f32[26,100]{1,0:T(8,128)S(1)}, u32[]{:S(2)}, u32[]{:S(2)}) collective-permute-start(f32[26,100]{1,0:T(8,128)S(1)} %concatenate.87), channel_id=1, source_target_pairs={{4,0},{8,4},{12,8},{16,12},{20,16},{24,20},{28,24},{32,28},{36,32}... | collective-permute-start | bytes 31208 | tf_op jit(solution)/shard_map/ppermute | solution.py:51
  12.8 1.9 %collective-permute-start = (f32[26,100]{1,0:T(8,128)S(1)}, f32[26,100]{1,0:T(8,128)S(1)}, u32[]{:S(2)}, u32[]{:S(2)}) collective-permute-start(f32[26,100]{1,0:T(8,128)S(1)} %concatenate.87), channel_id=1, source_target_pairs={{60,0},{0,4},{4,8},{8,12},{12,16},{16,20},{20,24},{24,28},{28,32},... | collective-permute-start | bytes 31208 | tf_op jit(solution)/shard_map/ppermute | solution.py:50
  33.5 10.7 %collective-permute-start.3 = (f32[26,264]{1,0:T(8,128)S(1)}, f32[26,264]{1,0:T(8,128)S(1)}, u32[]{:S(2)}, u32[]{:S(2)}) collective-permute-start(f32[26,264]{1,0:T(8,128)S(1)} %pad_maximum_fusion.10), channel_id=1, source_target_pairs={{64,0},{68,4},{72,8},{76,12},{80,16},{84,20},{88,24},{92,28},{96,3... | collective-permute-start | bytes 82376 | tf_op jit(solution)/shard_map/ppermute | solution.py:59
  44.2 1.9 %collective-permute-start.2 = (f32[26,264]{1,0:T(8,128)S(1)}, f32[26,264]{1,0:T(8,128)S(1)}, u32[]{:S(2)}, u32[]{:S(2)}) collective-permute-start(f32[26,264]{1,0:T(8,128)S(1)} %pad_maximum_fusion.10), channel_id=1, source_target_pairs={{448,0},{452,4},{456,8},{460,12},{464,16},{468,20},{472,24},{476,2... | collective-permute-start | bytes 82376 | tf_op jit(solution)/shard_map/ppermute | solution.py:58
  47.5 3.7 %collective-permute-done.2 = f32[26,264]{1,0:T(8,128)S(1)} collective-permute-done((f32[26,264]{1,0:T(8,128)S(1)}, f32[26,264]{1,0:T(8,128)S(1)}, u32[]{:S(2)}, u32[]{:S(2)}) %collective-permute-start.2) | collective-permute-done | bytes 27488 | tf_op jit(solution)/shard_map/ppermute | solution.py:58
  51.5 1.1 maximum_maximum_fusion.1
  52.7 1.3 %fusion.9 = f32[26,48,128]{2,1,0:T(8,128)S(1)} fusion(f32[26,49,130]{2,1,0:T(8,128)S(1)} %get-tuple-element.8, f32[26,49,130]{2,1,0:T(8,128)S(1)} %get-tuple-element.7, f32[26,48,1]{2,1,0:T(8,128)S(1)} %copy.187, f32[26,48,128]{2,1,0:T(8,128)S(1)} %bitcast.133, f32[26,48,1]{2,1,0:T(8,128)S(1)} %copy.186, f32[26]{0:T(128)S(1)} %get-tuple-element.62, ...), kind=kLoop, calls=%fused_computation.31 | loop fusion | flops 2236416 | bytes 5146680 | tf_op jit(solution)/shard_map/mul | solution.py:41
  57.0 1.4 %pad_maximum_fusion.2 = f32[4,2,13,2145]{3,1,2,0:T(2,128)} fusion(f32[1,2,13,2145]{3,1,2,0:T(2,128)S(1)} %bitcast.143, f32[1,2,13,2145]{3,1,2,0:T(2,128)S(1)} %bitcast.144, f32[1,2,13,2145]{3,1,2,0:T(2,128)S(1)} %bitcast.145, f32[1,2,13,2145]{3,1,2,0:T(2,128)S(1)} %bitcast.146), kind=kLoop, calls=%fused_computation.10 | loop fusion | flops 669240 | bytes 1784640 | tf_op jit(solution)/shard_map/stack | solution.py:108
  58.4 5.9 %all-to-all-start = ((f32[4,2,13,2145]{3,1,2,0:T(2,128)}), f32[4,2,13,2145]{3,1,2,0:T(2,128)S(1)}, u32[]{:S(2)}, u32[]{:S(2)}) async-start(f32[4,2,13,2145]{3,1,2,0:T(2,128)} %pad_maximum_fusion.2), calls=%async_computation | async-start | bytes 1810432 | tf_op jit(solution)/shard_map/all_to_all | solution.py:108
  64.6 11.7 %all-to-all-done = f32[4,2,13,2145]{3,1,2,0:T(2,128)S(1)} async-done(((f32[4,2,13,2145]{3,1,2,0:T(2,128)}), f32[4,2,13,2145]{3,1,2,0:T(2,128)S(1)}, u32[]{:S(2)}, u32[]{:S(2)}) %all-to-all-start) | async-done | bytes 892352 | tf_op jit(solution)/shard_map/all_to_all | solution.py:108
  76.3 0.8 slice_reduce_fusion
  77.8 1.0 convolution_bitcast_fusion.1
  78.8 1.0 convolution_bitcast_fusion
  80.5 6.3 %collective-permute-start.5 = (f32[104,4]{1,0:T(8,128)S(1)}, f32[104,4]{1,0:T(8,128)S(1)}, u32[]{:S(2)}, u32[]{:S(2)}) collective-permute-start(f32[104,4]{1,0:T(8,128)S(1)} %pad_maximum_fusion.9), channel_id=1, source_target_pairs={{508,0},{448,4},{452,8},{456,12},{460,16},{464,20},{468,24},{472,2... | collective-permute-start | bytes 5000 | tf_op jit(solution)/shard_map/ppermute | solution.py:158
  87.0 7.0 %collective-permute-start.4 = (f32[104,256]{1,0:T(8,128)S(1)}, f32[104,256]{1,0:T(8,128)S(1)}, u32[]{:S(2)}, u32[]{:S(2)}) collective-permute-start(f32[104,256]{1,0:T(8,128)S(1)} %slice_select_fusion.2), channel_id=1, source_target_pairs={{448,0},{452,4},{456,8},{460,12},{464,16},{468,20},{472,24},{476,2... | collective-permute-start | bytes 319496 | tf_op jit(solution)/shard_map/ppermute | solution.py:157
  94.0 2.3 %collective-permute-done.4 = f32[104,256]{1,0:T(8,128)S(1)} collective-permute-done((f32[104,256]{1,0:T(8,128)S(1)}, f32[104,256]{1,0:T(8,128)S(1)}, u32[]{:S(2)}, u32[]{:S(2)}) %collective-permute-start.4) | collective-permute-done | bytes 106528 | tf_op jit(solution)/shard_map/ppermute | solution.py:157
  96.4 5.6 %all-gather.1 = f32[4,104,260]{1,2,0:T(8,128)S(1)} all-gather(f32[1,104,260]{1,2,0:T(8,128)S(1)} %copy.199), channel_id=2, replica_groups=mesh['tile'=128,'lev'=4] {'lev'}, dimensions={0}, use_global_device_ids=true | all-gather | bytes 540800 | tf_op jit(solution)/shard_map/all_gather | solution.py:159
  103.4 0.7 copy.209
  105.0 1.2 maximum_maximum_fusion
  106.2 1.4 %fusion.2 = f32[104,12,128]{2,1,0:T(8,128)S(1)} fusion(f32[104,14,129]{2,1,0:T(8,128)S(1)} %get-tuple-element.10, f32[104,14,129]{2,1,0:T(8,128)S(1)} %get-tuple-element.9, f32[104,1,128]{2,1,0:T(1,128)S(1)} %bitcast.150, f32[104,12,128]{2,1,0:T(8,128)S(1)} %slice.648, f32[104,1,128]{2,1,0:T(1,128)S(1)} %bitcast.148, f32[104]{0:T(128)S(1)} %get-tuple-element.60, ...), kind=kLoop, calls=%fused_computation.14 | loop fusion | flops 2236416 | bytes 5225696 | tf_op jit(solution)/shard_map/mul | solution.py:41
  110.4 12.6 %all_to_all.10 = f32[4,2,13,1536]{3,1,2,0:T(2,128)S(1)} all-to-all(f32[4,2,13,1536]{3,1,2,0:T(2,128)S(1)} %copy.214), channel_id=1, replica_groups=mesh['tile'=128,'lev'=4] {'lev'}, dimensions={0} | all-to-all | bytes 1277952 | tf_op jit(solution)/shard_map/all_to_all | solution.py:115
  123.2 1.1 reshape.192
  (136 shorter events, 13.5 us)
Async XLA Ops:
  1.2 13.5 %copy-start = (f32[2,13,48,128]{3,2,1,0:T(8,128)S(1)}, f32[2,13,48,128]{3,2,1,0:T(8,128)}, u32[]{:S(2)}) copy-start(f32[2,13,48,128]{3,2,1,0:T(8,128)} %param.6) | copy-start | bytes 1916932
  1.2 13.5 %copy-start.5 = (s32[1,8]{1,0:T(1,128)S(1)}, s32[1,8]{1,0:T(1,128)}, u32[]{:S(2)}) copy-start(s32[1,8]{1,0:T(1,128)} %param.11) | copy-start | bytes 100
  1.2 13.5 %copy-start.4 = (f32[13]{0:T(128)S(1)}, f32[13]{0:T(128)}, u32[]{:S(2)}) copy-start(f32[13]{0:T(128)} %param.7) | copy-start | bytes 160
  1.2 13.6 %copy-start.3 = (s32[48,128]{1,0:T(8,128)S(1)}, s32[48,128]{1,0:T(8,128)}, u32[]{:S(2)}) copy-start(s32[48,128]{1,0:T(8,128)} %param.9) | copy-start | bytes 73732
  1.2 13.6 %copy-start.1 = (f32[2,2,52,52]{3,1,2,0:T(2,128)S(1)}, f32[2,2,52,52]{3,1,2,0:T(2,128)}, u32[]{:S(2)}) copy-start(f32[2,2,52,52]{3,1,2,0:T(2,128)} %param.10) | copy-start | bytes 129796
  2.8 30.3 %copy-start.2 = (s32[48,128]{1,0:T(8,128)S(1)}, s32[48,128]{1,0:T(8,128)}, u32[]{:S(2)}) copy-start(s32[48,128]{1,0:T(8,128)} %param.8) | copy-start | bytes 73732
  3.5 29.8 %collective-permute-start.1 = (f32[26,100]{1,0:T(8,128)S(1)}, f32[26,100]{1,0:T(8,128)S(1)}, u32[]{:S(2)}, u32[]{:S(2)}) collective-permute-start(f32[26,100]{1,0:T(8,128)S(1)} %concatenate.87), channel_id=1, source_target_pairs={{4,0},{8,4},{12,8},{16,12},{20,16},{24,20},{28,24},{32,28},{36,32}... | collective-permute-start | bytes 31208 | tf_op jit(solution)/shard_map/ppermute | solution.py:51
  12.8 20.6 %collective-permute-start = (f32[26,100]{1,0:T(8,128)S(1)}, f32[26,100]{1,0:T(8,128)S(1)}, u32[]{:S(2)}, u32[]{:S(2)}) collective-permute-start(f32[26,100]{1,0:T(8,128)S(1)} %concatenate.87), channel_id=1, source_target_pairs={{60,0},{0,4},{4,8},{8,12},{12,16},{16,20},{20,24},{24,28},{28,32},... | collective-permute-start | bytes 31208 | tf_op jit(solution)/shard_map/ppermute | solution.py:50
  33.5 13.6 %collective-permute-start.3 = (f32[26,264]{1,0:T(8,128)S(1)}, f32[26,264]{1,0:T(8,128)S(1)}, u32[]{:S(2)}, u32[]{:S(2)}) collective-permute-start(f32[26,264]{1,0:T(8,128)S(1)} %pad_maximum_fusion.10), channel_id=1, source_target_pairs={{64,0},{68,4},{72,8},{76,12},{80,16},{84,20},{88,24},{92,28},{96,3... | collective-permute-start | bytes 82376 | tf_op jit(solution)/shard_map/ppermute | solution.py:59
  44.2 7.0 %collective-permute-start.2 = (f32[26,264]{1,0:T(8,128)S(1)}, f32[26,264]{1,0:T(8,128)S(1)}, u32[]{:S(2)}, u32[]{:S(2)}) collective-permute-start(f32[26,264]{1,0:T(8,128)S(1)} %pad_maximum_fusion.10), channel_id=1, source_target_pairs={{448,0},{452,4},{456,8},{460,12},{464,16},{468,20},{472,24},{476,2... | collective-permute-start | bytes 82376 | tf_op jit(solution)/shard_map/ppermute | solution.py:58
  58.4 17.9 %all-to-all-start = ((f32[4,2,13,2145]{3,1,2,0:T(2,128)}), f32[4,2,13,2145]{3,1,2,0:T(2,128)S(1)}, u32[]{:S(2)}, u32[]{:S(2)}) async-start(f32[4,2,13,2145]{3,1,2,0:T(2,128)} %pad_maximum_fusion.2), calls=%async_computation | async-start | bytes 1810432 | tf_op jit(solution)/shard_map/all_to_all | solution.py:108
  80.5 13.5 %collective-permute-start.5 = (f32[104,4]{1,0:T(8,128)S(1)}, f32[104,4]{1,0:T(8,128)S(1)}, u32[]{:S(2)}, u32[]{:S(2)}) collective-permute-start(f32[104,4]{1,0:T(8,128)S(1)} %pad_maximum_fusion.9), channel_id=1, source_target_pairs={{508,0},{448,4},{452,8},{456,12},{460,16},{464,20},{468,24},{472,2... | collective-permute-start | bytes 5000 | tf_op jit(solution)/shard_map/ppermute | solution.py:158
  87.0 9.4 %collective-permute-start.4 = (f32[104,256]{1,0:T(8,128)S(1)}, f32[104,256]{1,0:T(8,128)S(1)}, u32[]{:S(2)}, u32[]{:S(2)}) collective-permute-start(f32[104,256]{1,0:T(8,128)S(1)} %slice_select_fusion.2), channel_id=1, source_target_pairs={{448,0},{452,4},{456,8},{460,12},{464,16},{468,20},{472,24},{476,2... | collective-permute-start | bytes 319496 | tf_op jit(solution)/shard_map/ppermute | solution.py:157
